TPU v7x, 512 devices: a whole 4x8x8 slice. The times are simulated.
512 devices in a mesh: replica: 32 (over x, y_hi, core), fsdp: 16 (over y_lo, z).
Axes of the slice: x: 4, y: 8 (y_hi: 4, y_lo: 2; y = y_hi * 2 + y_lo), z: 8, core: 2. Of those that a mesh axis runs over, the one named last changes fastest.
Arguments:
- numerators: float32 [32, 4096, 512], P('replica', 'fsdp'), may hold values from -6 to 6
- push_weights: float32 [32], P('replica'), may hold values from 0.5 to 2
- step_power: int32 [1], replicated, may hold values from 0 to 2
- activations: bfloat16 [32, 6144, 4096], P('replica', 'fsdp'), may hold values from -6 to 6
- targets: bfloat16 [32, 6144, 512], P('replica', 'fsdp'), may hold values from -6 to 6
- gain: float32 [4096], replicated, may hold values from 0.1 to 1.9
Outputs:
- mixed_numerators: float32 [32, 4096, 512], P('replica', 'fsdp')
- mixed_weights: float32 [32], P('replica')
All inputs are finite; a program needn't handle non-finite values.
Results may differ from a plain program's by a relative error of at most 0.015.
Values may be sent and summed in bfloat16 or wider, within the bound.
No kernel may reach another device: no remote copies, remote signals or barrier semaphores. Data moves between devices by JAX's collectives and lax.ppermute only.
A program may use at most 64 MiB of HBM per device.

v0:
```python
from functools import partial
import math

import jax
import jax.numpy as jnp
from jax import lax
from jax.sharding import PartitionSpec as P

DIST_KINDS = 3


def passed_along(value, axis, steps):
    count = lax.axis_size(axis)
    pairs = [(source, (source + steps) % count) for source in range(count)]
    return lax.ppermute(value, axis, pairs)


def send_updated(pair, by):
    return passed_along(pair, "replica", by)


def to_peer(sender, operand, power):
    branches = [partial(sender, by=1 << bit) for bit in range(DIST_KINDS)]
    return lax.switch(power, branches, operand)


def body(numerators, push_weights, step_power, activations, targets, gain):
    numer = numerators[0]
    power = step_power[0]
    features = activations.shape[2]
    replica_tokens = activations.shape[1] * lax.axis_size("fsdp")
    params = (numer / push_weights[0]).astype(jnp.bfloat16)
    act32 = activations[0].astype(jnp.float32)
    mean_sq = jnp.mean(act32 * act32, axis=1, keepdims=True)
    normed = (act32 * lax.rsqrt(mean_sq + 1e-05) * gain[None, :]).astype(jnp.bfloat16)
    columns = normed
    keys = jnp.dot(
        columns,
        lax.all_gather(params, "fsdp", axis=0, tiled=True),
        preferred_element_type=jnp.float32,
    ) / math.sqrt(features)
    errors = ((keys - targets[0].astype(jnp.float32)) / math.sqrt(replica_tokens)).astype(
        jnp.bfloat16
    )
    columns = normed
    grad = lax.psum_scatter(
        lax.dot_general(
            columns, errors, (((0,), (0,)), ((), ())), preferred_element_type=jnp.float32
        ).astype(jnp.bfloat16),
        "fsdp",
        scatter_dimension=0,
        tiled=True,
    ).astype(jnp.float32)
    updated = numer - 0.3 * grad
    peer_updated, peer_weight = to_peer(send_updated, (updated, push_weights), power)
    mixed_numerators = 0.5 * (updated + peer_updated)
    mixed_weights = 0.5 * (push_weights + peer_weight)
    return (mixed_numerators[None], mixed_weights)


def solution(mesh):
    return jax.shard_map(
        body,
        mesh=mesh,
        in_specs=(
            P("replica", "fsdp", None),
            P("replica"),
            P(),
            P("replica", "fsdp", None),
            P("replica", "fsdp", None),
            P(),
        ),
        out_specs=(P("replica", "fsdp", None), P("replica")),
        check_vma=False,
    )
```

profile of v0, /device:TPU:6, one launch (start us, length us, event | category | flops | bytes accessed | tf_op | source)
XLA Modules:
  0.0 219.2 jit_solution(8398441809625169285)
XLA Ops:
  7.2 0.0 copy-start
  7.2 0.0 copy-start.2
  7.2 0.0 all-gather.2.cloned.1.call-start
  8.0 2.0 fusion.8
  10.0 0.0 all-gather.2.cloned.1.call-update
  10.1 0.0 reduce-scatter.2.cloned.1.call-start
  10.1 2.6 %fusion = f32[384]{0:T(512)S(1)} fusion(bf16[1,384,4096]{2,1,0:T(8,128)(2,1)} %param.12), kind=kLoop, calls=%fused_computation.2 | loop fusion | flops 4718208 | bytes 3147264 | tf_op jit(solution)/shard_map/reduce_sum | solution.py:34
  12.7 81.7 %all-gather.2.cloned.1.call-done = bf16[4096,512]{1,0:T(8,128)(2,1)} async-done(((bf16[256,512]{1,0:T(8,128)(2,1)}), bf16[4096,512]{1,0:T(8,128)(2,1)}) %all-gather.2.cloned.1.call-update) | async-done | bytes 4194320 | tf_op jit(solution)/shard_map/all_gather | solution.py:39
  94.4 0.0 copy-done
  94.4 0.0 copy-done.2
  94.4 8.4 %convolution_convert_fusion = bf16[4096,512]{1,0:T(8,128)(2,1)} fusion(bf16[1,384,4096]{2,1,0:T(8,128)(2,1)S(1)} %copy-done, f32[4096]{0:T(1024)} %param.14, f32[384]{0:T(512)S(1)} %add_rsqrt_fusion, bf16[4096,512]{1,0:T(8,128)(2,1)} %all-gather.2.cloned.1.call-done, bf16[1,384,512]{2,1,0:T(8,128)(2,1)S(1)} %copy-done.2), kind=kOutput, calls=%fused_computation.5 | convolution fusion | flops 3236888576 | bytes 11945472 | tf_op jit(solution)/shard_map/dot_general | solution.py:47
  102.8 0.0 copy-start.1
  102.8 0.0 reduce-scatter.2.cloned.1.call-update
  103.5 82.4 %reduce-scatter.2.cloned.1.call-done = bf16[256,512]{1,0:T(8,128)(2,1)} async-done(((bf16[4096,512]{1,0:T(8,128)(2,1)}), bf16[256,512]{1,0:T(8,128)(2,1)}) %reduce-scatter.2.cloned.1.call-update) | async-done | bytes 262160 | tf_op jit(solution)/shard_map/reduce_scatter | solution.py:46
  185.9 0.0 copy-done.1
  185.9 1.0 bitcast_subtract_fusion
  186.9 21.7 %conditional.1 = (f32[256,512]{1,0:T(8,128)}, f32[1]{0:T(128)}) conditional(s32[]{:T(128)} %bitcast.5, (f32[256,512]{1,0:T(8,128)S(1)}, f32[1]{0:T(128)}) %tuple.20, (f32[256,512]{1,0:T(8,128)S(1)}, f32[1]{0:T(128)}) %tuple.20, (f32[256,512]{1,0:T(8,128)S(1)}, f32[1]{0:T(128)}) %tuple.20), branch_computations={%region_2.0_spmd, %region_3.0_spmd, %region_4.0_spmd} | conditional | bytes 2097264 | solution.py:24
  187.0 8.4 %collective-permute-start.4 = (f32[256,512]{1,0:T(8,128)S(1)}, f32[256,512]{1,0:T(8,128)}, u32[]{:S(2)}, u32[]{:S(2)}) collective-permute-start(f32[256,512]{1,0:T(8,128)S(1)} %get-tuple-element.16), channel_id=1, source_target_pairs={{0,64},{16,80},{32,96},{48,112},{64,128},{80,144},{96,160},{112,17... | collective-permute-start | bytes 1572872 | tf_op jit(solution)/shard_map/cond/branch_2_fun/ppermute | solution.py:15
  195.4 1.9 collective-permute-start.5
  197.3 11.3 %collective-permute-done.5 = f32[1]{0:T(128)} collective-permute-done((f32[1]{0:T(128)}, f32[1]{0:T(128)}, u32[]{:S(2)}, u32[]{:S(2)}) %collective-permute-start.5) | collective-permute-done | bytes 36 | tf_op jit(solution)/shard_map/cond/branch_2_fun/ppermute | solution.py:15
  208.6 0.0 collective-permute-done.4
  208.6 1.9 multiply_bitcast_fusion
  (1 shorter events, 0.0 us)
Async XLA Ops:
  7.2 87.3 %copy-start = (bf16[1,384,4096]{2,1,0:T(8,128)(2,1)S(1)}, bf16[1,384,4096]{2,1,0:T(8,128)(2,1)}, u32[]{:S(2)}) copy-start(bf16[1,384,4096]{2,1,0:T(8,128)(2,1)} %param.12) | copy-start | bytes 9437188
  7.2 87.3 %copy-start.2 = (bf16[1,384,512]{2,1,0:T(8,128)(2,1)S(1)}, bf16[1,384,512]{2,1,0:T(8,128)(2,1)}, u32[]{:S(2)}) copy-start(bf16[1,384,512]{2,1,0:T(8,128)(2,1)} %param.13) | copy-start | bytes 1179652
  7.2 87.2 %all-gather.2.cloned.1.call-start = ((), (), s32[]{:S(2)}) async-start(), calls=%async_computation.1 | async-start | bytes 4456448 | tf_op jit(solution)/shard_map/all_gather | solution.py:39
  10.1 175.9 %reduce-scatter.2.cloned.1.call-start = ((), (), s32[]{:S(2)}) async-start(), calls=%async_computation.2 | async-start | bytes 4456448 | tf_op jit(solution)/shard_map/reduce_scatter | solution.py:46
  102.8 83.1 %copy-start.1 = (f32[1,256,512]{2,1,0:T(8,128)S(1)}, f32[1,256,512]{2,1,0:T(8,128)}, u32[]{:S(2)}) copy-start(f32[1,256,512]{2,1,0:T(8,128)} %param.9) | copy-start | bytes 1572868
  187.0 21.7 %collective-permute-start.4 = (f32[256,512]{1,0:T(8,128)S(1)}, f32[256,512]{1,0:T(8,128)}, u32[]{:S(2)}, u32[]{:S(2)}) collective-permute-start(f32[256,512]{1,0:T(8,128)S(1)} %get-tuple-element.16), channel_id=1, source_target_pairs={{0,64},{16,80},{32,96},{48,112},{64,128},{80,144},{96,160},{112,17... | collective-permute-start | bytes 1572872 | tf_op jit(solution)/shard_map/cond/branch_2_fun/ppermute | solution.py:15
  195.4 13.2 %collective-permute-start.5 = (f32[1]{0:T(128)}, f32[1]{0:T(128)}, u32[]{:S(2)}, u32[]{:S(2)}) collective-permute-start(f32[1]{0:T(128)} %get-tuple-element.17), channel_id=1, source_target_pairs={{0,64},{16,80},{32,96},{48,112},{64,128},{80,144},{96,160},{112,17... | collective-permute-start | bytes 20 | tf_op jit(solution)/shard_map/cond/branch_2_fun/ppermute | solution.py:15
Sparse Core Ops, SparseCore 0:
  10.6 83.7 all-gather.1
  102.9 82.9 reduce-scatter.1
where the time goes:
time: 220 us; the launch traced here: 219 us
  waiting for transfers between devices  175 us (80%)
  between operations  17.3 us (8%)
  starting transfers between devices  10.4 us (5%)
  matrix products  8.36 us (4%)
  other arithmetic  7.54 us (3%)
    reduce_scatter x1, waiting for transfers between devices, body(): lax.psum_scatter(lax.dot_general(columns, errors, (((0,), (0,)), ((), ())...  82.4 us
    all_gather x1, waiting for transfers between devices, body(): lax.all_gather(params, 'fsdp', axis=0, tiled=True)  81.7 us
    ppermute x2, waiting for transfers between devices, passed_along(): return lax.ppermute(value, axis, pairs)  11.3 us
    ppermute x2, starting transfers between devices, passed_along(): return lax.ppermute(value, axis, pairs)  10.4 us
    dot_general x1, matrix products, body(): lax.dot_general(columns, errors, (((0,), (0,)), ((), ())), preferred_elem...  8.36 us
  transfers between devices with their start and end apart: 4, of which 3 were waited for; matrix products, arithmetic and copies ran while one was open for 1% of the time, Pallas kernels for 0%

commit v1 on v0

v1 whole, which is shorter than its diff:
```python
from functools import partial
import math

import jax
import jax.numpy as jnp
from jax import lax
from jax.sharding import Mesh, PartitionSpec as P

DIST_KINDS = 3
PAIR = 2


def passed_along(value, axis, steps):
    count = lax.axis_size(axis)
    pairs = [(source, (source + steps) % count) for source in range(count)]
    return lax.ppermute(value, axis, pairs)


def send_to_peer(pair, by):
    return passed_along(pair, "replica", by)


def to_peer(sender, operand, power):
    branches = [partial(sender, by=1 << bit) for bit in range(DIST_KINDS)]
    return lax.switch(power, branches, operand)


def body(numerators, push_weights, step_power, activations, targets, gain):
    numer = numerators[0]
    power = step_power[0]
    features = activations.shape[2]
    n_pair = lax.axis_size("fl")
    n_ring = lax.axis_size("fz")
    replica_tokens = activations.shape[1] * n_pair * n_ring
    params = (numer / push_weights[0]).astype(jnp.bfloat16)
    gathered = lax.all_gather(params, "fl", axis=0)
    gathered = lax.all_gather(gathered, "fz", axis=0)
    full_params = gathered.reshape(-1, params.shape[1])
    peer_numer, peer_weight = to_peer(send_to_peer, (numer, push_weights), power)
    act32 = activations[0].astype(jnp.float32)
    mean_sq = jnp.mean(act32 * act32, axis=1, keepdims=True)
    normed = (act32 * lax.rsqrt(mean_sq + 1e-05) * gain[None, :]).astype(jnp.bfloat16)
    tokens = normed.shape[0]
    normed = normed.reshape(tokens, n_pair, n_ring, -1).transpose(0, 2, 1, 3).reshape(tokens, -1)
    keys = jnp.dot(normed, full_params, preferred_element_type=jnp.float32) / math.sqrt(features)
    errors = ((keys - targets[0].astype(jnp.float32)) / math.sqrt(replica_tokens)).astype(
        jnp.bfloat16
    )
    peer_numer, peer_weight, errors = lax.optimization_barrier((peer_numer, peer_weight, errors))
    partial_grad = lax.dot_general(
        normed, errors, (((0,), (0,)), ((), ())), preferred_element_type=jnp.float32
    ).astype(jnp.bfloat16)
    blocks = partial_grad.reshape(n_ring, n_pair, -1, partial_grad.shape[1])
    grad16 = lax.psum_scatter(blocks, "fz", scatter_dimension=0)
    grad16 = lax.psum_scatter(grad16, "fl", scatter_dimension=0)
    peer_grad16 = to_peer(send_to_peer, grad16, power)
    updated = numer - 0.3 * grad16.astype(jnp.float32)
    peer_updated = peer_numer - 0.3 * peer_grad16.astype(jnp.float32)
    mixed_numerators = 0.5 * (updated + peer_updated)
    mixed_weights = 0.5 * (push_weights + peer_weight)
    return (mixed_numerators[None], mixed_weights)


def solution(mesh):
    n_replica, n_fsdp = mesh.devices.shape
    split = Mesh(mesh.devices.reshape(n_replica, PAIR, n_fsdp // PAIR), ("replica", "fl", "fz"))
    rows = P("replica", ("fl", "fz"), None)
    return jax.shard_map(
        body,
        mesh=split,
        in_specs=(rows, P("replica"), P(), rows, rows, P()),
        out_specs=(rows, P("replica")),
        check_vma=False,
    )
```

time: 220 us -> 194 us (0.88)
  waiting for transfers between devices: 175 us -> 137 us
  blocking collectives: 0 us -> 8.82 us
  local copies, waits for them, and re-layouts: 0.01 us -> 6.15 us
  other arithmetic: 7.54 us -> 4.86 us
    all_gather x1, waiting for transfers between devices: 81.7 us -> 38 us  [body(): gathered = lax.all_gather(gathered, 'fz', axis=0)]
    all_gather x0 -> x1, blocking collectives: none -> 8.82 us  [body(): gathered = lax.all_gather(params, 'fl', axis=0)]
    ppermute x2 -> x3, waiting for transfers between devices: 11.3 us -> 19.1 us  [passed_along(): return lax.ppermute(value, axis, pairs)]
    unnamed x6 -> x11, local copies, waits for them, and re-layouts: 0.01 us -> 5.71 us
    reduce_scatter x1 -> x2, waiting for transfers between devices: 82.4 us -> 79.7 us  [the longest x1 56.9 us: body(): grad16 = lax.psum_scatter(blocks, 'fz', scatter_dimension=0)]
    ppermute x2 -> x3, starting transfers between devices: 10.4 us -> 8.42 us  [passed_along(): return lax.ppermute(value, axis, pairs)]
    dot_general x1 -> x2, matrix products: 8.36 us -> 9.27 us  [the longest x1 4.97 us: body(): jnp.dot(normed, full_params, preferred_element_type=jnp.float32)]
  transfers between devices with their start and end apart: 4 -> 6, of which waited for: 3 -> 5; matrix products, arithmetic and copies ran while one was open for 1% -> 3% of each run, Pallas kernels for 0% -> 0%
where the time goes in v1:
time: 194 us; the launch traced here: 191 us
  waiting for transfers between devices  137 us (71%)
  between operations  16.9 us (9%)
  matrix products  9.27 us (5%)
  blocking collectives  8.82 us (5%)
  starting transfers between devices  8.54 us (4%)
  local copies, waits for them, and re-layouts  6.15 us (3%)
  other arithmetic  4.86 us (3%)
    reduce_scatter x1, waiting for transfers between devices, body(): grad16 = lax.psum_scatter(blocks, 'fz', scatter_dimension=0)  56.9 us
    all_gather x1, waiting for transfers between devices, body(): gathered = lax.all_gather(gathered, 'fz', axis=0)  38 us
    reduce_scatter x1, waiting for transfers between devices, body(): grad16 = lax.psum_scatter(grad16, 'fl', scatter_dimension=0)  22.8 us
    ppermute x3, waiting for transfers between devices, passed_along(): return lax.ppermute(value, axis, pairs)  19.1 us
    all_gather x1, blocking collectives, body(): gathered = lax.all_gather(params, 'fl', axis=0)  8.82 us
    ppermute x3, starting transfers between devices, passed_along(): return lax.ppermute(value, axis, pairs)  8.42 us
    unnamed x11, local copies, waits for them, and re-layouts  5.71 us
    dot_general x1, matrix products, body(): jnp.dot(normed, full_params, preferred_element_type=jnp.float32)  4.97 us
  transfers between devices with their start and end apart: 6, of which 5 were waited for; matrix products, arithmetic and copies ran while one was open for 3% of the time, Pallas kernels for 0%

profile of v1, /device:TPU:6, one launch (start us, length us, event | category | flops | bytes accessed | tf_op | source)
XLA Modules:
  0.0 191.4 jit_solution(17221124577360127879)
XLA Ops:
  7.2 0.0 all-gather.3.cloned.1.call-start
  7.9 0.0 copy-start.3
  7.9 1.1 divide_convert_fusion
  9.0 8.8 %all_gather.10 = bf16[2,256,512]{2,1,0:T(8,128)(2,1)} all-gather(bf16[1,256,512]{2,1,0:T(8,128)(2,1)S(1)} %divide_convert_fusion), channel_id=1, replica_groups=mesh['replica'=32,'fl'=2,'fz'=8] {'fl'}, dimensions={0}, use_global_device_ids=true | all-gather | bytes 786432 | tf_op jit(solution)/shard_map/all_gather | solution.py:36
  17.8 0.0 all-gather.3.cloned.1.call-update
  17.8 0.0 reduce-scatter.3.cloned.1.call-start
  17.8 3.4 %copy.14 = bf16[1,384,4096]{1,2,0:T(8,128)(2,1)S(1)} copy(bf16[1,384,4096]{2,1,0:T(8,128)(2,1)} %param.15) | data formatting | bytes 6291456 | tf_op args[3]
  21.3 0.0 copy-done.3
  22.0 0.8 multiply_reduce_fusion
  22.7 0.9 fusion
  23.6 0.0 copy-start
  23.6 1.7 copy-done
  25.3 0.4 copy.15
  25.7 0.6 copy-done.1
  26.3 16.4 %conditional.5 = (f32[256,512]{1,0:T(8,128)}, f32[1]{0:T(128)}) conditional(s32[]{:T(128)} %bitcast.4, (f32[256,512]{1,0:T(8,128)S(1)}, f32[1]{0:T(128)}) %tuple.59, (f32[256,512]{1,0:T(8,128)S(1)}, f32[1]{0:T(128)}) %tuple.60, (f32[256,512]{1,0:T(8,128)S(1)}, f32[1]{0:T(128)}) %tuple.61), branch_computations={%region_1.0_spmd, %region_2.0_spmd, %region_3.0_spmd} | conditional | bytes 2097264 | solution.py:25
  26.3 1.9 collective-permute-start
  28.2 4.6 %collective-permute-start.1 = (f32[1]{0:T(128)}, f32[1]{0:T(128)}, u32[]{:S(2)}, u32[]{:S(2)}) collective-permute-start(f32[1]{0:T(128)} %get-tuple-element.26), channel_id=1, source_target_pairs={{0,16},{16,32},{32,48},{48,64},{64,80},{80,96},{96,112},{112,128},... | collective-permute-start | bytes 20 | tf_op jit(solution)/shard_map/cond/branch_0_fun/ppermute | solution.py:16
  32.9 9.9 %collective-permute-done.1 = f32[1]{0:T(128)} collective-permute-done((f32[1]{0:T(128)}, f32[1]{0:T(128)}, u32[]{:S(2)}, u32[]{:S(2)}) %collective-permute-start.1) | collective-permute-done | bytes 36 | tf_op jit(solution)/shard_map/cond/branch_0_fun/ppermute | solution.py:16
  42.7 0.0 collective-permute-done
  42.7 38.0 %all-gather.3.cloned.1.call-done = bf16[16,256,512]{2,1,0:T(8,128)(2,1)} async-done(((bf16[2,256,512]{2,1,0:T(8,128)(2,1)}), bf16[16,256,512]{2,1,0:T(8,128)(2,1)}) %all-gather.3.cloned.1.call-update) | async-done | bytes 4194320 | tf_op jit(solution)/shard_map/all_gather | solution.py:37
  80.7 5.0 %fusion.4 = bf16[384,512]{1,0:T(8,128)(2,1)S(1)} fusion(bf16[8,2,256,512]{3,2,1,0:T(8,128)(2,1)} %bitcast.45, bf16[1,384,512]{2,1,0:T(8,128)(2,1)S(1)} %copy-done.4, bf16[384,8,2,256]{0,3,1,2:T(8,128)(2,1)} %copy-done), kind=kOutput, calls=%fused_computation.8 | convolution fusion | flops 1611595776 | bytes 8126464 | tf_op jit(solution)/shard_map/dot_general | solution.py:45
  85.7 4.3 %convolution_convert_fusion = bf16[4096,512]{1,0:T(8,128)(2,1)} fusion(bf16[384,4096]{0,1:T(8,128)(2,1)S(1)} %bitcast.37, bf16[384,512]{1,0:T(8,128)(2,1)S(1)} %fusion.4), kind=kOutput, calls=%fused_computation.2 | convolution fusion | flops 1612709888 | bytes 7733248 | tf_op jit(solution)/shard_map/dot_general | solution.py:50
  90.0 0.0 reduce-scatter.3.cloned.1.call-update
  90.0 0.0 reduce-scatter.5.cloned.1.call-start
  90.1 56.9 %reduce-scatter.3.cloned.1.call-done = bf16[1,2,256,512]{3,2,1,0:T(8,128)(2,1)} async-done(((bf16[8,2,256,512]{3,2,1,0:T(8,128)(2,1)}), bf16[1,2,256,512]{3,2,1,0:T(8,128)(2,1)}) %reduce-scatter.3.cloned.1.call-update) | async-done | bytes 524304 | tf_op jit(solution)/shard_map/reduce_scatter | solution.py:54
  147.0 0.0 reduce-scatter.5.cloned.1.call-update
  147.7 22.8 %reduce-scatter.5.cloned.1.call-done = bf16[1,256,512]{2,1,0:T(8,128)(2,1)} async-done(((bf16[2,256,512]{2,1,0:T(8,128)(2,1)}), bf16[1,256,512]{2,1,0:T(8,128)(2,1)}) %reduce-scatter.5.cloned.1.call-update) | async-done | bytes 262160 | tf_op jit(solution)/shard_map/reduce_scatter | solution.py:55
  170.4 11.1 %conditional.6 = (bf16[256,512]{1,0:T(8,128)(2,1)}) conditional(s32[]{:T(128)} %bitcast.4, bf16[256,512]{1,0:T(8,128)(2,1)} %bitcast.42, bf16[256,512]{1,0:T(8,128)(2,1)} %bitcast.43, bf16[256,512]{1,0:T(8,128)(2,1)} %bitcast.44), branch_computations={%region_6.0_spmd, %region_7.0_spmd, %region_8.0_spmd} | conditional | bytes 1048624
  170.4 1.9 collective-permute-start.6
  172.4 9.2 %collective-permute-done.6 = bf16[256,512]{1,0:T(8,128)(2,1)} collective-permute-done((bf16[256,512]{1,0:T(8,128)(2,1)}, bf16[256,512]{1,0:T(8,128)(2,1)}, u32[]{:S(2)}, u32[]{:S(2)}) %collective-permute-start.6) | collective-permute-done | bytes 262176 | tf_op jit(solution)/shard_map/cond/branch_0_fun/ppermute | solution.py:16
  181.6 0.0 copy-done.2
  181.6 2.1 %multiply_bitcast_fusion = f32[1,256,512]{2,1,0:T(8,128)} fusion(f32[256,512]{1,0:T(8,128)} %get-tuple-element.41, bf16[256,512]{1,0:T(8,128)(2,1)} %get-tuple-element.49, bf16[1,256,512]{2,1,0:T(8,128)(2,1)} %reduce-scatter.5.cloned.1.call-done, f32[1,256,512]{2,1,0:T(8,128)S(1)} %copy-done.2), kind=kLoop, calls=%fused_computation.9 | loop fusion | flops 1048576 | bytes 2097152 | tf_op jit(solution)/shard_map/broadcast_in_dim | solution.py:61
  (6 shorter events, 0.0 us)
Async XLA Ops:
  7.2 73.6 %all-gather.3.cloned.1.call-start = ((), (), s32[]{:S(2)}) async-start(), calls=%async_computation.4 | async-start | bytes 4718592 | tf_op jit(solution)/shard_map/all_gather | solution.py:37
  7.9 13.4 %copy-start.3 = (f32[4096]{0:T(1024)S(1)}, f32[4096]{0:T(1024)}, u32[]{:S(2)}) copy-start(f32[4096]{0:T(1024)} %param.17) | copy-start | bytes 49156
  17.8 129.2 %reduce-scatter.3.cloned.1.call-start = ((), (), s32[]{:S(2)}) async-start(), calls=%async_computation.2 | async-start | bytes 4718592 | tf_op jit(solution)/shard_map/reduce_scatter | solution.py:54
  23.6 1.7 copy-start
  25.3 1.0 copy-start.1
  25.3 55.5 %copy-start.4 = (bf16[1,384,512]{2,1,0:T(8,128)(2,1)S(1)}, bf16[1,384,512]{2,1,0:T(8,128)(2,1)}, u32[]{:S(2)}) copy-start(bf16[1,384,512]{2,1,0:T(8,128)(2,1)} %param.16) | copy-start | bytes 1179652
  26.3 16.4 %collective-permute-start = (f32[256,512]{1,0:T(8,128)S(1)}, f32[256,512]{1,0:T(8,128)}, u32[]{:S(2)}, u32[]{:S(2)}) collective-permute-start(f32[256,512]{1,0:T(8,128)S(1)} %get-tuple-element.25), channel_id=1, source_target_pairs={{0,16},{16,32},{32,48},{48,64},{64,80},{80,96},{96,112},{112,128},... | collective-permute-start | bytes 1572872 | tf_op jit(solution)/shard_map/cond/branch_0_fun/ppermute | solution.py:16
  28.2 14.5 %collective-permute-start.1 = (f32[1]{0:T(128)}, f32[1]{0:T(128)}, u32[]{:S(2)}, u32[]{:S(2)}) collective-permute-start(f32[1]{0:T(128)} %get-tuple-element.26), channel_id=1, source_target_pairs={{0,16},{16,32},{32,48},{48,64},{64,80},{80,96},{96,112},{112,128},... | collective-permute-start | bytes 20 | tf_op jit(solution)/shard_map/cond/branch_0_fun/ppermute | solution.py:16
  90.0 91.6 %copy-start.2 = (f32[1,256,512]{2,1,0:T(8,128)S(1)}, f32[1,256,512]{2,1,0:T(8,128)}, u32[]{:S(2)}) copy-start(f32[1,256,512]{2,1,0:T(8,128)} %param.12) | copy-start | bytes 1572868
  90.0 80.4 %reduce-scatter.5.cloned.1.call-start = ((), (), s32[]{:S(2)}) async-start(), calls=%async_computation.3 | async-start | bytes 786432 | tf_op jit(solution)/shard_map/reduce_scatter | solution.py:55
  170.4 11.1 %collective-permute-start.6 = (bf16[256,512]{1,0:T(8,128)(2,1)}, bf16[256,512]{1,0:T(8,128)(2,1)}, u32[]{:S(2)}, u32[]{:S(2)}) collective-permute-start(bf16[256,512]{1,0:T(8,128)(2,1)} %param.3), channel_id=1, source_target_pairs={{0,16},{16,32},{32,48},{48,64},{64,80},{80,96},{96,112},{112,128},... | collective-permute-start | bytes 786440 | tf_op jit(solution)/shard_map/cond/branch_0_fun/ppermute | solution.py:16
Sparse Core Ops, SparseCore 0:
  17.9 62.7 all-gather.2
  90.2 56.8 reduce-scatter.2
  149.8 20.5 reduce-scatter.4

commit v2 on v1

--- a/solution.py
+++ b/solution.py
@@ -18,6 +18,22 @@
 
 def send_to_peer(pair, by):
     return passed_along(pair, "replica", by)
+
+
+def finish_and_send(halves, by):
+    mine, other = halves
+    n_replica = lax.axis_size("replica")
+    n_pair = lax.axis_size("fl")
+    flip = [(side, n_pair - 1 - side) for side in range(n_pair)]
+    diagonal = [
+        (r * n_pair + side, ((r + by) % n_replica) * n_pair + n_pair - 1 - side)
+        for r in range(n_replica)
+        for side in range(n_pair)
+    ]
+    from_partner = lax.ppermute(other, "fl", flip)
+    peer_mine = passed_along(mine, "replica", by)
+    peer_other = lax.ppermute(other, ("replica", "fl"), diagonal)
+    return from_partner, peer_mine, peer_other
 
 
 def to_peer(sender, operand, power):
@@ -51,11 +67,15 @@
         normed, errors, (((0,), (0,)), ((), ())), preferred_element_type=jnp.float32
     ).astype(jnp.bfloat16)
     blocks = partial_grad.reshape(n_ring, n_pair, -1, partial_grad.shape[1])
-    grad16 = lax.psum_scatter(blocks, "fz", scatter_dimension=0)
-    grad16 = lax.psum_scatter(grad16, "fl", scatter_dimension=0)
-    peer_grad16 = to_peer(send_to_peer, grad16, power)
-    updated = numer - 0.3 * grad16.astype(jnp.float32)
-    peer_updated = peer_numer - 0.3 * peer_grad16.astype(jnp.float32)
+    halves = lax.psum_scatter(blocks, "fz", scatter_dimension=0)
+    side = lax.axis_index("fl")
+    mine = lax.dynamic_index_in_dim(halves, side, 0, keepdims=False)
+    other = lax.dynamic_index_in_dim(halves, n_pair - 1 - side, 0, keepdims=False)
+    from_partner, peer_mine, peer_other = to_peer(finish_and_send, (mine, other), power)
+    grad = mine.astype(jnp.float32) + from_partner.astype(jnp.float32)
+    peer_grad = peer_mine.astype(jnp.float32) + peer_other.astype(jnp.float32)
+    updated = numer - 0.3 * grad
+    peer_updated = peer_numer - 0.3 * peer_grad
     mixed_numerators = 0.5 * (updated + peer_updated)
     mixed_weights = 0.5 * (push_weights + peer_weight)
     return (mixed_numerators[None], mixed_weights)

time: 194 us -> 196 us (1.010)
  waiting for transfers between devices: 137 us -> 117 us
  starting transfers between devices: 8.54 us -> 25.6 us
    reduce_scatter x2 -> x1, waiting for transfers between devices: 79.7 us -> 56.2 us  [body(): halves = lax.psum_scatter(blocks, 'fz', scatter_dimension=0)]
    ppermute x0 -> x2, waiting for transfers between devices: none -> 19.5 us  [the longest x1 19.5 us: finish_and_send(): peer_other = lax.ppermute(other, ('replica', 'fl'), diagonal)]
    ppermute x0 -> x2, starting transfers between devices: none -> 9.85 us  [the longest x1 6.46 us: finish_and_send(): peer_other = lax.ppermute(other, ('replica', 'fl'), diagonal)]
    all_gather x1, waiting for transfers between devices: 38 us -> 29.3 us  [body(): gathered = lax.all_gather(gathered, 'fz', axis=0)]
    ppermute x3, waiting for transfers between devices: 19.1 us -> 11.7 us  [passed_along(): return lax.ppermute(value, axis, pairs)]
    ppermute x3, starting transfers between devices: 8.42 us -> 15.7 us  [passed_along(): return lax.ppermute(value, axis, pairs)]
  transfers between devices with their start and end apart: 6 -> 7, of which waited for: 5 -> 4; matrix products, arithmetic and copies ran while one was open for 3% -> 3% of each run, Pallas kernels for 0% -> 0%
where the time goes in v2:
time: 196 us; the launch traced here: 192 us
  waiting for transfers between devices  117 us (60%)
  starting transfers between devices  25.6 us (13%)
  between operations  17.3 us (9%)
  matrix products  9.26 us (5%)
  blocking collectives  8.82 us (4%)
  local copies, waits for them, and re-layouts  8.07 us (4%)
  other arithmetic  5.95 us (3%)
    reduce_scatter x1, waiting for transfers between devices, body(): halves = lax.psum_scatter(blocks, 'fz', scatter_dimension=0)  56.2 us
    all_gather x1, waiting for transfers between devices, body(): gathered = lax.all_gather(gathered, 'fz', axis=0)  29.3 us
    ppermute x1, waiting for transfers between devices, finish_and_send(): peer_other = lax.ppermute(other, ('replica', 'fl'), diagonal)  19.5 us
    ppermute x3, starting transfers between devices, passed_along(): return lax.ppermute(value, axis, pairs)  15.7 us
    ppermute x3, waiting for transfers between devices, passed_along(): return lax.ppermute(value, axis, pairs)  11.7 us
    all_gather x1, blocking collectives, body(): gathered = lax.all_gather(params, 'fl', axis=0)  8.82 us
    ppermute x1, starting transfers between devices, finish_and_send(): peer_other = lax.ppermute(other, ('replica', 'fl'), diagonal)  6.46 us
    unnamed x11, local copies, waits for them, and re-layouts  5.76 us
  transfers between devices with their start and end apart: 7, of which 4 were waited for; matrix products, arithmetic and copies ran while one was open for 3% of the time, Pallas kernels for 0%

profile of v2, /device:TPU:6, one launch (start us, length us, event | category | flops | bytes accessed | tf_op | source)
XLA Modules:
  0.0 192.0 jit_solution(10832551255822989269)
XLA Ops:
  7.2 0.0 all-gather.3.cloned.1.call-start
  7.9 1.1 divide_convert_fusion
  9.0 8.8 %all_gather.10 = bf16[2,256,512]{2,1,0:T(8,128)(2,1)} all-gather(bf16[1,256,512]{2,1,0:T(8,128)(2,1)S(1)} %divide_convert_fusion), channel_id=1, replica_groups=mesh['replica'=32,'fl'=2,'fz'=8] {'fl'}, dimensions={0}, use_global_device_ids=true | all-gather | bytes 786432 | tf_op jit(solution)/shard_map/all_gather | solution.py:52
  17.8 0.0 all-gather.3.cloned.1.call-update
  17.8 0.0 reduce-scatter.2.cloned.1.call-start
  17.8 3.4 %copy.14 = bf16[1,384,4096]{1,2,0:T(8,128)(2,1)S(1)} copy(bf16[1,384,4096]{2,1,0:T(8,128)(2,1)} %param.15) | data formatting | bytes 6291456 | tf_op args[3]
  22.0 0.8 multiply_reduce_fusion
  22.7 0.9 fusion
  23.6 1.7 copy-done
  25.3 0.4 copy.15
  25.7 0.7 copy-done.1
  26.3 25.1 %conditional.3 = (f32[256,512]{1,0:T(8,128)}, f32[1]{0:T(128)}) conditional(s32[]{:T(128)} %bitcast.7, (f32[256,512]{1,0:T(8,128)S(1)}, f32[1]{0:T(128)}) %tuple.72, (f32[256,512]{1,0:T(8,128)S(1)}, f32[1]{0:T(128)}) %tuple.73, (f32[256,512]{1,0:T(8,128)S(1)}, f32[1]{0:T(128)}) %tuple.74), branch_computations={%region_1.0_spmd, %region_2.0_spmd, %region_3.0_spmd} | conditional | bytes 2097264 | solution.py:41
  26.3 7.7 %collective-permute-start.4 = (f32[256,512]{1,0:T(8,128)S(1)}, f32[256,512]{1,0:T(8,128)}, u32[]{:S(2)}, u32[]{:S(2)}) collective-permute-start(f32[256,512]{1,0:T(8,128)S(1)} %get-tuple-element.79), channel_id=1, source_target_pairs={{0,64},{16,80},{32,96},{48,112},{64,128},{80,144},{96,160},{112,17... | collective-permute-start | bytes 1572872 | tf_op jit(solution)/shard_map/cond/branch_2_fun/ppermute | solution.py:16
  34.0 5.6 %collective-permute-start.5 = (f32[1]{0:T(128)}, f32[1]{0:T(128)}, u32[]{:S(2)}, u32[]{:S(2)}) collective-permute-start(f32[1]{0:T(128)} %get-tuple-element.80), channel_id=1, source_target_pairs={{0,64},{16,80},{32,96},{48,112},{64,128},{80,144},{96,160},{112,17... | collective-permute-start | bytes 20 | tf_op jit(solution)/shard_map/cond/branch_2_fun/ppermute | solution.py:16
  39.7 11.7 %collective-permute-done.5 = f32[1]{0:T(128)} collective-permute-done((f32[1]{0:T(128)}, f32[1]{0:T(128)}, u32[]{:S(2)}, u32[]{:S(2)}) %collective-permute-start.5) | collective-permute-done | bytes 36 | tf_op jit(solution)/shard_map/cond/branch_2_fun/ppermute | solution.py:16
  51.4 0.0 collective-permute-done.4
  51.4 29.3 %all-gather.3.cloned.1.call-done = bf16[16,256,512]{2,1,0:T(8,128)(2,1)} async-done(((bf16[2,256,512]{2,1,0:T(8,128)(2,1)}), bf16[16,256,512]{2,1,0:T(8,128)(2,1)}) %all-gather.3.cloned.1.call-update) | async-done | bytes 4194320 | tf_op jit(solution)/shard_map/all_gather | solution.py:53
  80.7 5.0 %fusion.4 = bf16[384,512]{1,0:T(8,128)(2,1)S(1)} fusion(bf16[8,2,256,512]{3,2,1,0:T(8,128)(2,1)} %bitcast.48, bf16[1,384,512]{2,1,0:T(8,128)(2,1)S(1)} %copy-done.4, bf16[384,8,2,256]{0,3,1,2:T(8,128)(2,1)} %copy-done), kind=kOutput, calls=%fused_computation.14 | convolution fusion | flops 1611595776 | bytes 8126464 | tf_op jit(solution)/shard_map/dot_general | solution.py:61
  85.7 4.3 %convolution_convert_fusion = bf16[4096,512]{1,0:T(8,128)(2,1)} fusion(bf16[384,4096]{0,1:T(8,128)(2,1)S(1)} %bitcast.44, bf16[384,512]{1,0:T(8,128)(2,1)S(1)} %fusion.4), kind=kOutput, calls=%fused_computation.8 | convolution fusion | flops 1612709888 | bytes 7733248 | tf_op jit(solution)/shard_map/dot_general | solution.py:66
  90.0 0.0 reduce-scatter.2.cloned.1.call-update
  90.0 0.0 copy-start.2
  90.8 56.2 %reduce-scatter.2.cloned.1.call-done = bf16[1,2,256,512]{3,2,1,0:T(8,128)(2,1)} async-done(((bf16[8,2,256,512]{3,2,1,0:T(8,128)(2,1)}), bf16[1,2,256,512]{3,2,1,0:T(8,128)(2,1)}) %reduce-scatter.2.cloned.1.call-update) | async-done | bytes 524304 | tf_op jit(solution)/shard_map/reduce_scatter | solution.py:70
  147.0 1.0 dynamic-slice_bitcast_fusion.3
  148.0 33.8 %conditional.5 = (bf16[256,512]{1,0:T(8,128)(2,1)}, f32[256,512]{1,0:T(8,128)S(1)}, f32[256,512]{1,0:T(8,128)S(1)}) conditional(s32[]{:T(128)} %bitcast.7, (bf16[256,512]{1,0:T(8,128)(2,1)S(1)}, s32[]{:T(128)}, bf16[1,2,256,512]{3,2,1,0:T(8,128)(2,1)}) %tuple.53, (bf16[256,512]{1,0:T(8,128)(2,1)S(1)}, s32[]{:T(128)}, ...), branch_computations={%region_5.6_spmd, %region_6.7_spmd, %region_7.8_spmd} | conditional | flops 524292 | bytes 5505218
  148.0 1.0 dynamic-slice_bitcast_fusion.2
  149.0 3.4 %collective-permute-start.14 = (bf16[256,512]{1,0:T(8,128)(2,1)S(1)}, bf16[256,512]{1,0:T(8,128)(2,1)S(1)}, u32[]{:S(2)}, u32[]{:S(2)}) collective-permute-start(bf16[256,512]{1,0:T(8,128)(2,1)S(1)} %dynamic-slice_bitcast_fusion.2), channel_id=1, source_target_pairs={{0,8},{8,0},{1,9},{9,1},{2,10},{10,2},{3,11},{11,3},{4,12},{12,4},... | collective-permute-start | bytes 786440 | tf_op jit(solution)/shard_map/cond/branch_2_fun/ppermute | solution.py:33
  152.4 6.5 %collective-permute-start.13 = (bf16[256,512]{1,0:T(8,128)(2,1)S(1)}, bf16[256,512]{1,0:T(8,128)(2,1)S(1)}, u32[]{:S(2)}, u32[]{:S(2)}) collective-permute-start(bf16[256,512]{1,0:T(8,128)(2,1)S(1)} %dynamic-slice_bitcast_fusion.2), channel_id=1, source_target_pairs={{0,72},{8,64},{16,88},{24,80},{32,104},{40,96},{48,120},{56,112},{... | collective-permute-start | bytes 786440 | tf_op jit(solution)/shard_map/cond/branch_2_fun/ppermute | solution.py:35
  158.8 2.4 %collective-permute-start.12 = (bf16[256,512]{1,0:T(8,128)(2,1)S(1)}, bf16[256,512]{1,0:T(8,128)(2,1)}, u32[]{:S(2)}, u32[]{:S(2)}) collective-permute-start(bf16[256,512]{1,0:T(8,128)(2,1)S(1)} %get-tuple-element.87), channel_id=1, source_target_pairs={{0,64},{16,80},{32,96},{48,112},{64,128},{80,144},{96,160},{112,17... | collective-permute-start | bytes 786440 | tf_op jit(solution)/shard_map/cond/branch_2_fun/ppermute | solution.py:16
  161.2 0.1 convert_element_type.83
  161.3 19.5 %collective-permute-done.13 = bf16[256,512]{1,0:T(8,128)(2,1)S(1)} collective-permute-done((bf16[256,512]{1,0:T(8,128)(2,1)S(1)}, bf16[256,512]{1,0:T(8,128)(2,1)S(1)}, u32[]{:S(2)}, u32[]{:S(2)}) %collective-permute-start.13) | collective-permute-done | bytes 262176 | tf_op jit(solution)/shard_map/cond/branch_2_fun/ppermute | solution.py:35
  180.8 1.0 convert_add_fusion.2
  181.8 2.2 %multiply_bitcast_fusion = f32[1,256,512]{2,1,0:T(8,128)} fusion(f32[256,512]{1,0:T(8,128)} %get-tuple-element.103, f32[256,512]{1,0:T(8,128)S(1)} %get-tuple-element.104, f32[256,512]{1,0:T(8,128)S(1)} %get-tuple-element.110, f32[1,256,512]{2,1,0:T(8,128)S(1)} %copy-done.2, bf16[1,2,256,512]{3,2,1,0:T(8,128)(2,1)} %reduce-scatter.2.cloned.1.call-done, ...), kind=kLoop, calls=%fused_computation.15 | loop fusion | flops 1048576 | bytes 2883588 | tf_op jit(solution)/shard_map/broadcast_in_dim | solution.py:81
  (11 shorter events, 0.0 us)
Async XLA Ops:
  7.2 73.6 %all-gather.3.cloned.1.call-start = ((), (), s32[]{:S(2)}) async-start(), calls=%async_computation.2 | async-start | bytes 4718592 | tf_op jit(solution)/shard_map/all_gather | solution.py:53
  7.9 13.4 %copy-start.3 = (f32[4096]{0:T(1024)S(1)}, f32[4096]{0:T(1024)}, u32[]{:S(2)}) copy-start(f32[4096]{0:T(1024)} %param.17) | copy-start | bytes 49156
  17.8 129.2 %reduce-scatter.2.cloned.1.call-start = ((), (), s32[]{:S(2)}) async-start(), calls=%async_computation.1 | async-start | bytes 4718592 | tf_op jit(solution)/shard_map/reduce_scatter | solution.py:70
  23.6 1.7 copy-start
  25.3 1.0 copy-start.1
  25.3 55.5 %copy-start.4 = (bf16[1,384,512]{2,1,0:T(8,128)(2,1)S(1)}, bf16[1,384,512]{2,1,0:T(8,128)(2,1)}, u32[]{:S(2)}) copy-start(bf16[1,384,512]{2,1,0:T(8,128)(2,1)} %param.16) | copy-start | bytes 1179652
  26.3 25.1 %collective-permute-start.4 = (f32[256,512]{1,0:T(8,128)S(1)}, f32[256,512]{1,0:T(8,128)}, u32[]{:S(2)}, u32[]{:S(2)}) collective-permute-start(f32[256,512]{1,0:T(8,128)S(1)} %get-tuple-element.79), channel_id=1, source_target_pairs={{0,64},{16,80},{32,96},{48,112},{64,128},{80,144},{96,160},{112,17... | collective-permute-start | bytes 1572872 | tf_op jit(solution)/shard_map/cond/branch_2_fun/ppermute | solution.py:16
  34.0 17.4 %collective-permute-start.5 = (f32[1]{0:T(128)}, f32[1]{0:T(128)}, u32[]{:S(2)}, u32[]{:S(2)}) collective-permute-start(f32[1]{0:T(128)} %get-tuple-element.80), channel_id=1, source_target_pairs={{0,64},{16,80},{32,96},{48,112},{64,128},{80,144},{96,160},{112,17... | collective-permute-start | bytes 20 | tf_op jit(solution)/shard_map/cond/branch_2_fun/ppermute | solution.py:16
  90.0 91.8 %copy-start.2 = (f32[1,256,512]{2,1,0:T(8,128)S(1)}, f32[1,256,512]{2,1,0:T(8,128)}, u32[]{:S(2)}) copy-start(f32[1,256,512]{2,1,0:T(8,128)} %param.12) | copy-start | bytes 1572868
  149.0 12.2 %collective-permute-start.14 = (bf16[256,512]{1,0:T(8,128)(2,1)S(1)}, bf16[256,512]{1,0:T(8,128)(2,1)S(1)}, u32[]{:S(2)}, u32[]{:S(2)}) collective-permute-start(bf16[256,512]{1,0:T(8,128)(2,1)S(1)} %dynamic-slice_bitcast_fusion.2), channel_id=1, source_target_pairs={{0,8},{8,0},{1,9},{9,1},{2,10},{10,2},{3,11},{11,3},{4,12},{12,4},... | collective-permute-start | bytes 786440 | tf_op jit(solution)/shard_map/cond/branch_2_fun/ppermute | solution.py:33
  152.4 28.4 %collective-permute-start.13 = (bf16[256,512]{1,0:T(8,128)(2,1)S(1)}, bf16[256,512]{1,0:T(8,128)(2,1)S(1)}, u32[]{:S(2)}, u32[]{:S(2)}) collective-permute-start(bf16[256,512]{1,0:T(8,128)(2,1)S(1)} %dynamic-slice_bitcast_fusion.2), channel_id=1, source_target_pairs={{0,72},{8,64},{16,88},{24,80},{32,104},{40,96},{48,120},{56,112},{... | collective-permute-start | bytes 786440 | tf_op jit(solution)/shard_map/cond/branch_2_fun/ppermute | solution.py:35
  158.8 21.9 %collective-permute-start.12 = (bf16[256,512]{1,0:T(8,128)(2,1)S(1)}, bf16[256,512]{1,0:T(8,128)(2,1)}, u32[]{:S(2)}, u32[]{:S(2)}) collective-permute-start(bf16[256,512]{1,0:T(8,128)(2,1)S(1)} %get-tuple-element.87), channel_id=1, source_target_pairs={{0,64},{16,80},{32,96},{48,112},{64,128},{80,144},{96,160},{112,17... | collective-permute-start | bytes 786440 | tf_op jit(solution)/shard_map/cond/branch_2_fun/ppermute | solution.py:16
Sparse Core Ops, SparseCore 0:
  17.9 62.7 all-gather.2
  90.1 56.8 reduce-scatter.1

commit v3 on v2

--- a/solution.py
+++ b/solution.py
@@ -36,6 +36,29 @@
     return from_partner, peer_mine, peer_other
 
 
+def ring_gather(block):
+    n = lax.axis_size("fz")
+    forward = [(i, (i + 1) % n) for i in range(n)]
+    backward = [(i, (i - 1) % n) for i in range(n)]
+    by_offset = {0: block}
+    ahead = behind = block
+    for k in range(1, n // 2 + 1):
+        ahead = lax.ppermute(ahead, "fz", forward)
+        by_offset[(n - k) % n] = ahead
+    for k in range(1, (n - 1) // 2 + 1):
+        behind = lax.ppermute(behind, "fz", backward)
+        by_offset[k] = behind
+    stacked = jnp.stack([by_offset[o] for o in range(n)])
+    doubled = jnp.concatenate([stacked, stacked])
+    start = (n - lax.axis_index("fz")) % n
+    return lax.dynamic_slice_in_dim(doubled, start, n, axis=0)
+
+
+def gather_and_send(operand, by):
+    numer, weight, block = operand
+    return passed_along((numer, weight), "replica", by), ring_gather(block)
+
+
 def to_peer(sender, operand, power):
     branches = [partial(sender, by=1 << bit) for bit in range(DIST_KINDS)]
     return lax.switch(power, branches, operand)
@@ -50,9 +73,12 @@
     replica_tokens = activations.shape[1] * n_pair * n_ring
     params = (numer / push_weights[0]).astype(jnp.bfloat16)
     gathered = lax.all_gather(params, "fl", axis=0)
-    gathered = lax.all_gather(gathered, "fz", axis=0)
-    full_params = gathered.reshape(-1, params.shape[1])
-    peer_numer, peer_weight = to_peer(send_to_peer, (numer, push_weights), power)
+    half = gathered.shape[-1] // 2
+    on_sparse = lax.all_gather(gathered[..., :half], "fz", axis=0)
+    (peer_numer, peer_weight), on_ring = to_peer(
+        gather_and_send, (numer, push_weights, gathered[..., half:]), power
+    )
+    full_params = jnp.concatenate([on_sparse, on_ring], axis=-1).reshape(-1, params.shape[1])
     act32 = activations[0].astype(jnp.float32)
     mean_sq = jnp.mean(act32 * act32, axis=1, keepdims=True)
     normed = (act32 * lax.rsqrt(mean_sq + 1e-05) * gain[None, :]).astype(jnp.bfloat16)
@@ -62,7 +88,6 @@
     errors = ((keys - targets[0].astype(jnp.float32)) / math.sqrt(replica_tokens)).astype(
         jnp.bfloat16
     )
-    peer_numer, peer_weight, errors = lax.optimization_barrier((peer_numer, peer_weight, errors))
     partial_grad = lax.dot_general(
         normed, errors, (((0,), (0,)), ((), ())), preferred_element_type=jnp.float32
     ).astype(jnp.bfloat16)

time: 196 us -> 212 us (1.082); the launches traced: 192 us -> 211 us
  waiting for transfers between devices: 117 us -> 92.6 us
  local copies, waits for them, and re-layouts: 8.07 us -> 30.9 us
  starting transfers between devices: 25.6 us -> 46 us
    ppermute x0 -> x7, starting transfers between devices: none -> 29.9 us  [the longest x3 19.9 us: ring_gather(): behind = lax.ppermute(behind, 'fz', backward)]
    all_gather x1, waiting for transfers between devices: 29.3 us -> 0.01 us  [body(): on_sparse = lax.all_gather(gathered[..., :half], 'fz', axis=0)]
    ppermute x0 -> x7, waiting for transfers between devices: none -> 19.7 us  [the longest x4 15.3 us: ring_gather(): ahead = lax.ppermute(ahead, 'fz', forward)]
    cond x0 -> x19, local copies, waits for them, and re-layouts: none -> 19.4 us
    ppermute x1, waiting for transfers between devices: 19.5 us -> 10.5 us  [finish_and_send(): peer_other = lax.ppermute(other, ('replica', 'fl'), diagonal)]
    ppermute x3, waiting for transfers between devices: 11.7 us -> 6.12 us  [passed_along(): return lax.ppermute(value, axis, pairs)]
    ppermute x3, starting transfers between devices: 15.7 us -> 10.7 us  [passed_along(): return lax.ppermute(value, axis, pairs)]
    ppermute x1, starting transfers between devices: 6.46 us -> 1.92 us  [finish_and_send(): peer_other = lax.ppermute(other, ('replica', 'fl'), diagonal)]
  transfers between devices with their start and end apart: 7 -> 14, of which waited for: 4 -> 9; matrix products, arithmetic and copies ran while one was open for 3% -> 14% of each run, Pallas kernels for 0% -> 0%
where the time goes in v3:
time: 212 us; the launch traced here: 211 us
  waiting for transfers between devices  92.6 us (44%)
  starting transfers between devices  46 us (22%)
  local copies, waits for them, and re-layouts  30.9 us (15%)
  between operations  17.2 us (8%)
  matrix products  9.3 us (4%)
  blocking collectives  8.71 us (4%)
  other arithmetic  6.11 us (3%)
    reduce_scatter x1, waiting for transfers between devices, body(): halves = lax.psum_scatter(blocks, 'fz', scatter_dimension=0)  56.1 us
    ppermute x3, starting transfers between devices, ring_gather(): behind = lax.ppermute(behind, 'fz', backward)  19.9 us
    cond x19, local copies, waits for them, and re-layouts  19.4 us
    ppermute x4, waiting for transfers between devices, ring_gather(): ahead = lax.ppermute(ahead, 'fz', forward)  15.3 us
    ppermute x3, starting transfers between devices, passed_along(): return lax.ppermute(value, axis, pairs)  10.7 us
    ppermute x1, waiting for transfers between devices, finish_and_send(): peer_other = lax.ppermute(other, ('replica', 'fl'), diagonal)  10.5 us
    ppermute x4, starting transfers between devices, ring_gather(): ahead = lax.ppermute(ahead, 'fz', forward)  10 us
    all_gather x1, blocking collectives, body(): gathered = lax.all_gather(params, 'fl', axis=0)  8.71 us
  transfers between devices with their start and end apart: 14, of which 9 were waited for; matrix products, arithmetic and copies ran while one was open for 14% of the time, Pallas kernels for 0%

profile of v3, /device:TPU:6, one launch (start us, length us, event | category | flops | bytes accessed | tf_op | source)
XLA Modules:
  0.0 211.0 jit_solution(15920396979594347992)
XLA Ops:
  9.0 8.7 %all_gather.10 = bf16[2,256,512]{2,1,0:T(8,128)(2,1)S(1)} all-gather(bf16[1,256,512]{2,1,0:T(8,128)(2,1)S(1)} %divide_convert_fusion), channel_id=1, replica_groups=mesh['replica'=32,'fl'=2,'fz'=8] {'fl'}, dimensions={0}, use_global_device_ids=true | all-gather | bytes 786432 | tf_op jit(solution)/shard_map/all_gather | solution.py:75
  19.1 3.4 %copy.11 = bf16[1,384,4096]{1,2,0:T(8,128)(2,1)S(1)} copy(bf16[1,384,4096]{2,1,0:T(8,128)(2,1)} %param.15) | data formatting | bytes 6291456 | tf_op args[3]
  25.8 79.2 %conditional.3 = (f32[256,512]{1,0:T(8,128)}, f32[1]{0:T(128)}, bf16[8,2,256,256]{3,2,1,0:T(8,128)(2,1)}) conditional(s32[]{:T(128)} %bitcast.33, (f32[256,512]{1,0:T(8,128)}, f32[1]{0:T(128)}, bf16[2,256,256]{2,1,0:T(8,128)(2,1)S(1)}) %tuple.50, (f32[256,512]{1,0:T(8,128)}, f32[1]{0:T(128)}, ...), branch_computations={%region_1.2_spmd, %region_2.3_spmd, %region_3.4_spmd} | conditional | flops 17 | bytes 24117876 | solution.py:64
  25.8 4.3 %collective-permute-start.5 = (bf16[2,256,256]{2,1,0:T(8,128)(2,1)S(1)}, bf16[2,256,256]{2,1,0:T(8,128)(2,1)S(1)}, u32[]{:S(2)}, u32[]{:S(2)}) collective-permute-start(bf16[2,256,256]{2,1,0:T(8,128)(2,1)S(1)} %get-tuple-element.83), channel_id=1, source_target_pairs={{0,1},{1,2},{2,3},{3,4},{4,5},{5,6},{6,7},{7,0},{8,9},{9,10},{10,1... | collective-permute-start | bytes 786440 | tf_op jit(solution)/shard_map/cond/branch_0_fun/ppermute | solution.py:46
  30.1 8.6 %collective-permute-start.2 = (bf16[2,256,256]{2,1,0:T(8,128)(2,1)S(1)}, bf16[2,256,256]{2,1,0:T(8,128)(2,1)}, u32[]{:S(2)}, u32[]{:S(2)}) collective-permute-start(bf16[2,256,256]{2,1,0:T(8,128)(2,1)S(1)} %get-tuple-element.83), channel_id=1, source_target_pairs={{0,7},{1,0},{2,1},{3,2},{4,3},{5,4},{6,5},{7,6},{8,15},{9,8},{10,9... | collective-permute-start | bytes 786440 | tf_op jit(solution)/shard_map/cond/branch_0_fun/ppermute | solution.py:49
  38.7 4.9 %collective-permute-done.5 = bf16[2,256,256]{2,1,0:T(8,128)(2,1)S(1)} collective-permute-done((bf16[2,256,256]{2,1,0:T(8,128)(2,1)S(1)}, bf16[2,256,256]{2,1,0:T(8,128)(2,1)S(1)}, u32[]{:S(2)}, u32[]{:S(2)}) %collective-permute-start.5) | collective-permute-done | bytes 262176 | tf_op jit(solution)/shard_map/cond/branch_0_fun/ppermute | solution.py:46
  43.6 1.9 collective-permute-start.6
  45.5 2.6 %collective-permute-done.2 = bf16[2,256,256]{2,1,0:T(8,128)(2,1)} collective-permute-done((bf16[2,256,256]{2,1,0:T(8,128)(2,1)S(1)}, bf16[2,256,256]{2,1,0:T(8,128)(2,1)}, u32[]{:S(2)}, u32[]{:S(2)}) %collective-permute-start.2) | collective-permute-done | bytes 262176 | tf_op jit(solution)/shard_map/cond/branch_0_fun/ppermute | solution.py:49
  48.1 5.7 %collective-permute-start.3 = (bf16[2,256,256]{2,1,0:T(8,128)(2,1)}, bf16[2,256,256]{2,1,0:T(8,128)(2,1)}, u32[]{:S(2)}, u32[]{:S(2)}) collective-permute-start(bf16[2,256,256]{2,1,0:T(8,128)(2,1)} %collective-permute-done.2), channel_id=1, source_target_pairs={{0,7},{1,0},{2,1},{3,2},{4,3},{5,4},{6,5},{7,6},{8,15},{9,8},{10,9... | collective-permute-start | bytes 786440 | tf_op jit(solution)/shard_map/cond/branch_0_fun/ppermute | solution.py:49
  53.9 1.9 collective-permute-start
  55.8 4.4 %collective-permute-start.1 = (f32[1]{0:T(128)}, f32[1]{0:T(128)}, u32[]{:S(2)}, u32[]{:S(2)}) collective-permute-start(f32[1]{0:T(128)} %get-tuple-element.82), channel_id=1, source_target_pairs={{0,16},{16,32},{32,48},{48,64},{64,80},{80,96},{96,112},{112,128},... | collective-permute-start | bytes 20 | tf_op jit(solution)/shard_map/cond/branch_0_fun/ppermute | solution.py:16
  60.2 1.9 collective-permute-start.7
  62.9 1.8 collective-permute-done.3
  64.7 5.6 %collective-permute-start.4 = (bf16[2,256,256]{2,1,0:T(8,128)(2,1)}, bf16[2,256,256]{2,1,0:T(8,128)(2,1)S(1)}, u32[]{:S(2)}, u32[]{:S(2)}) collective-permute-start(bf16[2,256,256]{2,1,0:T(8,128)(2,1)} %collective-permute-done.3), channel_id=1, source_target_pairs={{0,7},{1,0},{2,1},{3,2},{4,3},{5,4},{6,5},{7,6},{8,15},{9,8},{10,9... | collective-permute-start | bytes 786440 | tf_op jit(solution)/shard_map/cond/branch_0_fun/ppermute | solution.py:49
  70.3 1.7 bitcast_dynamic-update-slice_fusion.12
  72.0 3.4 %collective-permute-done.7 = bf16[2,256,256]{2,1,0:T(8,128)(2,1)} collective-permute-done((bf16[2,256,256]{2,1,0:T(8,128)(2,1)}, bf16[2,256,256]{2,1,0:T(8,128)(2,1)}, u32[]{:S(2)}, u32[]{:S(2)}) %collective-permute-start.7) | collective-permute-done | bytes 262176 | tf_op jit(solution)/shard_map/cond/branch_0_fun/ppermute | solution.py:46
  75.4 1.9 collective-permute-start.8
  77.3 1.7 bitcast_dynamic-update-slice_fusion.10
  79.7 6.9 %collective-permute-done.8 = bf16[2,256,256]{2,1,0:T(8,128)(2,1)S(1)} collective-permute-done((bf16[2,256,256]{2,1,0:T(8,128)(2,1)}, bf16[2,256,256]{2,1,0:T(8,128)(2,1)S(1)}, u32[]{:S(2)}, u32[]{:S(2)}) %collective-permute-start.8) | collective-permute-done | bytes 262176 | tf_op jit(solution)/shard_map/cond/branch_0_fun/ppermute | solution.py:46
  87.4 1.7 bitcast_dynamic-update-slice_fusion.4
  89.1 1.7 bitcast_dynamic-update-slice_fusion.2
  102.0 3.1 %constant_dynamic-slice_fusion = bf16[8,2,256,256]{3,2,1,0:T(8,128)(2,1)} fusion(bf16[16,2,256,256]{3,2,1,0:T(8,128)(2,1)} %bitcast_dynamic-update-slice_fusion.1, s32[]{:T(128)S(6)} %select_n.29), kind=kLoop, calls=%fused_computation.16 | loop fusion | bytes 4194308 | tf_op jit(solution)/shard_map/cond/branch_0_fun/dynamic_slice | solution.py:54
  105.1 5.0 %fusion.17 = bf16[384,512]{1,0:T(8,128)(2,1)S(1)} fusion(bf16[8,2,256,256]{3,2,1,0:T(8,128)(2,1)} %get-tuple-element.106, bf16[8,2,256,256]{3,2,1,0:T(8,128)(2,1)} %bitcast.116, bf16[1,384,512]{2,1,0:T(8,128)(2,1)} %param.16, bf16[384,8,2,256]{0,3,1,2:T(8,128)(2,1)} %copy-done), kind=kOutput, calls=%fused_computation.69 | convolution fusion | flops 1619984384 | bytes 8126464 | tf_op jit(solution)/shard_map/dot_general | solution.py:87
  110.1 4.3 %convolution_convert_fusion = bf16[4096,512]{1,0:T(8,128)(2,1)} fusion(bf16[384,4096]{0,1:T(8,128)(2,1)S(1)} %bitcast.115, bf16[384,512]{1,0:T(8,128)(2,1)S(1)} %fusion.17), kind=kOutput, calls=%fused_computation.59 | convolution fusion | flops 1612709888 | bytes 7733248 | tf_op jit(solution)/shard_map/dot_general | solution.py:91
  115.0 56.1 %reduce-scatter.2.cloned.1.call-done = bf16[1,2,256,512]{3,2,1,0:T(8,128)(2,1)} async-done(((bf16[8,2,256,512]{3,2,1,0:T(8,128)(2,1)}), bf16[1,2,256,512]{3,2,1,0:T(8,128)(2,1)}) %reduce-scatter.2.cloned.1.call-update) | async-done | bytes 524304 | tf_op jit(solution)/shard_map/reduce_scatter | solution.py:95
  172.1 28.6 %conditional.5 = (bf16[256,512]{1,0:T(8,128)(2,1)}, f32[256,512]{1,0:T(8,128)S(1)}, f32[256,512]{1,0:T(8,128)S(1)}) conditional(s32[]{:T(128)} %bitcast.33, (bf16[256,512]{1,0:T(8,128)(2,1)S(1)}, s32[]{:T(128)}, bf16[1,2,256,512]{3,2,1,0:T(8,128)(2,1)}) %tuple.51, (bf16[256,512]{1,0:T(8,128)(2,1)S(1)}, s32[]{:T(128)}, ...), branch_computations={%region_5.6_spmd, %region_6.7_spmd, %region_7.8_spmd} | conditional | flops 524292 | bytes 5505218
  173.1 3.4 %collective-permute-start.29 = (bf16[256,512]{1,0:T(8,128)(2,1)S(1)}, bf16[256,512]{1,0:T(8,128)(2,1)S(1)}, u32[]{:S(2)}, u32[]{:S(2)}) collective-permute-start(bf16[256,512]{1,0:T(8,128)(2,1)S(1)} %dynamic-slice_bitcast_fusion), channel_id=1, source_target_pairs={{0,8},{8,0},{1,9},{9,1},{2,10},{10,2},{3,11},{11,3},{4,12},{12,4},... | collective-permute-start | bytes 786440 | tf_op jit(solution)/shard_map/cond/branch_0_fun/ppermute | solution.py:33
  176.5 1.9 collective-permute-start.28
  178.4 4.4 %collective-permute-start.27 = (bf16[256,512]{1,0:T(8,128)(2,1)S(1)}, bf16[256,512]{1,0:T(8,128)(2,1)}, u32[]{:S(2)}, u32[]{:S(2)}) collective-permute-start(bf16[256,512]{1,0:T(8,128)(2,1)S(1)} %get-tuple-element.90), channel_id=1, source_target_pairs={{0,16},{16,32},{32,48},{48,64},{64,80},{80,96},{96,112},{112,128},... | collective-permute-start | bytes 786440 | tf_op jit(solution)/shard_map/cond/branch_0_fun/ppermute | solution.py:16
  183.0 10.5 %collective-permute-done.28 = bf16[256,512]{1,0:T(8,128)(2,1)S(1)} collective-permute-done((bf16[256,512]{1,0:T(8,128)(2,1)S(1)}, bf16[256,512]{1,0:T(8,128)(2,1)S(1)}, u32[]{:S(2)}, u32[]{:S(2)}) %collective-permute-start.28) | collective-permute-done | bytes 262176 | tf_op jit(solution)/shard_map/cond/branch_0_fun/ppermute | solution.py:35
  193.6 6.1 %collective-permute-done.27 = bf16[256,512]{1,0:T(8,128)(2,1)} collective-permute-done((bf16[256,512]{1,0:T(8,128)(2,1)S(1)}, bf16[256,512]{1,0:T(8,128)(2,1)}, u32[]{:S(2)}, u32[]{:S(2)}) %collective-permute-start.27) | collective-permute-done | bytes 262176 | tf_op jit(solution)/shard_map/cond/branch_0_fun/ppermute | solution.py:16
  200.7 2.3 %multiply_bitcast_fusion = f32[1,256,512]{2,1,0:T(8,128)} fusion(f32[256,512]{1,0:T(8,128)} %get-tuple-element.108, f32[256,512]{1,0:T(8,128)S(1)} %get-tuple-element.109, f32[256,512]{1,0:T(8,128)S(1)} %get-tuple-element.115, f32[1,256,512]{2,1,0:T(8,128)} %param.12, bf16[1,2,256,512]{3,2,1,0:T(8,128)(2,1)} %reduce-scatter.2.cloned.1.call-done, s32[]{:T(128)S(6)} %select_n.38), kind=kLoop, calls=%fused_computation.70 | loop fusion | flops 1048576 | bytes 2883588 | tf_op jit(solution)/shard_map/broadcast_in_dim | solution.py:106
  (41 shorter events, 21.7 us)
Async XLA Ops:
  7.2 97.9 %all-gather.3.cloned.1.call-start = ((), (), s32[]{:S(2)}) async-start(), calls=%async_computation.2 | async-start | bytes 2359296 | tf_op jit(solution)/shard_map/all_gather | solution.py:77
  8.9 13.6 %copy-start.7 = (f32[4096]{0:T(1024)S(1)}, f32[4096]{0:T(1024)}, u32[]{:S(2)}) copy-start(f32[4096]{0:T(1024)} %param.17) | copy-start | bytes 49156
  18.4 152.7 %reduce-scatter.2.cloned.1.call-start = ((), (), s32[]{:S(2)}) async-start(), calls=%async_computation.1 | async-start | bytes 4718592 | tf_op jit(solution)/shard_map/reduce_scatter | solution.py:95
  24.2 1.6 copy-start
  25.8 17.8 %collective-permute-start.5 = (bf16[2,256,256]{2,1,0:T(8,128)(2,1)S(1)}, bf16[2,256,256]{2,1,0:T(8,128)(2,1)S(1)}, u32[]{:S(2)}, u32[]{:S(2)}) collective-permute-start(bf16[2,256,256]{2,1,0:T(8,128)(2,1)S(1)} %get-tuple-element.83), channel_id=1, source_target_pairs={{0,1},{1,2},{2,3},{3,4},{4,5},{5,6},{6,7},{7,0},{8,9},{9,10},{10,1... | collective-permute-start | bytes 786440 | tf_op jit(solution)/shard_map/cond/branch_0_fun/ppermute | solution.py:46
  30.1 18.0 %collective-permute-start.2 = (bf16[2,256,256]{2,1,0:T(8,128)(2,1)S(1)}, bf16[2,256,256]{2,1,0:T(8,128)(2,1)}, u32[]{:S(2)}, u32[]{:S(2)}) collective-permute-start(bf16[2,256,256]{2,1,0:T(8,128)(2,1)S(1)} %get-tuple-element.83), channel_id=1, source_target_pairs={{0,7},{1,0},{2,1},{3,2},{4,3},{5,4},{6,5},{7,6},{8,15},{9,8},{10,9... | collective-permute-start | bytes 786440 | tf_op jit(solution)/shard_map/cond/branch_0_fun/ppermute | solution.py:49
  43.6 10.2 %copy-start.1 = (bf16[2,256,256]{2,1,0:T(8,128)(2,1)}, bf16[2,256,256]{2,1,0:T(8,128)(2,1)S(1)}, u32[]{:S(2)}) copy-start(bf16[2,256,256]{2,1,0:T(8,128)(2,1)S(1)} %collective-permute-done.5) | copy-start | bytes 786436 | tf_op jit(solution)/shard_map/cond
  43.6 16.6 %collective-permute-start.6 = (bf16[2,256,256]{2,1,0:T(8,128)(2,1)S(1)}, bf16[2,256,256]{2,1,0:T(8,128)(2,1)}, u32[]{:S(2)}, u32[]{:S(2)}) collective-permute-start(bf16[2,256,256]{2,1,0:T(8,128)(2,1)S(1)} %collective-permute-done.5), channel_id=1, source_target_pairs={{0,1},{1,2},{2,3},{3,4},{4,5},{5,6},{6,7},{7,0},{8,9},{9,10},{10,1... | collective-permute-start | bytes 786440 | tf_op jit(solution)/shard_map/cond/branch_0_fun/ppermute | solution.py:46
  48.1 16.5 %collective-permute-start.3 = (bf16[2,256,256]{2,1,0:T(8,128)(2,1)}, bf16[2,256,256]{2,1,0:T(8,128)(2,1)}, u32[]{:S(2)}, u32[]{:S(2)}) collective-permute-start(bf16[2,256,256]{2,1,0:T(8,128)(2,1)} %collective-permute-done.2), channel_id=1, source_target_pairs={{0,7},{1,0},{2,1},{3,2},{4,3},{5,4},{6,5},{7,6},{8,15},{9,8},{10,9... | collective-permute-start | bytes 786440 | tf_op jit(solution)/shard_map/cond/branch_0_fun/ppermute | solution.py:49
  53.9 51.2 %collective-permute-start = (f32[256,512]{1,0:T(8,128)}, f32[256,512]{1,0:T(8,128)}, u32[]{:S(2)}, u32[]{:S(2)}) collective-permute-start(f32[256,512]{1,0:T(8,128)} %get-tuple-element.81), channel_id=1, source_target_pairs={{0,16},{16,32},{32,48},{48,64},{64,80},{80,96},{96,112},{112,128},... | collective-permute-start | bytes 1572872 | tf_op jit(solution)/shard_map/cond/branch_0_fun/ppermute | solution.py:16
  55.8 49.3 %collective-permute-start.1 = (f32[1]{0:T(128)}, f32[1]{0:T(128)}, u32[]{:S(2)}, u32[]{:S(2)}) collective-permute-start(f32[1]{0:T(128)} %get-tuple-element.82), channel_id=1, source_target_pairs={{0,16},{16,32},{32,48},{48,64},{64,80},{80,96},{96,112},{112,128},... | collective-permute-start | bytes 20 | tf_op jit(solution)/shard_map/cond/branch_0_fun/ppermute | solution.py:16
  60.2 15.2 %collective-permute-start.7 = (bf16[2,256,256]{2,1,0:T(8,128)(2,1)}, bf16[2,256,256]{2,1,0:T(8,128)(2,1)}, u32[]{:S(2)}, u32[]{:S(2)}) collective-permute-start(bf16[2,256,256]{2,1,0:T(8,128)(2,1)} %collective-permute-done.6), channel_id=1, source_target_pairs={{0,1},{1,2},{2,3},{3,4},{4,5},{5,6},{6,7},{7,0},{8,9},{9,10},{10,1... | collective-permute-start | bytes 786440 | tf_op jit(solution)/shard_map/cond/branch_0_fun/ppermute | solution.py:46
  62.9 38.4 %copy-start.2 = (bf16[2,256,256]{2,1,0:T(8,128)(2,1)S(1)}, bf16[2,256,256]{2,1,0:T(8,128)(2,1)}, u32[]{:S(2)}) copy-start(bf16[2,256,256]{2,1,0:T(8,128)(2,1)} %copy-done.1) | copy-start | bytes 786436 | tf_op jit(solution)/shard_map/cond
  64.7 14.3 %collective-permute-start.4 = (bf16[2,256,256]{2,1,0:T(8,128)(2,1)}, bf16[2,256,256]{2,1,0:T(8,128)(2,1)S(1)}, u32[]{:S(2)}, u32[]{:S(2)}) collective-permute-start(bf16[2,256,256]{2,1,0:T(8,128)(2,1)} %collective-permute-done.3), channel_id=1, source_target_pairs={{0,7},{1,0},{2,1},{3,2},{4,3},{5,4},{6,5},{7,6},{8,15},{9,8},{10,9... | collective-permute-start | bytes 786440 | tf_op jit(solution)/shard_map/cond/branch_0_fun/ppermute | solution.py:49
  75.4 11.3 %collective-permute-start.8 = (bf16[2,256,256]{2,1,0:T(8,128)(2,1)}, bf16[2,256,256]{2,1,0:T(8,128)(2,1)S(1)}, u32[]{:S(2)}, u32[]{:S(2)}) collective-permute-start(bf16[2,256,256]{2,1,0:T(8,128)(2,1)} %collective-permute-done.7), channel_id=1, source_target_pairs={{0,1},{1,2},{2,3},{3,4},{4,5},{5,6},{6,7},{7,0},{8,9},{9,10},{10,1... | collective-permute-start | bytes 786440 | tf_op jit(solution)/shard_map/cond/branch_0_fun/ppermute | solution.py:46
  173.1 9.9 %collective-permute-start.29 = (bf16[256,512]{1,0:T(8,128)(2,1)S(1)}, bf16[256,512]{1,0:T(8,128)(2,1)S(1)}, u32[]{:S(2)}, u32[]{:S(2)}) collective-permute-start(bf16[256,512]{1,0:T(8,128)(2,1)S(1)} %dynamic-slice_bitcast_fusion), channel_id=1, source_target_pairs={{0,8},{8,0},{1,9},{9,1},{2,10},{10,2},{3,11},{11,3},{4,12},{12,4},... | collective-permute-start | bytes 786440 | tf_op jit(solution)/shard_map/cond/branch_0_fun/ppermute | solution.py:33
  176.5 17.1 %collective-permute-start.28 = (bf16[256,512]{1,0:T(8,128)(2,1)S(1)}, bf16[256,512]{1,0:T(8,128)(2,1)S(1)}, u32[]{:S(2)}, u32[]{:S(2)}) collective-permute-start(bf16[256,512]{1,0:T(8,128)(2,1)S(1)} %dynamic-slice_bitcast_fusion), channel_id=1, source_target_pairs={{0,24},{8,16},{16,40},{24,32},{32,56},{40,48},{48,72},{56,64},{64,... | collective-permute-start | bytes 786440 | tf_op jit(solution)/shard_map/cond/branch_0_fun/ppermute | solution.py:35
  178.4 21.2 %collective-permute-start.27 = (bf16[256,512]{1,0:T(8,128)(2,1)S(1)}, bf16[256,512]{1,0:T(8,128)(2,1)}, u32[]{:S(2)}, u32[]{:S(2)}) collective-permute-start(bf16[256,512]{1,0:T(8,128)(2,1)S(1)} %get-tuple-element.90), channel_id=1, source_target_pairs={{0,16},{16,32},{32,48},{48,64},{64,80},{80,96},{96,112},{112,128},... | collective-permute-start | bytes 786440 | tf_op jit(solution)/shard_map/cond/branch_0_fun/ppermute | solution.py:16
Sparse Core Ops, SparseCore 0:
  18.5 55.7 all-gather.2
  114.5 56.5 reduce-scatter.1

commit v4 on v3

--- a/solution.py
+++ b/solution.py
@@ -36,7 +36,7 @@
     return from_partner, peer_mine, peer_other
 
 
-def ring_gather(block):
+def ring_blocks(block):
     n = lax.axis_size("fz")
     forward = [(i, (i + 1) % n) for i in range(n)]
     backward = [(i, (i - 1) % n) for i in range(n)]
@@ -48,15 +48,7 @@
     for k in range(1, (n - 1) // 2 + 1):
         behind = lax.ppermute(behind, "fz", backward)
         by_offset[k] = behind
-    stacked = jnp.stack([by_offset[o] for o in range(n)])
-    doubled = jnp.concatenate([stacked, stacked])
-    start = (n - lax.axis_index("fz")) % n
-    return lax.dynamic_slice_in_dim(doubled, start, n, axis=0)
-
-
-def gather_and_send(operand, by):
-    numer, weight, block = operand
-    return passed_along((numer, weight), "replica", by), ring_gather(block)
+    return by_offset
 
 
 def to_peer(sender, operand, power):
@@ -72,28 +64,35 @@
     n_ring = lax.axis_size("fz")
     replica_tokens = activations.shape[1] * n_pair * n_ring
     params = (numer / push_weights[0]).astype(jnp.bfloat16)
-    gathered = lax.all_gather(params, "fl", axis=0)
-    half = gathered.shape[-1] // 2
-    on_sparse = lax.all_gather(gathered[..., :half], "fz", axis=0)
-    (peer_numer, peer_weight), on_ring = to_peer(
-        gather_and_send, (numer, push_weights, gathered[..., half:]), power
-    )
-    full_params = jnp.concatenate([on_sparse, on_ring], axis=-1).reshape(-1, params.shape[1])
+    side = lax.axis_index("fl")
+    spot = lax.axis_index("fz")
+    own_row = lax.all_gather(params, "fz", axis=0, tiled=True)
+    flip = [(i, n_pair - 1 - i) for i in range(n_pair)]
+    partner_rows = ring_blocks(lax.ppermute(params, "fl", flip))
     act32 = activations[0].astype(jnp.float32)
     mean_sq = jnp.mean(act32 * act32, axis=1, keepdims=True)
     normed = (act32 * lax.rsqrt(mean_sq + 1e-05) * gain[None, :]).astype(jnp.bfloat16)
     tokens = normed.shape[0]
     normed = normed.reshape(tokens, n_pair, n_ring, -1).transpose(0, 2, 1, 3).reshape(tokens, -1)
-    keys = jnp.dot(normed, full_params, preferred_element_type=jnp.float32) / math.sqrt(features)
+    by_block = normed.reshape(tokens, n_ring, n_pair, -1)
+    own_cols = lax.dynamic_index_in_dim(by_block, side, 2, keepdims=False).reshape(tokens, -1)
+    keys = jnp.dot(own_cols, own_row, preferred_element_type=jnp.float32)
+    for offset, rows in sorted(partner_rows.items()):
+        cols = lax.dynamic_slice(
+            by_block, (0, (spot + offset) % n_ring, n_pair - 1 - side, 0), (tokens, 1, 1, rows.shape[0])
+        ).reshape(tokens, -1)
+        keys = keys + jnp.dot(cols, rows, preferred_element_type=jnp.float32)
+    keys = keys / math.sqrt(features)
     errors = ((keys - targets[0].astype(jnp.float32)) / math.sqrt(replica_tokens)).astype(
         jnp.bfloat16
     )
     partial_grad = lax.dot_general(
         normed, errors, (((0,), (0,)), ((), ())), preferred_element_type=jnp.float32
     ).astype(jnp.bfloat16)
+    early, weight, partial_grad = lax.optimization_barrier((numer, push_weights, partial_grad))
+    peer_numer, peer_weight = to_peer(send_to_peer, (early, weight), power)
     blocks = partial_grad.reshape(n_ring, n_pair, -1, partial_grad.shape[1])
     halves = lax.psum_scatter(blocks, "fz", scatter_dimension=0)
-    side = lax.axis_index("fl")
     mine = lax.dynamic_index_in_dim(halves, side, 0, keepdims=False)
     other = lax.dynamic_index_in_dim(halves, n_pair - 1 - side, 0, keepdims=False)
     from_partner, peer_mine, peer_other = to_peer(finish_and_send, (mine, other), power)

time: 212 us -> 187 us (0.88)
  local copies, waits for them, and re-layouts: 30.9 us -> 10.4 us
  waiting for transfers between devices: 92.6 us -> 76.7 us
  matrix products: 9.3 us -> 22.2 us
  blocking collectives: 8.71 us -> 0 us
  other arithmetic: 6.11 us -> 9.94 us
  starting transfers between devices: 46 us -> 49.3 us
    cond x19 -> x0, local copies, waits for them, and re-layouts: 19.4 us -> none
    ppermute x3, waiting for transfers between devices: 6.12 us -> 23.7 us  [passed_along(): return lax.ppermute(value, axis, pairs)]
    reduce_scatter x1, waiting for transfers between devices: 56.1 us -> 41.8 us  [body(): halves = lax.psum_scatter(blocks, 'fz', scatter_dimension=0)]
    dot_general x1 -> x8, matrix products: 5 us -> 15.7 us  [the longest x7 13.1 us: body(): keys = keys + jnp.dot(cols, rows, preferred_element_type=jnp.float32)]
    ppermute x7 -> x8, waiting for transfers between devices: 19.7 us -> 10.2 us  [the longest x4 6.95 us: ring_blocks(): ahead = lax.ppermute(ahead, 'fz', forward)]
    ppermute x1, waiting for transfers between devices: 10.5 us -> 1.04 us  [finish_and_send(): peer_other = lax.ppermute(other, ('replica', 'fl'), diagonal)]
    all_gather x1 -> x0, blocking collectives: 8.71 us -> none  [body(): gathered = lax.all_gather(params, 'fl', axis=0)]
    ppermute x7 -> x8, starting transfers between devices: 29.9 us -> 33.5 us  [the longest x3 20 us: ring_blocks(): behind = lax.ppermute(behind, 'fz', backward)]
  transfers between devices with their start and end apart: 14 -> 15, of which waited for: 9 -> 9; matrix products, arithmetic and copies ran while one was open for 14% -> 16% of each run, Pallas kernels for 0% -> 0%
where the time goes in v4:
time: 187 us; the launch traced here: 186 us
  waiting for transfers between devices  76.7 us (41%)
  starting transfers between devices  49.3 us (26%)
  matrix products  22.2 us (12%)
  between operations  17.3 us (9%)
  local copies, waits for them, and re-layouts  10.4 us (6%)
  other arithmetic  9.94 us (5%)
    reduce_scatter x1, waiting for transfers between devices, body(): halves = lax.psum_scatter(blocks, 'fz', scatter_dimension=0)  41.8 us
    ppermute x3, waiting for transfers between devices, passed_along(): return lax.ppermute(value, axis, pairs)  23.7 us
    ppermute x3, starting transfers between devices, ring_blocks(): behind = lax.ppermute(behind, 'fz', backward)  20 us
    dot_general x7, matrix products, body(): keys = keys + jnp.dot(cols, rows, preferred_element_type=jnp.float32)  13.1 us
    ppermute x3, starting transfers between devices, passed_along(): return lax.ppermute(value, axis, pairs)  11 us
    ppermute x4, starting transfers between devices, ring_blocks(): ahead = lax.ppermute(ahead, 'fz', forward)  10 us
    ppermute x4, waiting for transfers between devices, ring_blocks(): ahead = lax.ppermute(ahead, 'fz', forward)  6.95 us
    dot_general x1, matrix products, body(): lax.dot_general(normed, errors, (((0,), (0,)), ((), ())), preferred_eleme...  6.52 us
  transfers between devices with their start and end apart: 15, of which 9 were waited for; matrix products, arithmetic and copies ran while one was open for 16% of the time, Pallas kernels for 0%

profile of v4, /device:TPU:6, one launch (start us, length us, event | category | flops | bytes accessed | tf_op | source)
XLA Modules:
  0.0 186.1 jit_solution(17229811161912891656)
XLA Ops:
  9.7 3.5 %collective-permute-start.15 = (bf16[256,512]{1,0:T(8,128)(2,1)}, bf16[256,512]{1,0:T(8,128)(2,1)S(1)}, u32[]{:S(2)}, u32[]{:S(2)}) collective-permute-start(bf16[256,512]{1,0:T(8,128)(2,1)} %divide_convert_fusion), channel_id=1, source_target_pairs={{0,8},{8,0},{1,9},{9,1},{2,10},{10,2},{3,11},{11,3},{4,12},{12,4},... | collective-permute-start | bytes 786440 | tf_op jit(solution)/shard_map/ppermute | solution.py:71
  13.2 3.4 %copy.16 = bf16[1,384,4096]{1,2,0:T(8,128)(2,1)S(1)} copy(bf16[1,384,4096]{2,1,0:T(8,128)(2,1)} %param.15) | data formatting | bytes 6291456 | tf_op args[3]
  17.4 2.4 %collective-permute-done.15 = bf16[256,512]{1,0:T(8,128)(2,1)S(1)} collective-permute-done((bf16[256,512]{1,0:T(8,128)(2,1)}, bf16[256,512]{1,0:T(8,128)(2,1)S(1)}, u32[]{:S(2)}, u32[]{:S(2)}) %collective-permute-start.15) | collective-permute-done | bytes 262176 | tf_op jit(solution)/shard_map/ppermute | solution.py:71
  19.9 4.3 %collective-permute-start.19 = (bf16[256,512]{1,0:T(8,128)(2,1)S(1)}, bf16[256,512]{1,0:T(8,128)(2,1)}, u32[]{:S(2)}, u32[]{:S(2)}) collective-permute-start(bf16[256,512]{1,0:T(8,128)(2,1)S(1)} %collective-permute-done.15), channel_id=1, source_target_pairs={{0,1},{1,2},{2,3},{3,4},{4,5},{5,6},{6,7},{7,0},{8,9},{9,10},{10,1... | collective-permute-start | bytes 786440 | tf_op jit(solution)/shard_map/ppermute | solution.py:46
  24.1 2.1 %multiply_convert_fusion = bf16[384,2,8,256]{0,3,2,1:T(8,128)(2,1)} fusion(f32[2,8,256]{2,1,0:T(8,128)S(1)} %mul.42, f32[384]{0:T(512)S(1)} %add_rsqrt_fusion, bf16[384,2,8,256]{0,3,2,1:T(8,128)(2,1)S(1)} %bitcast.75), kind=kLoop, calls=%fused_computation.6 | loop fusion | flops 6291456 | bytes 6309376 | tf_op jit(solution)/shard_map/convert_element_type | solution.py:74
  26.2 8.6 %collective-permute-start.16 = (bf16[256,512]{1,0:T(8,128)(2,1)S(1)}, bf16[256,512]{1,0:T(8,128)(2,1)}, u32[]{:S(2)}, u32[]{:S(2)}) collective-permute-start(bf16[256,512]{1,0:T(8,128)(2,1)S(1)} %collective-permute-done.15), channel_id=1, source_target_pairs={{0,7},{1,0},{2,1},{3,2},{4,3},{5,4},{6,5},{7,6},{8,15},{9,8},{10,9... | collective-permute-start | bytes 786440 | tf_op jit(solution)/shard_map/ppermute | solution.py:49
  34.8 5.9 %collective-permute-done.19 = bf16[256,512]{1,0:T(8,128)(2,1)} collective-permute-done((bf16[256,512]{1,0:T(8,128)(2,1)S(1)}, bf16[256,512]{1,0:T(8,128)(2,1)}, u32[]{:S(2)}, u32[]{:S(2)}) %collective-permute-start.19) | collective-permute-done | bytes 262176 | tf_op jit(solution)/shard_map/ppermute | solution.py:46
  40.7 1.9 %collective-permute-start.20 = (bf16[256,512]{1,0:T(8,128)(2,1)}, bf16[256,512]{1,0:T(8,128)(2,1)}, u32[]{:S(2)}, u32[]{:S(2)}) collective-permute-start(bf16[256,512]{1,0:T(8,128)(2,1)} %collective-permute-done.19), channel_id=1, source_target_pairs={{0,1},{1,2},{2,3},{3,4},{4,5},{5,6},{6,7},{7,0},{8,9},{9,10},{10,1... | collective-permute-start | bytes 786440 | tf_op jit(solution)/shard_map/ppermute | solution.py:46
  42.6 2.1 %fusion.60 = bf16[384,8,2,256]{0,3,1,2:T(8,128)(2,1)} fusion(f32[2,8,256]{2,1,0:T(8,128)S(1)} %mul.42, f32[384]{0:T(512)S(1)} %add_rsqrt_fusion, bf16[384,2,8,256]{0,3,2,1:T(8,128)(2,1)S(1)} %bitcast.76), kind=kLoop, calls=%fused_computation.65 | loop fusion | flops 6291456 | bytes 6309376 | tf_op jit(solution)/shard_map/transpose | solution.py:76
  45.0 5.8 %collective-permute-start.17 = (bf16[256,512]{1,0:T(8,128)(2,1)}, bf16[256,512]{1,0:T(8,128)(2,1)}, u32[]{:S(2)}, u32[]{:S(2)}) collective-permute-start(bf16[256,512]{1,0:T(8,128)(2,1)} %collective-permute-done.16), channel_id=1, source_target_pairs={{0,7},{1,0},{2,1},{3,2},{4,3},{5,4},{6,5},{7,6},{8,15},{9,8},{10,9... | collective-permute-start | bytes 786440 | tf_op jit(solution)/shard_map/ppermute | solution.py:49
  50.8 2.7 %constant_dynamic-slice_fusion = bf16[384,1,8,256]{0,3,2,1:T(8,128)(2,1)} fusion(bf16[384,2,8,256]{0,3,2,1:T(8,128)(2,1)} %multiply_convert_fusion, s32[]{:T(128)S(6)} %select_n.76), kind=kLoop, calls=%fused_computation.60 | loop fusion | bytes 3145732 | tf_op jit(solution)/shard_map/dynamic-slice
  53.5 2.0 %copy.17 = bf16[384,8,2,256]{0,3,2,1:T(8,128)(2,1)} copy(bf16[384,8,2,256]{0,3,1,2:T(8,128)(2,1)S(1)} %copy-done) | data formatting | bytes 6291456 | tf_op jit(solution)/shard_map/transpose | solution.py:76
  56.6 1.9 %collective-permute-start.21 = (bf16[256,512]{1,0:T(8,128)(2,1)}, bf16[256,512]{1,0:T(8,128)(2,1)}, u32[]{:S(2)}, u32[]{:S(2)}) collective-permute-start(bf16[256,512]{1,0:T(8,128)(2,1)} %collective-permute-done.20), channel_id=1, source_target_pairs={{0,1},{1,2},{2,3},{3,4},{4,5},{5,6},{6,7},{7,0},{8,9},{9,10},{10,1... | collective-permute-start | bytes 786440 | tf_op jit(solution)/shard_map/ppermute | solution.py:46
  58.5 2.2 %fusion.16 = f32[384,512]{1,0:T(8,128)} fusion(bf16[256,512]{1,0:T(8,128)(2,1)} %collective-permute-done.19, bf16[384,2,8,256]{0,3,2,1:T(8,128)(2,1)} %multiply_convert_fusion, s32[]{:T(128)} %select_n.77, s32[]{:T(128)S(6)} %select_n.93), kind=kOutput, calls=%fused_computation.33 | convolution fusion | flops 100663296 | bytes 1245700 | tf_op jit(solution)/shard_map/dot_general | solution.py:84
  61.3 5.6 %collective-permute-start.18 = (bf16[256,512]{1,0:T(8,128)(2,1)}, bf16[256,512]{1,0:T(8,128)(2,1)}, u32[]{:S(2)}, u32[]{:S(2)}) collective-permute-start(bf16[256,512]{1,0:T(8,128)(2,1)} %collective-permute-done.17), channel_id=1, source_target_pairs={{0,7},{1,0},{2,1},{3,2},{4,3},{5,4},{6,5},{7,6},{8,15},{9,8},{10,9... | collective-permute-start | bytes 786440 | tf_op jit(solution)/shard_map/ppermute | solution.py:49
  66.9 2.3 %fusion.18 = f32[384,512]{1,0:T(8,128)} fusion(bf16[256,512]{1,0:T(8,128)(2,1)} %collective-permute-done.20, bf16[384,2,8,256]{0,3,2,1:T(8,128)(2,1)} %multiply_convert_fusion, s32[]{:T(128)} %select_n.77, s32[]{:T(128)S(6)} %select_n.91), kind=kOutput, calls=%fused_computation.35 | convolution fusion | flops 100663296 | bytes 1245700 | tf_op jit(solution)/shard_map/dot_general | solution.py:84
  69.1 1.9 %collective-permute-start.22 = (bf16[256,512]{1,0:T(8,128)(2,1)}, bf16[256,512]{1,0:T(8,128)(2,1)}, u32[]{:S(2)}, u32[]{:S(2)}) collective-permute-start(bf16[256,512]{1,0:T(8,128)(2,1)} %collective-permute-done.21), channel_id=1, source_target_pairs={{0,1},{1,2},{2,3},{3,4},{4,5},{5,6},{6,7},{7,0},{8,9},{9,10},{10,1... | collective-permute-start | bytes 786440 | tf_op jit(solution)/shard_map/ppermute | solution.py:46
  71.0 2.3 %fusion.20 = f32[384,512]{1,0:T(8,128)} fusion(bf16[256,512]{1,0:T(8,128)(2,1)} %collective-permute-done.21, bf16[384,2,8,256]{0,3,2,1:T(8,128)(2,1)} %multiply_convert_fusion, s32[]{:T(128)} %select_n.77, s32[]{:T(128)S(6)} %select_n.89), kind=kOutput, calls=%fused_computation.37 | convolution fusion | flops 100663296 | bytes 1245700 | tf_op jit(solution)/shard_map/dot_general | solution.py:84
  73.3 2.6 %fusion.48 = f32[384,512]{1,0:T(8,128)S(1)} fusion(bf16[384,2048]{0,1:T(8,128)(2,1)S(1)} %bitcast.82, bf16[2048,512]{1,0:T(8,128)(2,1)} %all-gather.2.cloned.1.call-done), kind=kOutput, calls=%fused_computation.64 | convolution fusion | flops 805306368 | bytes 4456448 | tf_op jit(solution)/shard_map/dot_general | solution.py:79
  80.0 2.3 %convolution_add_fusion.1 = f32[384,512]{1,0:T(8,128)} fusion(f32[384,512]{1,0:T(8,128)S(1)} %convolution_add_fusion.2, bf16[256,512]{1,0:T(8,128)(2,1)} %collective-permute-done.18, bf16[384,2,8,256]{0,3,2,1:T(8,128)(2,1)} %multiply_convert_fusion, s32[]{:T(128)} %select_n.77, s32[]{:T(128)S(6)} %select_n.85), kind=kOutput, calls=%fused_computation.16 | convolution fusion | flops 100859904 | bytes 2032132 | tf_op jit(solution)/shard_map/dot_general | solution.py:84
  82.3 6.5 %convolution_convert_fusion = bf16[4096,512]{1,0:T(8,128)(2,1)} fusion(bf16[384,4096]{0,1:T(8,128)(2,1)S(1)} %bitcast.78, f32[384,512]{1,0:T(8,128)} %fusion.16, f32[384,512]{1,0:T(8,128)} %fusion.18, f32[384,512]{1,0:T(8,128)} %fusion.20, f32[384,512]{1,0:T(8,128)} %convolution_add_fusion.1, bf16[256,512]{1,0:T(8,128)(2,1)} %collective-permute-done.22, ...), kind=kOutput, calls=%fused_computation.8 | convolution fusion | flops 1715142656 | bytes 11338244 | tf_op jit(solution)/shard_map/dot_general | solution.py:89
  89.9 16.2 %conditional.5 = (f32[256,512]{1,0:T(8,128)}, f32[1]{0:T(128)}) conditional(s32[]{:T(128)} %bitcast.20, (f32[256,512]{1,0:T(8,128)S(1)}, f32[1]{0:T(128)}) %tuple.74, (f32[256,512]{1,0:T(8,128)S(1)}, f32[1]{0:T(128)}) %tuple.75, (f32[256,512]{1,0:T(8,128)S(1)}, f32[1]{0:T(128)}) %tuple.76), branch_computations={%region_5.6_spmd, %region_6.7_spmd, %region_7.8_spmd} | conditional | bytes 2097264 | solution.py:56
  89.9 1.9 %collective-permute-start = (f32[256,512]{1,0:T(8,128)S(1)}, f32[256,512]{1,0:T(8,128)}, u32[]{:S(2)}, u32[]{:S(2)}) collective-permute-start(f32[256,512]{1,0:T(8,128)S(1)} %get-tuple-element.61), channel_id=1, source_target_pairs={{0,16},{16,32},{32,48},{48,64},{64,80},{80,96},{96,112},{112,128},... | collective-permute-start | bytes 1572872 | tf_op jit(solution)/shard_map/cond/branch_0_fun/ppermute | solution.py:16
  91.8 4.6 %collective-permute-start.1 = (f32[1]{0:T(128)}, f32[1]{0:T(128)}, u32[]{:S(2)}, u32[]{:S(2)}) collective-permute-start(f32[1]{0:T(128)} %get-tuple-element.62), channel_id=1, source_target_pairs={{0,16},{16,32},{32,48},{48,64},{64,80},{80,96},{96,112},{112,128},... | collective-permute-start | bytes 20 | tf_op jit(solution)/shard_map/cond/branch_0_fun/ppermute | solution.py:16
  96.5 9.6 %collective-permute-done.1 = f32[1]{0:T(128)} collective-permute-done((f32[1]{0:T(128)}, f32[1]{0:T(128)}, u32[]{:S(2)}, u32[]{:S(2)}) %collective-permute-start.1) | collective-permute-done | bytes 36 | tf_op jit(solution)/shard_map/cond/branch_0_fun/ppermute | solution.py:16
  106.7 41.8 %reduce-scatter.2.cloned.1.call-done = bf16[1,2,256,512]{3,2,1,0:T(8,128)(2,1)} async-done(((bf16[8,2,256,512]{3,2,1,0:T(8,128)(2,1)}), bf16[1,2,256,512]{3,2,1,0:T(8,128)(2,1)}) %reduce-scatter.2.cloned.1.call-update) | async-done | bytes 524304 | tf_op jit(solution)/shard_map/reduce_scatter | solution.py:95
  149.4 26.4 %conditional.6 = (bf16[256,512]{1,0:T(8,128)(2,1)}, f32[256,512]{1,0:T(8,128)S(1)}, bf16[256,512]{1,0:T(8,128)(2,1)}) conditional(s32[]{:T(128)} %bitcast.20, (bf16[256,512]{1,0:T(8,128)(2,1)S(1)}, bf16[1,2,256,512]{3,2,1,0:T(8,128)(2,1)}, s32[]{:T(128)}) %tuple.54, (bf16[256,512]{1,0:T(8,128)(2,1)S(1)}, ...), branch_computations={%region_2.3_spmd, %region_3.4_spmd, %region_4.5_spmd} | conditional | flops 393216 | bytes 4718740
  150.4 2.8 %collective-permute-start.7 = (bf16[256,512]{1,0:T(8,128)(2,1)S(1)}, bf16[256,512]{1,0:T(8,128)(2,1)S(1)}, u32[]{:S(2)}, u32[]{:S(2)}) collective-permute-start(bf16[256,512]{1,0:T(8,128)(2,1)S(1)} %dynamic-slice_bitcast_fusion), channel_id=1, source_target_pairs={{0,24},{8,16},{16,40},{24,32},{32,56},{40,48},{48,72},{56,64},{64,... | collective-permute-start | bytes 786440 | tf_op jit(solution)/shard_map/cond/branch_0_fun/ppermute | solution.py:35
  153.2 4.5 %collective-permute-start.6 = (bf16[256,512]{1,0:T(8,128)(2,1)S(1)}, bf16[256,512]{1,0:T(8,128)(2,1)}, u32[]{:S(2)}, u32[]{:S(2)}) collective-permute-start(bf16[256,512]{1,0:T(8,128)(2,1)S(1)} %get-tuple-element.52), channel_id=1, source_target_pairs={{0,16},{16,32},{32,48},{48,64},{64,80},{80,96},{96,112},{112,128},... | collective-permute-start | bytes 786440 | tf_op jit(solution)/shard_map/cond/branch_0_fun/ppermute | solution.py:16
  157.7 1.9 %collective-permute-start.8 = (bf16[256,512]{1,0:T(8,128)(2,1)S(1)}, bf16[256,512]{1,0:T(8,128)(2,1)}, u32[]{:S(2)}, u32[]{:S(2)}) collective-permute-start(bf16[256,512]{1,0:T(8,128)(2,1)S(1)} %dynamic-slice_bitcast_fusion), channel_id=1, source_target_pairs={{0,8},{8,0},{1,9},{9,1},{2,10},{10,2},{3,11},{11,3},{4,12},{12,4},... | collective-permute-start | bytes 786440 | tf_op jit(solution)/shard_map/cond/branch_0_fun/ppermute | solution.py:33
  160.7 14.1 %collective-permute-done.6 = bf16[256,512]{1,0:T(8,128)(2,1)} collective-permute-done((bf16[256,512]{1,0:T(8,128)(2,1)S(1)}, bf16[256,512]{1,0:T(8,128)(2,1)}, u32[]{:S(2)}, u32[]{:S(2)}) %collective-permute-start.6) | collective-permute-done | bytes 262176 | tf_op jit(solution)/shard_map/cond/branch_0_fun/ppermute | solution.py:16
  175.9 2.2 %fusion.12 = f32[1,256,512]{2,1,0:T(8,128)} fusion(bf16[256,512]{1,0:T(8,128)(2,1)} %get-tuple-element.87, f32[256,512]{1,0:T(8,128)} %get-tuple-element.80, f32[256,512]{1,0:T(8,128)S(1)} %get-tuple-element.81, f32[1,256,512]{2,1,0:T(8,128)S(1)} %copy-done.2, bf16[1,2,256,512]{3,2,1,0:T(8,128)(2,1)} %reduce-scatter.2.cloned.1.call-done, s32[]{:T(128)S(6)} %select_n.76), kind=kLoop, calls=%fused_computation.27 | loop fusion | flops 1179648 | bytes 2621444 | tf_op jit(solution)/shard_map/broadcast_in_dim | solution.py:105
  (36 shorter events, 12.9 us)
Async XLA Ops:
  7.2 66.2 %all-gather.2.cloned.1.call-start = ((), (), s32[]{:S(2)}) async-start(), calls=%async_computation.1 | async-start | bytes 2359296 | tf_op jit(solution)/shard_map/all_gather | solution.py:69
  9.7 138.8 %reduce-scatter.2.cloned.1.call-start = ((), (), s32[]{:S(2)}) async-start(), calls=%async_computation.2 | async-start | bytes 4718592 | tf_op jit(solution)/shard_map/reduce_scatter | solution.py:95
  9.7 10.1 %collective-permute-start.15 = (bf16[256,512]{1,0:T(8,128)(2,1)}, bf16[256,512]{1,0:T(8,128)(2,1)S(1)}, u32[]{:S(2)}, u32[]{:S(2)}) collective-permute-start(bf16[256,512]{1,0:T(8,128)(2,1)} %divide_convert_fusion), channel_id=1, source_target_pairs={{0,8},{8,0},{1,9},{9,1},{2,10},{10,2},{3,11},{11,3},{4,12},{12,4},... | collective-permute-start | bytes 786440 | tf_op jit(solution)/shard_map/ppermute | solution.py:71
  16.6 0.8 copy-start.5
  19.9 20.9 %collective-permute-start.19 = (bf16[256,512]{1,0:T(8,128)(2,1)S(1)}, bf16[256,512]{1,0:T(8,128)(2,1)}, u32[]{:S(2)}, u32[]{:S(2)}) collective-permute-start(bf16[256,512]{1,0:T(8,128)(2,1)S(1)} %collective-permute-done.15), channel_id=1, source_target_pairs={{0,1},{1,2},{2,3},{3,4},{4,5},{5,6},{6,7},{7,0},{8,9},{9,10},{10,1... | collective-permute-start | bytes 786440 | tf_op jit(solution)/shard_map/ppermute | solution.py:46
  26.2 18.7 %collective-permute-start.16 = (bf16[256,512]{1,0:T(8,128)(2,1)S(1)}, bf16[256,512]{1,0:T(8,128)(2,1)}, u32[]{:S(2)}, u32[]{:S(2)}) collective-permute-start(bf16[256,512]{1,0:T(8,128)(2,1)S(1)} %collective-permute-done.15), channel_id=1, source_target_pairs={{0,7},{1,0},{2,1},{3,2},{4,3},{5,4},{6,5},{7,6},{8,15},{9,8},{10,9... | collective-permute-start | bytes 786440 | tf_op jit(solution)/shard_map/ppermute | solution.py:49
  40.7 15.9 %collective-permute-start.20 = (bf16[256,512]{1,0:T(8,128)(2,1)}, bf16[256,512]{1,0:T(8,128)(2,1)}, u32[]{:S(2)}, u32[]{:S(2)}) collective-permute-start(bf16[256,512]{1,0:T(8,128)(2,1)} %collective-permute-done.19), channel_id=1, source_target_pairs={{0,1},{1,2},{2,3},{3,4},{4,5},{5,6},{6,7},{7,0},{8,9},{9,10},{10,1... | collective-permute-start | bytes 786440 | tf_op jit(solution)/shard_map/ppermute | solution.py:46
  44.7 8.8 %copy-start = (bf16[384,8,2,256]{0,3,1,2:T(8,128)(2,1)S(1)}, bf16[384,8,2,256]{0,3,1,2:T(8,128)(2,1)}, u32[]{:S(2)}) copy-start(bf16[384,8,2,256]{0,3,1,2:T(8,128)(2,1)} %fusion.60) | copy-start | bytes 9437188
  45.0 16.3 %collective-permute-start.17 = (bf16[256,512]{1,0:T(8,128)(2,1)}, bf16[256,512]{1,0:T(8,128)(2,1)}, u32[]{:S(2)}, u32[]{:S(2)}) collective-permute-start(bf16[256,512]{1,0:T(8,128)(2,1)} %collective-permute-done.16), channel_id=1, source_target_pairs={{0,7},{1,0},{2,1},{3,2},{4,3},{5,4},{6,5},{7,6},{8,15},{9,8},{10,9... | collective-permute-start | bytes 786440 | tf_op jit(solution)/shard_map/ppermute | solution.py:49
  55.5 17.8 %copy-start.3 = (bf16[384,1,8,256]{0,3,2,1:T(8,128)(2,1)S(1)}, bf16[384,1,8,256]{0,3,2,1:T(8,128)(2,1)}, u32[]{:S(2)}) copy-start(bf16[384,1,8,256]{0,3,2,1:T(8,128)(2,1)} %constant_dynamic-slice_fusion) | copy-start | bytes 4718596
  56.6 12.5 %collective-permute-start.21 = (bf16[256,512]{1,0:T(8,128)(2,1)}, bf16[256,512]{1,0:T(8,128)(2,1)}, u32[]{:S(2)}, u32[]{:S(2)}) collective-permute-start(bf16[256,512]{1,0:T(8,128)(2,1)} %collective-permute-done.20), channel_id=1, source_target_pairs={{0,1},{1,2},{2,3},{3,4},{4,5},{5,6},{6,7},{7,0},{8,9},{9,10},{10,1... | collective-permute-start | bytes 786440 | tf_op jit(solution)/shard_map/ppermute | solution.py:46
  61.3 18.7 %collective-permute-start.18 = (bf16[256,512]{1,0:T(8,128)(2,1)}, bf16[256,512]{1,0:T(8,128)(2,1)}, u32[]{:S(2)}, u32[]{:S(2)}) collective-permute-start(bf16[256,512]{1,0:T(8,128)(2,1)} %collective-permute-done.17), channel_id=1, source_target_pairs={{0,7},{1,0},{2,1},{3,2},{4,3},{5,4},{6,5},{7,6},{8,15},{9,8},{10,9... | collective-permute-start | bytes 786440 | tf_op jit(solution)/shard_map/ppermute | solution.py:49
  69.1 13.2 %collective-permute-start.22 = (bf16[256,512]{1,0:T(8,128)(2,1)}, bf16[256,512]{1,0:T(8,128)(2,1)}, u32[]{:S(2)}, u32[]{:S(2)}) collective-permute-start(bf16[256,512]{1,0:T(8,128)(2,1)} %collective-permute-done.21), channel_id=1, source_target_pairs={{0,1},{1,2},{2,3},{3,4},{4,5},{5,6},{6,7},{7,0},{8,9},{9,10},{10,1... | collective-permute-start | bytes 786440 | tf_op jit(solution)/shard_map/ppermute | solution.py:46
  77.1 5.2 %copy-start.1 = (bf16[384,8,2,256]{0,3,2,1:T(8,128)(2,1)S(1)}, bf16[384,8,2,256]{0,3,2,1:T(8,128)(2,1)}, u32[]{:S(2)}) copy-start(bf16[384,8,2,256]{0,3,2,1:T(8,128)(2,1)} %copy.17) | copy-start | bytes 9437188
  77.1 5.2 %copy-start.4 = (bf16[1,384,512]{2,1,0:T(8,128)(2,1)S(1)}, bf16[1,384,512]{2,1,0:T(8,128)(2,1)}, u32[]{:S(2)}) copy-start(bf16[1,384,512]{2,1,0:T(8,128)(2,1)} %param.16) | copy-start | bytes 1179652
  88.9 1.1 copy-start.2
  89.9 16.2 %collective-permute-start = (f32[256,512]{1,0:T(8,128)S(1)}, f32[256,512]{1,0:T(8,128)}, u32[]{:S(2)}, u32[]{:S(2)}) collective-permute-start(f32[256,512]{1,0:T(8,128)S(1)} %get-tuple-element.61), channel_id=1, source_target_pairs={{0,16},{16,32},{32,48},{48,64},{64,80},{80,96},{96,112},{112,128},... | collective-permute-start | bytes 1572872 | tf_op jit(solution)/shard_map/cond/branch_0_fun/ppermute | solution.py:16
  91.8 14.2 %collective-permute-start.1 = (f32[1]{0:T(128)}, f32[1]{0:T(128)}, u32[]{:S(2)}, u32[]{:S(2)}) collective-permute-start(f32[1]{0:T(128)} %get-tuple-element.62), channel_id=1, source_target_pairs={{0,16},{16,32},{32,48},{48,64},{64,80},{80,96},{96,112},{112,128},... | collective-permute-start | bytes 20 | tf_op jit(solution)/shard_map/cond/branch_0_fun/ppermute | solution.py:16
  150.4 10.3 %collective-permute-start.7 = (bf16[256,512]{1,0:T(8,128)(2,1)S(1)}, bf16[256,512]{1,0:T(8,128)(2,1)S(1)}, u32[]{:S(2)}, u32[]{:S(2)}) collective-permute-start(bf16[256,512]{1,0:T(8,128)(2,1)S(1)} %dynamic-slice_bitcast_fusion), channel_id=1, source_target_pairs={{0,24},{8,16},{16,40},{24,32},{32,56},{40,48},{48,72},{56,64},{64,... | collective-permute-start | bytes 786440 | tf_op jit(solution)/shard_map/cond/branch_0_fun/ppermute | solution.py:35
  153.2 21.6 %collective-permute-start.6 = (bf16[256,512]{1,0:T(8,128)(2,1)S(1)}, bf16[256,512]{1,0:T(8,128)(2,1)}, u32[]{:S(2)}, u32[]{:S(2)}) collective-permute-start(bf16[256,512]{1,0:T(8,128)(2,1)S(1)} %get-tuple-element.52), channel_id=1, source_target_pairs={{0,16},{16,32},{32,48},{48,64},{64,80},{80,96},{96,112},{112,128},... | collective-permute-start | bytes 786440 | tf_op jit(solution)/shard_map/cond/branch_0_fun/ppermute | solution.py:16
  157.7 18.1 %collective-permute-start.8 = (bf16[256,512]{1,0:T(8,128)(2,1)S(1)}, bf16[256,512]{1,0:T(8,128)(2,1)}, u32[]{:S(2)}, u32[]{:S(2)}) collective-permute-start(bf16[256,512]{1,0:T(8,128)(2,1)S(1)} %dynamic-slice_bitcast_fusion), channel_id=1, source_target_pairs={{0,8},{8,0},{1,9},{9,1},{2,10},{10,2},{3,11},{11,3},{4,12},{12,4},... | collective-permute-start | bytes 786440 | tf_op jit(solution)/shard_map/cond/branch_0_fun/ppermute | solution.py:33
Sparse Core Ops, SparseCore 0:
  10.6 54.8 all-gather.1
  89.0 59.4 reduce-scatter.1

commit v5 on v1

--- a/solution.py
+++ b/solution.py
@@ -51,11 +51,16 @@
         normed, errors, (((0,), (0,)), ((), ())), preferred_element_type=jnp.float32
     ).astype(jnp.bfloat16)
     blocks = partial_grad.reshape(n_ring, n_pair, -1, partial_grad.shape[1])
-    grad16 = lax.psum_scatter(blocks, "fz", scatter_dimension=0)
-    grad16 = lax.psum_scatter(grad16, "fl", scatter_dimension=0)
-    peer_grad16 = to_peer(send_to_peer, grad16, power)
-    updated = numer - 0.3 * grad16.astype(jnp.float32)
-    peer_updated = peer_numer - 0.3 * peer_grad16.astype(jnp.float32)
+    halves = lax.psum_scatter(blocks, "fz", scatter_dimension=0)
+    side = lax.axis_index("fl")
+    mine = lax.dynamic_index_in_dim(halves, side, 0, keepdims=False)
+    other = lax.dynamic_index_in_dim(halves, n_pair - 1 - side, 0, keepdims=False)
+    flip = [(i, n_pair - 1 - i) for i in range(n_pair)]
+    from_partner = lax.ppermute(other, "fl", flip)
+    grad = mine.astype(jnp.float32) + from_partner.astype(jnp.float32)
+    peer_grad = to_peer(send_to_peer, grad.astype(jnp.bfloat16), power).astype(jnp.float32)
+    updated = numer - 0.3 * grad
+    peer_updated = peer_numer - 0.3 * peer_grad
     mixed_numerators = 0.5 * (updated + peer_updated)
     mixed_weights = 0.5 * (push_weights + peer_weight)
     return (mixed_numerators[None], mixed_weights)

time: 194 us -> 188 us (0.969)
  the two profiles are of different devices: /device:TPU:6 before, /device:TPU:8 now
where the time goes in v5:
time: 188 us
  waiting for transfers between devices  124 us (66%)
  between operations  17.2 us (9%)
  starting transfers between devices  14.1 us (8%)
  blocking collectives  10.9 us (6%)
  matrix products  9.28 us (5%)
  local copies, waits for them, and re-layouts  7.11 us (4%)
  other arithmetic  5.91 us (3%)
    reduce_scatter x1, waiting for transfers between devices, body(): halves = lax.psum_scatter(blocks, 'fz', scatter_dimension=0)  57 us
    ppermute x3, waiting for transfers between devices, passed_along(): return lax.ppermute(value, axis, pairs)  35.2 us
    all_gather x1, waiting for transfers between devices, body(): gathered = lax.all_gather(gathered, 'fz', axis=0)  24.5 us
    ppermute x3, starting transfers between devices, passed_along(): return lax.ppermute(value, axis, pairs)  11.5 us
    all_gather x1, blocking collectives, body(): gathered = lax.all_gather(params, 'fl', axis=0)  10.9 us
    ppermute x1, waiting for transfers between devices, body(): from_partner = lax.ppermute(other, 'fl', flip)  6.79 us
    unnamed x11, local copies, waits for them, and re-layouts  5.76 us
    dot_general x1, matrix products, body(): jnp.dot(normed, full_params, preferred_element_type=jnp.float32)  4.98 us
  transfers between devices with their start and end apart: 6, of which 5 were waited for; matrix products, arithmetic and copies ran while one was open for 3% of the time, Pallas kernels for 0%

profile of v5, /device:TPU:8, one launch (start us, length us, event | category | flops | bytes accessed | tf_op | source)
XLA Modules:
  0.0 188.0 jit_solution(2339841532000355196)
XLA Ops:
  7.2 0.0 all-gather.3.cloned.1.call-start
  7.9 0.0 copy-start.3
  7.9 1.1 divide_convert_fusion
  9.0 10.9 %all_gather.10 = bf16[2,256,512]{2,1,0:T(8,128)(2,1)} all-gather(bf16[1,256,512]{2,1,0:T(8,128)(2,1)S(1)} %divide_convert_fusion), channel_id=1, replica_groups=mesh['replica'=32,'fl'=2,'fz'=8] {'fl'}, dimensions={0}, use_global_device_ids=true | all-gather | bytes 786432 | tf_op jit(solution)/shard_map/all_gather | solution.py:36
  19.9 0.0 all-gather.3.cloned.1.call-update
  19.9 0.0 reduce-scatter.2.cloned.1.call-start
  19.9 3.4 %copy.14 = bf16[1,384,4096]{1,2,0:T(8,128)(2,1)S(1)} copy(bf16[1,384,4096]{2,1,0:T(8,128)(2,1)} %param.15) | data formatting | bytes 6291456 | tf_op args[3]
  23.4 0.0 copy-done.3
  24.0 0.8 multiply_reduce_fusion
  24.8 0.9 fusion
  25.7 0.0 copy-start
  25.7 1.7 copy-done
  27.4 0.4 copy.15
  27.8 0.7 copy-done.1
  28.4 27.8 %conditional.5 = (f32[256,512]{1,0:T(8,128)}, f32[1]{0:T(128)}) conditional(s32[]{:T(128)} %bitcast.4, (f32[256,512]{1,0:T(8,128)S(1)}, f32[1]{0:T(128)}) %tuple.57, (f32[256,512]{1,0:T(8,128)S(1)}, f32[1]{0:T(128)}) %tuple.58, (f32[256,512]{1,0:T(8,128)S(1)}, f32[1]{0:T(128)}) %tuple.59), branch_computations={%region_1.0_spmd, %region_2.0_spmd, %region_3.0_spmd} | conditional | bytes 2097264 | solution.py:25
  28.4 2.4 %collective-permute-start.2 = (f32[256,512]{1,0:T(8,128)S(1)}, f32[256,512]{1,0:T(8,128)}, u32[]{:S(2)}, u32[]{:S(2)}) collective-permute-start(f32[256,512]{1,0:T(8,128)S(1)} %get-tuple-element.27), channel_id=1, source_target_pairs={{0,32},{16,48},{32,64},{48,80},{64,96},{80,112},{96,128},{112,144}... | collective-permute-start | bytes 1572872 | tf_op jit(solution)/shard_map/cond/branch_1_fun/ppermute | solution.py:16
  30.8 4.8 %collective-permute-start.3 = (f32[1]{0:T(128)}, f32[1]{0:T(128)}, u32[]{:S(2)}, u32[]{:S(2)}) collective-permute-start(f32[1]{0:T(128)} %get-tuple-element.28), channel_id=1, source_target_pairs={{0,32},{16,48},{32,64},{48,80},{64,96},{80,112},{96,128},{112,144}... | collective-permute-start | bytes 20 | tf_op jit(solution)/shard_map/cond/branch_1_fun/ppermute | solution.py:16
  35.6 20.5 %collective-permute-done.3 = f32[1]{0:T(128)} collective-permute-done((f32[1]{0:T(128)}, f32[1]{0:T(128)}, u32[]{:S(2)}, u32[]{:S(2)}) %collective-permute-start.3) | collective-permute-done | bytes 36 | tf_op jit(solution)/shard_map/cond/branch_1_fun/ppermute | solution.py:16
  56.2 0.0 collective-permute-done.2
  56.2 24.5 %all-gather.3.cloned.1.call-done = bf16[16,256,512]{2,1,0:T(8,128)(2,1)} async-done(((bf16[2,256,512]{2,1,0:T(8,128)(2,1)}), bf16[16,256,512]{2,1,0:T(8,128)(2,1)}) %all-gather.3.cloned.1.call-update) | async-done | bytes 4194320 | tf_op jit(solution)/shard_map/all_gather | solution.py:37
  80.7 5.0 %fusion.4 = bf16[384,512]{1,0:T(8,128)(2,1)S(1)} fusion(bf16[8,2,256,512]{3,2,1,0:T(8,128)(2,1)} %bitcast.44, bf16[1,384,512]{2,1,0:T(8,128)(2,1)S(1)} %copy-done.4, bf16[384,8,2,256]{0,3,1,2:T(8,128)(2,1)} %copy-done), kind=kOutput, calls=%fused_computation.8 | convolution fusion | flops 1611595776 | bytes 8126464 | tf_op jit(solution)/shard_map/dot_general | solution.py:45
  85.7 4.3 %convolution_convert_fusion = bf16[4096,512]{1,0:T(8,128)(2,1)} fusion(bf16[384,4096]{0,1:T(8,128)(2,1)S(1)} %bitcast.40, bf16[384,512]{1,0:T(8,128)(2,1)S(1)} %fusion.4), kind=kOutput, calls=%fused_computation.2 | convolution fusion | flops 1612709888 | bytes 7733248 | tf_op jit(solution)/shard_map/dot_general | solution.py:50
  90.0 0.0 reduce-scatter.2.cloned.1.call-update
  90.0 57.0 %reduce-scatter.2.cloned.1.call-done = bf16[1,2,256,512]{3,2,1,0:T(8,128)(2,1)} async-done(((bf16[8,2,256,512]{3,2,1,0:T(8,128)(2,1)}), bf16[1,2,256,512]{3,2,1,0:T(8,128)(2,1)}) %reduce-scatter.2.cloned.1.call-update) | async-done | bytes 524304 | tf_op jit(solution)/shard_map/reduce_scatter | solution.py:54
  147.0 1.0 dynamic-slice_bitcast_fusion
  148.0 2.4 %collective-permute-start.9 = (bf16[256,512]{1,0:T(8,128)(2,1)S(1)}, bf16[256,512]{1,0:T(8,128)(2,1)S(1)}, u32[]{:S(2)}, u32[]{:S(2)}) collective-permute-start(bf16[256,512]{1,0:T(8,128)(2,1)S(1)} %dynamic-slice_bitcast_fusion), channel_id=1, source_target_pairs={{0,8},{8,0},{1,9},{9,1},{2,10},{10,2},{3,11},{11,3},{4,12},{12,4},... | collective-permute-start | bytes 786440 | tf_op jit(solution)/shard_map/ppermute | solution.py:59
  151.0 6.8 %collective-permute-done.9 = bf16[256,512]{1,0:T(8,128)(2,1)S(1)} collective-permute-done((bf16[256,512]{1,0:T(8,128)(2,1)S(1)}, bf16[256,512]{1,0:T(8,128)(2,1)S(1)}, u32[]{:S(2)}, u32[]{:S(2)}) %collective-permute-start.9) | collective-permute-done | bytes 262176 | tf_op jit(solution)/shard_map/ppermute | solution.py:59
  157.8 1.0 fusion.5
  158.9 19.0 %conditional.6 = (bf16[256,512]{1,0:T(8,128)(2,1)}) conditional(s32[]{:T(128)} %bitcast.4, bf16[256,512]{1,0:T(8,128)(2,1)S(1)} %fusion.5, bf16[256,512]{1,0:T(8,128)(2,1)S(1)} %fusion.5, bf16[256,512]{1,0:T(8,128)(2,1)S(1)} %fusion.5), branch_computations={%region_5.6_spmd, %region_6.7_spmd, %region_7.8_spmd} | conditional | bytes 1048624
  158.9 4.3 %collective-permute-start.7 = (bf16[256,512]{1,0:T(8,128)(2,1)S(1)}, bf16[256,512]{1,0:T(8,128)(2,1)}, u32[]{:S(2)}, u32[]{:S(2)}) collective-permute-start(bf16[256,512]{1,0:T(8,128)(2,1)S(1)} %param.4), channel_id=1, source_target_pairs={{0,32},{16,48},{32,64},{48,80},{64,96},{80,112},{96,128},{112,144}... | collective-permute-start | bytes 786440 | tf_op jit(solution)/shard_map/cond/branch_1_fun/ppermute | solution.py:16
  163.2 14.6 %collective-permute-done.7 = bf16[256,512]{1,0:T(8,128)(2,1)} collective-permute-done((bf16[256,512]{1,0:T(8,128)(2,1)S(1)}, bf16[256,512]{1,0:T(8,128)(2,1)}, u32[]{:S(2)}, u32[]{:S(2)}) %collective-permute-start.7) | collective-permute-done | bytes 262176 | tf_op jit(solution)/shard_map/cond/branch_1_fun/ppermute | solution.py:16
  177.8 2.2 %multiply_bitcast_fusion = f32[1,256,512]{2,1,0:T(8,128)} fusion(f32[256,512]{1,0:T(8,128)} %get-tuple-element.41, bf16[256,512]{1,0:T(8,128)(2,1)} %get-tuple-element.49, bf16[256,512]{1,0:T(8,128)(2,1)S(1)} %collective-permute-done.9, bf16[1,2,256,512]{3,2,1,0:T(8,128)(2,1)} %reduce-scatter.2.cloned.1.call-done, s32[]{:T(128)S(6)} %select_n.7, ...), kind=kLoop, calls=%fused_computation.10 | loop fusion | flops 1310720 | bytes 2359300 | tf_op jit(solution)/shard_map/broadcast_in_dim | solution.py:66
  (7 shorter events, 0.0 us)
Async XLA Ops:
  7.2 73.5 %all-gather.3.cloned.1.call-start = ((), (), s32[]{:S(2)}) async-start(), calls=%async_computation.2 | async-start | bytes 4718592 | tf_op jit(solution)/shard_map/all_gather | solution.py:37
  7.9 15.5 %copy-start.3 = (f32[4096]{0:T(1024)S(1)}, f32[4096]{0:T(1024)}, u32[]{:S(2)}) copy-start(f32[4096]{0:T(1024)} %param.17) | copy-start | bytes 49156
  19.9 127.1 %reduce-scatter.2.cloned.1.call-start = ((), (), s32[]{:S(2)}) async-start(), calls=%async_computation.1 | async-start | bytes 4718592 | tf_op jit(solution)/shard_map/reduce_scatter | solution.py:54
  25.7 1.7 copy-start
  27.4 1.0 copy-start.1
  27.4 53.3 %copy-start.4 = (bf16[1,384,512]{2,1,0:T(8,128)(2,1)S(1)}, bf16[1,384,512]{2,1,0:T(8,128)(2,1)}, u32[]{:S(2)}) copy-start(bf16[1,384,512]{2,1,0:T(8,128)(2,1)} %param.16) | copy-start | bytes 1179652
  28.4 27.8 %collective-permute-start.2 = (f32[256,512]{1,0:T(8,128)S(1)}, f32[256,512]{1,0:T(8,128)}, u32[]{:S(2)}, u32[]{:S(2)}) collective-permute-start(f32[256,512]{1,0:T(8,128)S(1)} %get-tuple-element.27), channel_id=1, source_target_pairs={{0,32},{16,48},{32,64},{48,80},{64,96},{80,112},{96,128},{112,144}... | collective-permute-start | bytes 1572872 | tf_op jit(solution)/shard_map/cond/branch_1_fun/ppermute | solution.py:16
  30.8 25.4 %collective-permute-start.3 = (f32[1]{0:T(128)}, f32[1]{0:T(128)}, u32[]{:S(2)}, u32[]{:S(2)}) collective-permute-start(f32[1]{0:T(128)} %get-tuple-element.28), channel_id=1, source_target_pairs={{0,32},{16,48},{32,64},{48,80},{64,96},{80,112},{96,128},{112,144}... | collective-permute-start | bytes 20 | tf_op jit(solution)/shard_map/cond/branch_1_fun/ppermute | solution.py:16
  90.0 87.9 %copy-start.2 = (f32[1,256,512]{2,1,0:T(8,128)S(1)}, f32[1,256,512]{2,1,0:T(8,128)}, u32[]{:S(2)}) copy-start(f32[1,256,512]{2,1,0:T(8,128)} %param.12) | copy-start | bytes 1572868
  148.0 9.9 %collective-permute-start.9 = (bf16[256,512]{1,0:T(8,128)(2,1)S(1)}, bf16[256,512]{1,0:T(8,128)(2,1)S(1)}, u32[]{:S(2)}, u32[]{:S(2)}) collective-permute-start(bf16[256,512]{1,0:T(8,128)(2,1)S(1)} %dynamic-slice_bitcast_fusion), channel_id=1, source_target_pairs={{0,8},{8,0},{1,9},{9,1},{2,10},{10,2},{3,11},{11,3},{4,12},{12,4},... | collective-permute-start | bytes 786440 | tf_op jit(solution)/shard_map/ppermute | solution.py:59
  158.9 19.0 %collective-permute-start.7 = (bf16[256,512]{1,0:T(8,128)(2,1)S(1)}, bf16[256,512]{1,0:T(8,128)(2,1)}, u32[]{:S(2)}, u32[]{:S(2)}) collective-permute-start(bf16[256,512]{1,0:T(8,128)(2,1)S(1)} %param.4), channel_id=1, source_target_pairs={{0,32},{16,48},{32,64},{48,80},{64,96},{80,112},{96,128},{112,144}... | collective-permute-start | bytes 786440 | tf_op jit(solution)/shard_map/cond/branch_1_fun/ppermute | solution.py:16
Sparse Core Ops, SparseCore 0:
  20.0 60.6 all-gather.2
  90.1 56.8 reduce-scatter.1

commit v6 on v2

--- a/solution.py
+++ b/solution.py
@@ -4,10 +4,55 @@
 import jax
 import jax.numpy as jnp
 from jax import lax
+from jax.experimental import pallas as pl
+from jax.experimental.pallas import tpu as pltpu
 from jax.sharding import Mesh, PartitionSpec as P
 
 DIST_KINDS = 3
 PAIR = 2
+CHUNK = 512
+
+
+def grad_kernel(normed_ref, normed_t_ref, params_ref, targets_ref, out_ref, keys_acc, errors_ref, *, key_scale, error_scale):
+    keys_acc[...] = jnp.zeros_like(keys_acc)
+
+    def key_step(i, carry):
+        at = pl.multiple_of(i * CHUNK, CHUNK)
+        keys_acc[...] += jnp.dot(
+            normed_ref[:, pl.ds(at, CHUNK)], params_ref[pl.ds(at, CHUNK), :],
+            preferred_element_type=jnp.float32,
+        )
+        return carry
+
+    lax.fori_loop(0, normed_ref.shape[1] // CHUNK, key_step, 0)
+    keys = keys_acc[...] / key_scale
+    errors_ref[...] = ((keys - targets_ref[...].astype(jnp.float32)) / error_scale).astype(jnp.bfloat16)
+
+    def grad_step(i, carry):
+        at = pl.multiple_of(i * CHUNK, CHUNK)
+        out_ref[pl.ds(at, CHUNK), :] = jnp.dot(
+            normed_t_ref[pl.ds(at, CHUNK), :], errors_ref[...],
+            preferred_element_type=jnp.float32,
+        ).astype(jnp.bfloat16)
+        return carry
+
+    lax.fori_loop(0, normed_t_ref.shape[0] // CHUNK, grad_step, 0)
+
+
+def block_gradient(normed, params, targets, key_scale, error_scale):
+    tokens, features = normed.shape
+    width = params.shape[1]
+    flops = 4 * tokens * features * width
+    moved = 2 * (2 * tokens * features + 2 * features * width + tokens * width)
+    vmem = pl.BlockSpec(memory_space=pltpu.VMEM)
+    return pl.pallas_call(
+        partial(grad_kernel, key_scale=key_scale, error_scale=error_scale),
+        out_shape=jax.ShapeDtypeStruct((features, width), jnp.bfloat16),
+        in_specs=[vmem] * 4,
+        out_specs=vmem,
+        scratch_shapes=[pltpu.VMEM((tokens, width), jnp.float32), pltpu.VMEM((tokens, width), jnp.bfloat16)],
+        cost_estimate=pl.CostEstimate(flops=flops, bytes_accessed=moved, transcendentals=0),
+    )(normed, normed.T, params, targets)
 
 
 def passed_along(value, axis, steps):
@@ -58,14 +103,10 @@
     normed = (act32 * lax.rsqrt(mean_sq + 1e-05) * gain[None, :]).astype(jnp.bfloat16)
     tokens = normed.shape[0]
     normed = normed.reshape(tokens, n_pair, n_ring, -1).transpose(0, 2, 1, 3).reshape(tokens, -1)
-    keys = jnp.dot(normed, full_params, preferred_element_type=jnp.float32) / math.sqrt(features)
-    errors = ((keys - targets[0].astype(jnp.float32)) / math.sqrt(replica_tokens)).astype(
-        jnp.bfloat16
+    peer_numer, peer_weight, normed = lax.optimization_barrier((peer_numer, peer_weight, normed))
+    partial_grad = block_gradient(
+        normed, full_params, targets[0], math.sqrt(features), math.sqrt(replica_tokens)
     )
-    peer_numer, peer_weight, errors = lax.optimization_barrier((peer_numer, peer_weight, errors))
-    partial_grad = lax.dot_general(
-        normed, errors, (((0,), (0,)), ((), ())), preferred_element_type=jnp.float32
-    ).astype(jnp.bfloat16)
     blocks = partial_grad.reshape(n_ring, n_pair, -1, partial_grad.shape[1])
     halves = lax.psum_scatter(blocks, "fz", scatter_dimension=0)
     side = lax.axis_index("fl")

time: 196 us -> 191 us (0.974); the launches traced: 192 us -> 190 us
  Pallas kernels: 0 us -> 12.6 us
  local copies, waits for them, and re-layouts: 8.07 us -> 17.6 us
  starting transfers between devices: 25.6 us -> 16.3 us
  matrix products: 9.26 us -> 0 us
  waiting for transfers between devices: 117 us -> 109 us
  other arithmetic: 5.95 us -> 8.3 us
    pallas_call x0 -> x1, Pallas kernels: none -> 12.6 us  [block_gradient(): pl.pallas_call(partial(grad_kernel, key_scale=key_scale, error_scale=erro...]
    dot_general x2 -> x0, matrix products: 9.26 us -> none  [the longest x1 4.97 us: body(): jnp.dot(normed, full_params, preferred_element_type=jnp.float32)]
    ppermute x1, waiting for transfers between devices: 19.5 us -> 10.5 us  [finish_and_send(): peer_other = lax.ppermute(other, ('replica', 'fl'), diagonal)]
    convert_element_type x0 -> x1, local copies, waits for them, and re-layouts: none -> 6.73 us  [body(): act32 = activations[0].astype(jnp.float32)]
    ppermute x3, starting transfers between devices: 15.7 us -> 10.9 us  [passed_along(): return lax.ppermute(value, axis, pairs)]
    ppermute x1, starting transfers between devices: 6.46 us -> 1.92 us  [finish_and_send(): peer_other = lax.ppermute(other, ('replica', 'fl'), diagonal)]
    ppermute x3, waiting for transfers between devices: 11.7 us -> 16.1 us  [passed_along(): return lax.ppermute(value, axis, pairs)]
    optimization_barrier x0 -> x1, local copies, waits for them, and re-layouts: none -> 3.47 us  [body(): lax.optimization_barrier((peer_numer, peer_weight, normed))]
  transfers between devices with their start and end apart: 7 -> 7, of which waited for: 4 -> 6; matrix products, arithmetic and copies ran while one was open for 3% -> 10% of each run, Pallas kernels for 0% -> 0%
where the time goes in v6:
time: 191 us; the launch traced here: 190 us
  waiting for transfers between devices  109 us (57%)
  local copies, waits for them, and re-layouts  17.6 us (9%)
  between operations  17.3 us (9%)
  starting transfers between devices  16.3 us (9%)
  Pallas kernels  12.6 us (7%)
  blocking collectives  8.82 us (5%)
  other arithmetic  8.3 us (4%)
    reduce_scatter x1, waiting for transfers between devices, body(): halves = lax.psum_scatter(blocks, 'fz', scatter_dimension=0)  56.2 us
    all_gather x1, waiting for transfers between devices, body(): gathered = lax.all_gather(gathered, 'fz', axis=0)  26 us
    ppermute x3, waiting for transfers between devices, passed_along(): return lax.ppermute(value, axis, pairs)  16.1 us
    pallas_call x1, Pallas kernels, block_gradient(): pl.pallas_call(partial(grad_kernel, key_scale=key_scale, error_scale=erro...  12.6 us
    ppermute x3, starting transfers between devices, passed_along(): return lax.ppermute(value, axis, pairs)  10.9 us
    ppermute x1, waiting for transfers between devices, finish_and_send(): peer_other = lax.ppermute(other, ('replica', 'fl'), diagonal)  10.5 us
    all_gather x1, blocking collectives, body(): gathered = lax.all_gather(params, 'fl', axis=0)  8.82 us
    convert_element_type x1, local copies, waits for them, and re-layouts, body(): act32 = activations[0].astype(jnp.float32)  6.73 us
  transfers between devices with their start and end apart: 7, of which 6 were waited for; matrix products, arithmetic and copies ran while one was open for 10% of the time, Pallas kernels for 0%

profile of v6, /device:TPU:6, one launch (start us, length us, event | category | flops | bytes accessed | tf_op | source)
XLA Modules:
  0.0 190.1 jit_solution(9984922710073704613)
XLA Ops:
  7.2 0.0 all-gather.3.cloned.1.call-start
  7.9 1.1 divide_convert_fusion
  8.9 8.8 %all_gather.10 = bf16[2,256,512]{2,1,0:T(8,128)(2,1)} all-gather(bf16[1,256,512]{2,1,0:T(8,128)(2,1)S(1)} %divide_convert_fusion), channel_id=1, replica_groups=mesh['replica'=32,'fl'=2,'fz'=8] {'fl'}, dimensions={0}, use_global_device_ids=true | all-gather | bytes 786432 | tf_op jit(solution)/shard_map/all_gather | solution.py:97
  17.8 0.0 all-gather.3.cloned.1.call-update
  17.8 0.0 reduce-scatter.2.cloned.1.call-start
  18.5 5.4 %copy.16 = f32[48,8,16,256]{3,2,1,0:T(8,128)} copy(bf16[48,8,16,256]{3,1,2,0:T(8,128)(2,1)} %bitcast.33) | data formatting | bytes 9437184
  23.9 6.7 %copy.13 = f32[384,2,8,256]{0,3,1,2:T(8,128)} copy(f32[384,2,8,256]{3,2,1,0:T(8,128)} %bitcast.31) | data formatting | bytes 12582912 | tf_op jit(solution)/shard_map/convert_element_type | solution.py:101
  30.6 0.0 copy-done.3
  30.7 16.6 %conditional.3 = (f32[256,512]{1,0:T(8,128)}, f32[1]{0:T(128)}) conditional(s32[]{:T(128)} %bitcast.4, (f32[256,512]{1,0:T(8,128)}, f32[1]{0:T(128)}) %tuple.72, (f32[256,512]{1,0:T(8,128)}, f32[1]{0:T(128)}) %tuple.73, (f32[256,512]{1,0:T(8,128)}, f32[1]{0:T(128)}) %tuple.74), branch_computations={%region_0.0_spmd, %region_1.0_spmd, %region_2.0_spmd} | conditional | bytes 2097264 | solution.py:86
  30.7 1.9 %collective-permute-start = (f32[256,512]{1,0:T(8,128)}, f32[256,512]{1,0:T(8,128)}, u32[]{:S(2)}, u32[]{:S(2)}) collective-permute-start(f32[256,512]{1,0:T(8,128)} %get-tuple-element.75), channel_id=1, source_target_pairs={{0,16},{16,32},{32,48},{48,64},{64,80},{80,96},{96,112},{112,128},... | collective-permute-start | bytes 1572872 | tf_op jit(solution)/shard_map/cond/branch_0_fun/ppermute | solution.py:61
  32.6 4.6 %collective-permute-start.1 = (f32[1]{0:T(128)}, f32[1]{0:T(128)}, u32[]{:S(2)}, u32[]{:S(2)}) collective-permute-start(f32[1]{0:T(128)} %get-tuple-element.76), channel_id=1, source_target_pairs={{0,16},{16,32},{32,48},{48,64},{64,80},{80,96},{96,112},{112,128},... | collective-permute-start | bytes 20 | tf_op jit(solution)/shard_map/cond/branch_0_fun/ppermute | solution.py:61
  37.2 10.0 %collective-permute-done.1 = f32[1]{0:T(128)} collective-permute-done((f32[1]{0:T(128)}, f32[1]{0:T(128)}, u32[]{:S(2)}, u32[]{:S(2)}) %collective-permute-start.1) | collective-permute-done | bytes 36 | tf_op jit(solution)/shard_map/cond/branch_0_fun/ppermute | solution.py:61
  47.2 0.0 collective-permute-done
  47.2 0.0 copy-done.1
  47.2 0.7 multiply_reduce_fusion
  47.9 3.3 %multiply_convert_fusion = bf16[384,2,8,256]{0,3,1,2:T(8,128)(2,1)S(1)} fusion(f32[384,2,8,256]{0,3,1,2:T(8,128)} %copy.13, f32[2,8,256]{2,0,1:T(2,128)S(1)} %copy.14, f32[384]{0:T(512)S(1)} %add_rsqrt_fusion), kind=kLoop, calls=%fused_computation.6 | loop fusion | flops 4718592 | bytes 9455104 | tf_op jit(solution)/shard_map/convert_element_type | solution.py:103
  51.2 3.5 %copy.15.normed_ref = bf16[384,4096]{1,0:T(8,128)(2,1)} copy(bf16[384,4096]{0,1:T(8,128)(2,1)S(1)} %bitcast.29) | data formatting | bytes 6291456 | tf_op jit(solution)/shard_map/optimization_barrier | solution.py:106
  54.7 26.0 %all-gather.3.cloned.1.call-done = bf16[16,256,512]{2,1,0:T(8,128)(2,1)} async-done(((bf16[2,256,512]{2,1,0:T(8,128)(2,1)}), bf16[16,256,512]{2,1,0:T(8,128)(2,1)}) %all-gather.3.cloned.1.call-update) | async-done | bytes 4194320 | tf_op jit(solution)/shard_map/all_gather | solution.py:98
  80.7 12.6 %shard_map.77 = bf16[4096,512]{1,0:T(8,128)(2,1)} custom-call(bf16[384,4096]{1,0:T(8,128)(2,1)} %copy.15.normed_ref, bf16[4096,384]{1,0:T(8,128)(2,1)} %bitcast.30, bf16[4096,512]{1,0:T(8,128)(2,1)} %bitcast.34, bf16[384,512]{1,0:T(8,128)(2,1)} %bitcast.38), custom_call_target="tpu_custom_call" | custom-call | flops 3221225472 | bytes 15073280 | tf_op jit(solution)/shard_map/pallas_call | solution.py:48
  93.3 0.0 reduce-scatter.2.cloned.1.call-update
  94.1 56.2 %reduce-scatter.2.cloned.1.call-done = bf16[1,2,256,512]{3,2,1,0:T(8,128)(2,1)} async-done(((bf16[8,2,256,512]{3,2,1,0:T(8,128)(2,1)}), bf16[1,2,256,512]{3,2,1,0:T(8,128)(2,1)}) %reduce-scatter.2.cloned.1.call-update) | async-done | bytes 524304 | tf_op jit(solution)/shard_map/reduce_scatter | solution.py:111
  150.3 1.0 dynamic-slice_bitcast_fusion.3
  151.3 28.6 %conditional.5 = (bf16[256,512]{1,0:T(8,128)(2,1)}, f32[256,512]{1,0:T(8,128)S(1)}, f32[256,512]{1,0:T(8,128)S(1)}) conditional(s32[]{:T(128)} %bitcast.4, (bf16[256,512]{1,0:T(8,128)(2,1)S(1)}, s32[]{:T(128)}, bf16[1,2,256,512]{3,2,1,0:T(8,128)(2,1)}) %tuple.53, (bf16[256,512]{1,0:T(8,128)(2,1)S(1)}, s32[]{:T(128)}, ...), branch_computations={%region_5.6_spmd, %region_6.7_spmd, %region_7.8_spmd} | conditional | flops 524292 | bytes 5505218
  151.3 1.0 dynamic-slice_bitcast_fusion
  152.3 3.4 %collective-permute-start.8 = (bf16[256,512]{1,0:T(8,128)(2,1)S(1)}, bf16[256,512]{1,0:T(8,128)(2,1)S(1)}, u32[]{:S(2)}, u32[]{:S(2)}) collective-permute-start(bf16[256,512]{1,0:T(8,128)(2,1)S(1)} %dynamic-slice_bitcast_fusion), channel_id=1, source_target_pairs={{0,8},{8,0},{1,9},{9,1},{2,10},{10,2},{3,11},{11,3},{4,12},{12,4},... | collective-permute-start | bytes 786440 | tf_op jit(solution)/shard_map/cond/branch_0_fun/ppermute | solution.py:78
  155.7 1.9 %collective-permute-start.7 = (bf16[256,512]{1,0:T(8,128)(2,1)S(1)}, bf16[256,512]{1,0:T(8,128)(2,1)S(1)}, u32[]{:S(2)}, u32[]{:S(2)}) collective-permute-start(bf16[256,512]{1,0:T(8,128)(2,1)S(1)} %dynamic-slice_bitcast_fusion), channel_id=1, source_target_pairs={{0,24},{8,16},{16,40},{24,32},{32,56},{40,48},{48,72},{56,64},{64,... | collective-permute-start | bytes 786440 | tf_op jit(solution)/shard_map/cond/branch_0_fun/ppermute | solution.py:80
  157.6 4.4 %collective-permute-start.6 = (bf16[256,512]{1,0:T(8,128)(2,1)S(1)}, bf16[256,512]{1,0:T(8,128)(2,1)}, u32[]{:S(2)}, u32[]{:S(2)}) collective-permute-start(bf16[256,512]{1,0:T(8,128)(2,1)S(1)} %get-tuple-element.81), channel_id=1, source_target_pairs={{0,16},{16,32},{32,48},{48,64},{64,80},{80,96},{96,112},{112,128},... | collective-permute-start | bytes 786440 | tf_op jit(solution)/shard_map/cond/branch_0_fun/ppermute | solution.py:61
  162.0 0.1 collective-permute-done.8
  162.2 10.5 %collective-permute-done.7 = bf16[256,512]{1,0:T(8,128)(2,1)S(1)} collective-permute-done((bf16[256,512]{1,0:T(8,128)(2,1)S(1)}, bf16[256,512]{1,0:T(8,128)(2,1)S(1)}, u32[]{:S(2)}, u32[]{:S(2)}) %collective-permute-start.7) | collective-permute-done | bytes 262176 | tf_op jit(solution)/shard_map/cond/branch_0_fun/ppermute | solution.py:80
  172.7 6.1 %collective-permute-done.6 = bf16[256,512]{1,0:T(8,128)(2,1)} collective-permute-done((bf16[256,512]{1,0:T(8,128)(2,1)S(1)}, bf16[256,512]{1,0:T(8,128)(2,1)}, u32[]{:S(2)}, u32[]{:S(2)}) %collective-permute-start.6) | collective-permute-done | bytes 262176 | tf_op jit(solution)/shard_map/cond/branch_0_fun/ppermute | solution.py:61
  178.9 1.0 convert_add_fusion
  179.9 2.2 %multiply_bitcast_fusion = f32[1,256,512]{2,1,0:T(8,128)} fusion(f32[256,512]{1,0:T(8,128)} %get-tuple-element.103, f32[256,512]{1,0:T(8,128)S(1)} %get-tuple-element.104, f32[256,512]{1,0:T(8,128)S(1)} %get-tuple-element.110, f32[1,256,512]{2,1,0:T(8,128)S(1)} %copy-done.2, bf16[1,2,256,512]{3,2,1,0:T(8,128)(2,1)} %reduce-scatter.2.cloned.1.call-done, ...), kind=kLoop, calls=%fused_computation.8 | loop fusion | flops 1048576 | bytes 2883588 | tf_op jit(solution)/shard_map/broadcast_in_dim | solution.py:122
  (10 shorter events, 0.1 us)
Async XLA Ops:
  7.2 73.6 %all-gather.3.cloned.1.call-start = ((), (), s32[]{:S(2)}) async-start(), calls=%async_computation.2 | async-start | bytes 4718592 | tf_op jit(solution)/shard_map/all_gather | solution.py:98
  17.8 132.5 %reduce-scatter.2.cloned.1.call-start = ((), (), s32[]{:S(2)}) async-start(), calls=%async_computation.1 | async-start | bytes 4718592 | tf_op jit(solution)/shard_map/reduce_scatter | solution.py:111
  23.9 6.7 %copy-start.3 = (f32[4096]{0:T(1024)S(1)}, f32[4096]{0:T(1024)}, u32[]{:S(2)}) copy-start(f32[4096]{0:T(1024)} %param.17) | copy-start | bytes 49156
  23.9 23.3 %copy-start.1 = (bf16[1,384,4096]{2,1,0:T(8,128)(2,1)S(1)}, bf16[1,384,4096]{2,1,0:T(8,128)(2,1)}, u32[]{:S(2)}) copy-start(bf16[1,384,4096]{2,1,0:T(8,128)(2,1)} %param.15) | copy-start | bytes 9437188
  30.7 16.6 %collective-permute-start = (f32[256,512]{1,0:T(8,128)}, f32[256,512]{1,0:T(8,128)}, u32[]{:S(2)}, u32[]{:S(2)}) collective-permute-start(f32[256,512]{1,0:T(8,128)} %get-tuple-element.75), channel_id=1, source_target_pairs={{0,16},{16,32},{32,48},{48,64},{64,80},{80,96},{96,112},{112,128},... | collective-permute-start | bytes 1572872 | tf_op jit(solution)/shard_map/cond/branch_0_fun/ppermute | solution.py:61
  32.6 14.6 %collective-permute-start.1 = (f32[1]{0:T(128)}, f32[1]{0:T(128)}, u32[]{:S(2)}, u32[]{:S(2)}) collective-permute-start(f32[1]{0:T(128)} %get-tuple-element.76), channel_id=1, source_target_pairs={{0,16},{16,32},{32,48},{48,64},{64,80},{80,96},{96,112},{112,128},... | collective-permute-start | bytes 20 | tf_op jit(solution)/shard_map/cond/branch_0_fun/ppermute | solution.py:61
  51.2 29.5 %copy-start = (bf16[384,2,8,256]{0,3,1,2:T(8,128)(2,1)}, bf16[384,2,8,256]{0,3,1,2:T(8,128)(2,1)S(1)}, u32[]{:S(2)}) copy-start(bf16[384,2,8,256]{0,3,1,2:T(8,128)(2,1)S(1)} %multiply_convert_fusion) | copy-start | bytes 9437188
  93.3 86.6 %copy-start.2 = (f32[1,256,512]{2,1,0:T(8,128)S(1)}, f32[1,256,512]{2,1,0:T(8,128)}, u32[]{:S(2)}) copy-start(f32[1,256,512]{2,1,0:T(8,128)} %param.12) | copy-start | bytes 1572868
  152.3 9.9 %collective-permute-start.8 = (bf16[256,512]{1,0:T(8,128)(2,1)S(1)}, bf16[256,512]{1,0:T(8,128)(2,1)S(1)}, u32[]{:S(2)}, u32[]{:S(2)}) collective-permute-start(bf16[256,512]{1,0:T(8,128)(2,1)S(1)} %dynamic-slice_bitcast_fusion), channel_id=1, source_target_pairs={{0,8},{8,0},{1,9},{9,1},{2,10},{10,2},{3,11},{11,3},{4,12},{12,4},... | collective-permute-start | bytes 786440 | tf_op jit(solution)/shard_map/cond/branch_0_fun/ppermute | solution.py:78
  155.7 17.1 %collective-permute-start.7 = (bf16[256,512]{1,0:T(8,128)(2,1)S(1)}, bf16[256,512]{1,0:T(8,128)(2,1)S(1)}, u32[]{:S(2)}, u32[]{:S(2)}) collective-permute-start(bf16[256,512]{1,0:T(8,128)(2,1)S(1)} %dynamic-slice_bitcast_fusion), channel_id=1, source_target_pairs={{0,24},{8,16},{16,40},{24,32},{32,56},{40,48},{48,72},{56,64},{64,... | collective-permute-start | bytes 786440 | tf_op jit(solution)/shard_map/cond/branch_0_fun/ppermute | solution.py:80
  157.6 21.3 %collective-permute-start.6 = (bf16[256,512]{1,0:T(8,128)(2,1)S(1)}, bf16[256,512]{1,0:T(8,128)(2,1)}, u32[]{:S(2)}, u32[]{:S(2)}) collective-permute-start(bf16[256,512]{1,0:T(8,128)(2,1)S(1)} %get-tuple-element.81), channel_id=1, source_target_pairs={{0,16},{16,32},{32,48},{48,64},{64,80},{80,96},{96,112},{112,128},... | collective-permute-start | bytes 786440 | tf_op jit(solution)/shard_map/cond/branch_0_fun/ppermute | solution.py:61
Sparse Core Ops, SparseCore 0:
  17.9 62.7 all-gather.2
  93.5 56.8 reduce-scatter.1

commit v7 on v1

--- a/solution.py
+++ b/solution.py
@@ -47,12 +47,19 @@
         jnp.bfloat16
     )
     peer_numer, peer_weight, errors = lax.optimization_barrier((peer_numer, peer_weight, errors))
-    partial_grad = lax.dot_general(
-        normed, errors, (((0,), (0,)), ((), ())), preferred_element_type=jnp.float32
-    ).astype(jnp.bfloat16)
-    blocks = partial_grad.reshape(n_ring, n_pair, -1, partial_grad.shape[1])
+    side = lax.axis_index("fl")
+    flip = [(i, n_pair - 1 - i) for i in range(n_pair)]
+    by_block = normed.reshape(tokens, n_ring, n_pair, -1)
+    own_cols = lax.dynamic_index_in_dim(by_block, side, 2, keepdims=False).reshape(tokens, -1)
+    partner_cols = lax.dynamic_index_in_dim(by_block, n_pair - 1 - side, 2, keepdims=False)
+    their_cols = lax.ppermute(partner_cols, "fl", flip).reshape(tokens, -1)
+    their_errors = lax.ppermute(errors, "fl", flip)
+    contract = (((0,), (0,)), ((), ()))
+    mine = lax.dot_general(own_cols, errors, contract, preferred_element_type=jnp.float32)
+    theirs = lax.dot_general(their_cols, their_errors, contract, preferred_element_type=jnp.float32)
+    pair_sum = mine.astype(jnp.bfloat16).astype(jnp.float32) + theirs.astype(jnp.bfloat16).astype(jnp.float32)
+    blocks = pair_sum.astype(jnp.bfloat16).reshape(n_ring, -1, pair_sum.shape[1])
     grad16 = lax.psum_scatter(blocks, "fz", scatter_dimension=0)
-    grad16 = lax.psum_scatter(grad16, "fl", scatter_dimension=0)
     peer_grad16 = to_peer(send_to_peer, grad16, power)
     updated = numer - 0.3 * grad16.astype(jnp.float32)
     peer_updated = peer_numer - 0.3 * peer_grad16.astype(jnp.float32)

time: 194 us -> 176 us (0.907)
  waiting for transfers between devices: 137 us -> 107 us
  starting transfers between devices: 8.54 us -> 13.9 us
  other arithmetic: 4.86 us -> 7.17 us
  local copies, waits for them, and re-layouts: 6.15 us -> 8.45 us
    all_gather x1, waiting for transfers between devices: 38 us -> 0.01 us  [body(): gathered = lax.all_gather(gathered, 'fz', axis=0)]
    ppermute x3, waiting for transfers between devices: 19.1 us -> 52.7 us  [passed_along(): return lax.ppermute(value, axis, pairs)]
    reduce_scatter x1 -> x0, waiting for transfers between devices: 22.8 us -> none  [body(): grad16 = lax.psum_scatter(grad16, 'fl', scatter_dimension=0)]
    reduce_scatter x1, waiting for transfers between devices: 56.9 us -> 46.9 us  [body(): grad16 = lax.psum_scatter(blocks, 'fz', scatter_dimension=0)]
    ppermute x0 -> x2, waiting for transfers between devices: none -> 7.85 us  [the longest x1 7.85 us: body(): their_errors = lax.ppermute(errors, 'fl', flip)]
    unnamed x11 -> x8, local copies, waits for them, and re-layouts: 5.71 us -> 0.02 us
    convert_element_type x0 -> x1, local copies, waits for them, and re-layouts: none -> 5.56 us  [body(): act32 = activations[0].astype(jnp.float32)]
    ppermute x0 -> x2, starting transfers between devices: none -> 5.39 us  [the longest x1 3.47 us: body(): their_cols = lax.ppermute(partner_cols, 'fl', flip).reshape(tokens, -1)]
  transfers between devices with their start and end apart: 6 -> 7, of which waited for: 5 -> 4; matrix products, arithmetic and copies ran while one was open for 3% -> 12% of each run, Pallas kernels for 0% -> 0%
where the time goes in v7:
time: 176 us; the launch traced here: 174 us
  waiting for transfers between devices  107 us (61%)
  between operations  17.2 us (10%)
  starting transfers between devices  13.9 us (8%)
  matrix products  10.8 us (6%)
  blocking collectives  8.82 us (5%)
  local copies, waits for them, and re-layouts  8.45 us (5%)
  other arithmetic  7.17 us (4%)
    ppermute x3, waiting for transfers between devices, passed_along(): return lax.ppermute(value, axis, pairs)  52.7 us
    reduce_scatter x1, waiting for transfers between devices, body(): grad16 = lax.psum_scatter(blocks, 'fz', scatter_dimension=0)  46.9 us
    all_gather x1, blocking collectives, body(): gathered = lax.all_gather(params, 'fl', axis=0)  8.82 us
    ppermute x3, starting transfers between devices, passed_along(): return lax.ppermute(value, axis, pairs)  8.43 us
    ppermute x1, waiting for transfers between devices, body(): their_errors = lax.ppermute(errors, 'fl', flip)  7.85 us
    dot_general x1, matrix products, body(): jnp.dot(normed, full_params, preferred_element_type=jnp.float32)  6.82 us
    convert_element_type x1, local copies, waits for them, and re-layouts, body(): act32 = activations[0].astype(jnp.float32)  5.56 us
  transfers between devices with their start and end apart: 7, of which 4 were waited for; matrix products, arithmetic and copies ran while one was open for 12% of the time, Pallas kernels for 0%

profile of v7, /device:TPU:6, one launch (start us, length us, event | category | flops | bytes accessed | tf_op | source)
XLA Modules:
  0.0 173.8 jit_solution(11913679313061415400)
XLA Ops:
  7.2 0.0 all-gather.3.cloned.1.call-start
  7.9 1.1 divide_convert_fusion
  8.9 8.8 %all_gather.10 = bf16[2,256,512]{2,1,0:T(8,128)(2,1)} all-gather(bf16[1,256,512]{2,1,0:T(8,128)(2,1)S(1)} %divide_convert_fusion), channel_id=1, replica_groups=mesh['replica'=32,'fl'=2,'fz'=8] {'fl'}, dimensions={0}, use_global_device_ids=true | all-gather | bytes 786432 | tf_op jit(solution)/shard_map/all_gather | solution.py:36
  17.8 0.0 all-gather.3.cloned.1.call-update
  17.8 0.0 reduce-scatter.2.cloned.1.call-start
  17.8 0.7 mul.42
  18.6 5.6 %copy.11 = f32[1,384,4096]{1,2,0:T(8,128)} copy(bf16[1,384,4096]{2,1,0:T(8,128)(2,1)} %param.15) | data formatting | bytes 9437184 | tf_op jit(solution)/shard_map/convert_element_type | solution.py:40
  24.1 0.7 multiply_reduce_fusion
  24.8 3.2 %multiply_convert_fusion = bf16[384,2,8,256]{0,3,2,1:T(8,128)(2,1)S(1)} fusion(f32[384,2,8,256]{0,3,2,1:T(8,128)} %bitcast.40, f32[2,8,256]{2,1,0:T(8,128)S(1)} %mul.42, f32[384]{0:T(512)S(1)} %add_rsqrt_fusion), kind=kLoop, calls=%fused_computation | loop fusion | flops 4718592 | bytes 9455104 | tf_op jit(solution)/shard_map/convert_element_type | solution.py:42
  28.1 0.0 copy-start.1
  28.1 0.0 copy-start.3
  28.1 2.1 %dynamic-slice_bitcast_fusion = (bf16[384,8,256]{0,2,1:T(8,128)(2,1)}, bf16[384,1,8,256]{0,3,2,1:T(8,128)(2,1)}) fusion(bf16[384,2,8,256]{0,3,2,1:T(8,128)(2,1)S(1)} %multiply_convert_fusion, s32[]{:T(128)S(6)} %select_n.8, s32[]{:T(128)S(6)} %select_n.7), kind=kLoop, calls=%fused_computation.7 | loop fusion | bytes 6291464 | tf_op jit(solution)/shard_map/jit(dynamic_index_in_dim)/squeeze | solution.py:54
  30.2 3.5 %collective-permute-start.9 = (bf16[384,8,256]{0,2,1:T(8,128)(2,1)}, bf16[384,8,256]{0,2,1:T(8,128)(2,1)S(1)}, u32[]{:S(2)}, u32[]{:S(2)}) collective-permute-start(bf16[384,8,256]{0,2,1:T(8,128)(2,1)} %get-tuple-element.43), channel_id=1, source_target_pairs={{0,8},{8,0},{1,9},{9,1},{2,10},{10,2},{3,11},{11,3},{4,12},{12,4},... | collective-permute-start | bytes 4718600 | tf_op jit(solution)/shard_map/ppermute | solution.py:55
  34.4 47.8 %conditional.5 = (f32[256,512]{1,0:T(8,128)}, f32[1]{0:T(128)}) conditional(s32[]{:T(128)} %bitcast.3, (f32[256,512]{1,0:T(8,128)S(1)}, f32[1]{0:T(128)}) %tuple.58, (f32[256,512]{1,0:T(8,128)S(1)}, f32[1]{0:T(128)}) %tuple.59, (f32[256,512]{1,0:T(8,128)S(1)}, f32[1]{0:T(128)}) %tuple.60), branch_computations={%region_1.0_spmd, %region_2.0_spmd, %region_3.0_spmd} | conditional | bytes 2097264 | solution.py:25
  34.4 1.9 %collective-permute-start = (f32[256,512]{1,0:T(8,128)S(1)}, f32[256,512]{1,0:T(8,128)}, u32[]{:S(2)}, u32[]{:S(2)}) collective-permute-start(f32[256,512]{1,0:T(8,128)S(1)} %get-tuple-element.25), channel_id=1, source_target_pairs={{0,16},{16,32},{32,48},{48,64},{64,80},{80,96},{96,112},{112,128},... | collective-permute-start | bytes 1572872 | tf_op jit(solution)/shard_map/cond/branch_0_fun/ppermute | solution.py:16
  36.3 4.6 %collective-permute-start.1 = (f32[1]{0:T(128)}, f32[1]{0:T(128)}, u32[]{:S(2)}, u32[]{:S(2)}) collective-permute-start(f32[1]{0:T(128)} %get-tuple-element.26), channel_id=1, source_target_pairs={{0,16},{16,32},{32,48},{48,64},{64,80},{80,96},{96,112},{112,128},... | collective-permute-start | bytes 20 | tf_op jit(solution)/shard_map/cond/branch_0_fun/ppermute | solution.py:16
  40.9 41.3 %collective-permute-done.1 = f32[1]{0:T(128)} collective-permute-done((f32[1]{0:T(128)}, f32[1]{0:T(128)}, u32[]{:S(2)}, u32[]{:S(2)}) %collective-permute-start.1) | collective-permute-done | bytes 36 | tf_op jit(solution)/shard_map/cond/branch_0_fun/ppermute | solution.py:16
  82.2 0.0 collective-permute-done
  82.2 0.0 copy-done.3
  82.2 6.8 %fusion.14 = bf16[384,512]{1,0:T(8,128)(2,1)S(1)} fusion(bf16[8,2,256,512]{3,2,1,0:T(8,128)(2,1)} %bitcast.43, bf16[1,384,512]{2,1,0:T(8,128)(2,1)S(1)} %copy-done.3, f32[2,8,256]{2,1,0:T(8,128)S(1)} %mul.42, f32[384,2,8,256]{0,3,2,1:T(8,128)} %bitcast.41, f32[384]{0:T(512)S(1)} %add_rsqrt_fusion), kind=kOutput, calls=%fused_computation.12 | convolution fusion | flops 1616314368 | bytes 11290112 | tf_op jit(solution)/shard_map/dot_general | solution.py:45
  89.1 1.9 %collective-permute-start.10 = (bf16[384,512]{1,0:T(8,128)(2,1)S(1)}, bf16[384,512]{1,0:T(8,128)(2,1)S(1)}, u32[]{:S(2)}, u32[]{:S(2)}) collective-permute-start(bf16[384,512]{1,0:T(8,128)(2,1)S(1)} %fusion.14), channel_id=1, source_target_pairs={{0,8},{8,0},{1,9},{9,1},{2,10},{10,2},{3,11},{11,3},{4,12},{12,4},... | collective-permute-start | bytes 1179656 | tf_op jit(solution)/shard_map/ppermute | solution.py:56
  91.0 0.0 copy-done.2
  91.0 1.3 convolution_convert_fusion.1
  92.3 0.0 collective-permute-done.9
  92.3 7.8 %collective-permute-done.10 = bf16[384,512]{1,0:T(8,128)(2,1)S(1)} collective-permute-done((bf16[384,512]{1,0:T(8,128)(2,1)S(1)}, bf16[384,512]{1,0:T(8,128)(2,1)S(1)}, u32[]{:S(2)}, u32[]{:S(2)}) %collective-permute-start.10) | collective-permute-done | bytes 393248 | tf_op jit(solution)/shard_map/ppermute | solution.py:56
  100.1 2.7 %add_convert_fusion = bf16[2048,512]{1,0:T(8,128)(2,1)} fusion(bf16[2048,512]{1,0:T(8,128)(2,1)S(1)} %convolution_convert_fusion.1, bf16[384,2048]{0,1:T(8,128)(2,1)S(1)} %bitcast.47, bf16[384,512]{1,0:T(8,128)(2,1)S(1)} %collective-permute-done.10), kind=kOutput, calls=%fused_computation.2 | convolution fusion | flops 810549248 | bytes 6160384 | tf_op jit(solution)/shard_map/dot_general | solution.py:59
  102.8 0.0 reduce-scatter.2.cloned.1.call-update
  103.5 46.9 %reduce-scatter.2.cloned.1.call-done = bf16[1,256,512]{2,1,0:T(8,128)(2,1)} async-done(((bf16[8,256,512]{2,1,0:T(8,128)(2,1)}), bf16[1,256,512]{2,1,0:T(8,128)(2,1)}) %reduce-scatter.2.cloned.1.call-update) | async-done | bytes 262160 | tf_op jit(solution)/shard_map/reduce_scatter | solution.py:62
  150.3 13.3 %conditional.6 = (bf16[256,512]{1,0:T(8,128)(2,1)}) conditional(s32[]{:T(128)} %bitcast.3, bf16[256,512]{1,0:T(8,128)(2,1)} %bitcast.49, bf16[256,512]{1,0:T(8,128)(2,1)} %bitcast.50, bf16[256,512]{1,0:T(8,128)(2,1)} %bitcast.51), branch_computations={%region_5.6_spmd, %region_6.7_spmd, %region_7.8_spmd} | conditional | bytes 1048624
  150.3 1.9 %collective-permute-start.6 = (bf16[256,512]{1,0:T(8,128)(2,1)}, bf16[256,512]{1,0:T(8,128)(2,1)}, u32[]{:S(2)}, u32[]{:S(2)}) collective-permute-start(bf16[256,512]{1,0:T(8,128)(2,1)} %param.3), channel_id=1, source_target_pairs={{0,16},{16,32},{32,48},{48,64},{64,80},{80,96},{96,112},{112,128},... | collective-permute-start | bytes 786440 | tf_op jit(solution)/shard_map/cond/branch_0_fun/ppermute | solution.py:16
  152.2 11.4 %collective-permute-done.6 = bf16[256,512]{1,0:T(8,128)(2,1)} collective-permute-done((bf16[256,512]{1,0:T(8,128)(2,1)}, bf16[256,512]{1,0:T(8,128)(2,1)}, u32[]{:S(2)}, u32[]{:S(2)}) %collective-permute-start.6) | collective-permute-done | bytes 262176 | tf_op jit(solution)/shard_map/cond/branch_0_fun/ppermute | solution.py:16
  163.7 2.1 %multiply_bitcast_fusion = f32[1,256,512]{2,1,0:T(8,128)} fusion(f32[256,512]{1,0:T(8,128)} %get-tuple-element.41, bf16[256,512]{1,0:T(8,128)(2,1)} %get-tuple-element.51, bf16[1,256,512]{2,1,0:T(8,128)(2,1)} %reduce-scatter.2.cloned.1.call-done, f32[1,256,512]{2,1,0:T(8,128)S(1)} %copy-done.1), kind=kLoop, calls=%fused_computation.13 | loop fusion | flops 1048576 | bytes 2097152 | tf_op jit(solution)/shard_map/broadcast_in_dim | solution.py:68
  (6 shorter events, 0.0 us)
Async XLA Ops:
  7.2 75.1 %all-gather.3.cloned.1.call-start = ((), (), s32[]{:S(2)}) async-start(), calls=%async_computation.2 | async-start | bytes 4718592 | tf_op jit(solution)/shard_map/all_gather | solution.py:37
  17.8 132.5 %reduce-scatter.2.cloned.1.call-start = ((), (), s32[]{:S(2)}) async-start(), calls=%async_computation.1 | async-start | bytes 2359296 | tf_op jit(solution)/shard_map/reduce_scatter | solution.py:62
  18.6 5.6 %copy-start = (bf16[1,384,4096]{2,1,0:T(8,128)(2,1)S(1)}, bf16[1,384,4096]{2,1,0:T(8,128)(2,1)}, u32[]{:S(2)}) copy-start(bf16[1,384,4096]{2,1,0:T(8,128)(2,1)} %param.15) | copy-start | bytes 9437188
  28.1 6.3 %copy-start.1 = (f32[1,256,512]{2,1,0:T(8,128)S(1)}, f32[1,256,512]{2,1,0:T(8,128)}, u32[]{:S(2)}) copy-start(f32[1,256,512]{2,1,0:T(8,128)} %param.12) | copy-start | bytes 1572868
  28.1 54.1 %copy-start.3 = (bf16[1,384,512]{2,1,0:T(8,128)(2,1)S(1)}, bf16[1,384,512]{2,1,0:T(8,128)(2,1)}, u32[]{:S(2)}) copy-start(bf16[1,384,512]{2,1,0:T(8,128)(2,1)} %param.16) | copy-start | bytes 1179652
  30.2 62.0 %collective-permute-start.9 = (bf16[384,8,256]{0,2,1:T(8,128)(2,1)}, bf16[384,8,256]{0,2,1:T(8,128)(2,1)S(1)}, u32[]{:S(2)}, u32[]{:S(2)}) collective-permute-start(bf16[384,8,256]{0,2,1:T(8,128)(2,1)} %get-tuple-element.43), channel_id=1, source_target_pairs={{0,8},{8,0},{1,9},{9,1},{2,10},{10,2},{3,11},{11,3},{4,12},{12,4},... | collective-permute-start | bytes 4718600 | tf_op jit(solution)/shard_map/ppermute | solution.py:55
  34.4 47.8 %collective-permute-start = (f32[256,512]{1,0:T(8,128)S(1)}, f32[256,512]{1,0:T(8,128)}, u32[]{:S(2)}, u32[]{:S(2)}) collective-permute-start(f32[256,512]{1,0:T(8,128)S(1)} %get-tuple-element.25), channel_id=1, source_target_pairs={{0,16},{16,32},{32,48},{48,64},{64,80},{80,96},{96,112},{112,128},... | collective-permute-start | bytes 1572872 | tf_op jit(solution)/shard_map/cond/branch_0_fun/ppermute | solution.py:16
  36.3 45.9 %collective-permute-start.1 = (f32[1]{0:T(128)}, f32[1]{0:T(128)}, u32[]{:S(2)}, u32[]{:S(2)}) collective-permute-start(f32[1]{0:T(128)} %get-tuple-element.26), channel_id=1, source_target_pairs={{0,16},{16,32},{32,48},{48,64},{64,80},{80,96},{96,112},{112,128},... | collective-permute-start | bytes 20 | tf_op jit(solution)/shard_map/cond/branch_0_fun/ppermute | solution.py:16
  82.2 8.8 %copy-start.2 = (bf16[384,1,8,256]{0,3,2,1:T(8,128)(2,1)S(1)}, bf16[384,1,8,256]{0,3,2,1:T(8,128)(2,1)}, u32[]{:S(2)}) copy-start(bf16[384,1,8,256]{0,3,2,1:T(8,128)(2,1)} %get-tuple-element.44) | copy-start | bytes 4718596
  89.1 11.1 %collective-permute-start.10 = (bf16[384,512]{1,0:T(8,128)(2,1)S(1)}, bf16[384,512]{1,0:T(8,128)(2,1)S(1)}, u32[]{:S(2)}, u32[]{:S(2)}) collective-permute-start(bf16[384,512]{1,0:T(8,128)(2,1)S(1)} %fusion.14), channel_id=1, source_target_pairs={{0,8},{8,0},{1,9},{9,1},{2,10},{10,2},{3,11},{11,3},{4,12},{12,4},... | collective-permute-start | bytes 1179656 | tf_op jit(solution)/shard_map/ppermute | solution.py:56
  150.3 13.3 %collective-permute-start.6 = (bf16[256,512]{1,0:T(8,128)(2,1)}, bf16[256,512]{1,0:T(8,128)(2,1)}, u32[]{:S(2)}, u32[]{:S(2)}) collective-permute-start(bf16[256,512]{1,0:T(8,128)(2,1)} %param.3), channel_id=1, source_target_pairs={{0,16},{16,32},{32,48},{48,64},{64,80},{80,96},{96,112},{112,128},... | collective-permute-start | bytes 786440 | tf_op jit(solution)/shard_map/cond/branch_0_fun/ppermute | solution.py:16
Sparse Core Ops, SparseCore 0:
  17.9 62.7 all-gather.2
  103.0 47.3 reduce-scatter.1

commit v8 on v7

--- a/solution.py
+++ b/solution.py
@@ -36,7 +36,6 @@
     gathered = lax.all_gather(params, "fl", axis=0)
     gathered = lax.all_gather(gathered, "fz", axis=0)
     full_params = gathered.reshape(-1, params.shape[1])
-    peer_numer, peer_weight = to_peer(send_to_peer, (numer, push_weights), power)
     act32 = activations[0].astype(jnp.float32)
     mean_sq = jnp.mean(act32 * act32, axis=1, keepdims=True)
     normed = (act32 * lax.rsqrt(mean_sq + 1e-05) * gain[None, :]).astype(jnp.bfloat16)
@@ -46,7 +45,6 @@
     errors = ((keys - targets[0].astype(jnp.float32)) / math.sqrt(replica_tokens)).astype(
         jnp.bfloat16
     )
-    peer_numer, peer_weight, errors = lax.optimization_barrier((peer_numer, peer_weight, errors))
     side = lax.axis_index("fl")
     flip = [(i, n_pair - 1 - i) for i in range(n_pair)]
     by_block = normed.reshape(tokens, n_ring, n_pair, -1)
@@ -59,6 +57,8 @@
     theirs = lax.dot_general(their_cols, their_errors, contract, preferred_element_type=jnp.float32)
     pair_sum = mine.astype(jnp.bfloat16).astype(jnp.float32) + theirs.astype(jnp.bfloat16).astype(jnp.float32)
     blocks = pair_sum.astype(jnp.bfloat16).reshape(n_ring, -1, pair_sum.shape[1])
+    early, weight, blocks = lax.optimization_barrier((numer, push_weights, blocks))
+    peer_numer, peer_weight = to_peer(send_to_peer, (early, weight), power)
     grad16 = lax.psum_scatter(blocks, "fz", scatter_dimension=0)
     peer_grad16 = to_peer(send_to_peer, grad16, power)
     updated = numer - 0.3 * grad16.astype(jnp.float32)

time: 176 us -> 175 us (level)
  starting transfers between devices: 13.9 us -> 24 us
  waiting for transfers between devices: 107 us -> 97.2 us
    all_gather x1, waiting for transfers between devices: 0.01 us -> 47 us  [body(): gathered = lax.all_gather(gathered, 'fz', axis=0)]
    reduce_scatter x1, waiting for transfers between devices: 46.9 us -> 17.4 us  [body(): grad16 = lax.psum_scatter(blocks, 'fz', scatter_dimension=0)]
    ppermute x3, waiting for transfers between devices: 52.7 us -> 24.8 us  [passed_along(): return lax.ppermute(value, axis, pairs)]
    ppermute x3, starting transfers between devices: 8.43 us -> 17.1 us  [passed_along(): return lax.ppermute(value, axis, pairs)]
  transfers between devices with their start and end apart: 7 -> 7, of which waited for: 4 -> 5; matrix products, arithmetic and copies ran while one was open for 12% -> 12% of each run, Pallas kernels for 0% -> 0%
where the time goes in v8:
time: 175 us; the launch traced here: 174 us
  waiting for transfers between devices  97.2 us (56%)
  starting transfers between devices  24 us (14%)
  between operations  17.2 us (10%)
  matrix products  10.7 us (6%)
  blocking collectives  8.82 us (5%)
  local copies, waits for them, and re-layouts  8.44 us (5%)
  other arithmetic  7.17 us (4%)
    all_gather x1, waiting for transfers between devices, body(): gathered = lax.all_gather(gathered, 'fz', axis=0)  47 us
    ppermute x3, waiting for transfers between devices, passed_along(): return lax.ppermute(value, axis, pairs)  24.8 us
    reduce_scatter x1, waiting for transfers between devices, body(): grad16 = lax.psum_scatter(blocks, 'fz', scatter_dimension=0)  17.4 us
    ppermute x3, starting transfers between devices, passed_along(): return lax.ppermute(value, axis, pairs)  17.1 us
    all_gather x1, blocking collectives, body(): gathered = lax.all_gather(params, 'fl', axis=0)  8.82 us
    ppermute x1, waiting for transfers between devices, body(): their_errors = lax.ppermute(errors, 'fl', flip)  7.91 us
    dot_general x1, matrix products, body(): jnp.dot(normed, full_params, preferred_element_type=jnp.float32)  6.81 us
    convert_element_type x1, local copies, waits for them, and re-layouts, body(): act32 = activations[0].astype(jnp.float32)  5.56 us
  transfers between devices with their start and end apart: 7, of which 5 were waited for; matrix products, arithmetic and copies ran while one was open for 12% of the time, Pallas kernels for 0%

profile of v8, /device:TPU:6, one launch (start us, length us, event | category | flops | bytes accessed | tf_op | source)
XLA Modules:
  0.0 173.6 jit_solution(6856458930763344377)
XLA Ops:
  7.2 0.0 all-gather.3.cloned.1.call-start
  7.9 1.1 divide_convert_fusion
  8.9 8.8 %all_gather.10 = bf16[2,256,512]{2,1,0:T(8,128)(2,1)} all-gather(bf16[1,256,512]{2,1,0:T(8,128)(2,1)S(1)} %divide_convert_fusion), channel_id=1, replica_groups=mesh['replica'=32,'fl'=2,'fz'=8] {'fl'}, dimensions={0}, use_global_device_ids=true | all-gather | bytes 786432 | tf_op jit(solution)/shard_map/all_gather | solution.py:36
  17.8 0.0 all-gather.3.cloned.1.call-update
  17.8 0.0 reduce-scatter.2.cloned.1.call-start
  17.8 0.7 mul.42
  18.6 5.6 %copy.11 = f32[1,384,4096]{1,2,0:T(8,128)} copy(bf16[1,384,4096]{2,1,0:T(8,128)(2,1)} %param.15) | data formatting | bytes 9437184 | tf_op jit(solution)/shard_map/convert_element_type | solution.py:39
  24.1 0.0 copy-done
  24.1 0.7 multiply_reduce_fusion
  24.8 3.2 %multiply_convert_fusion = bf16[384,2,8,256]{0,3,2,1:T(8,128)(2,1)S(1)} fusion(f32[384,2,8,256]{0,3,2,1:T(8,128)} %bitcast.40, f32[2,8,256]{2,1,0:T(8,128)S(1)} %mul.42, f32[384]{0:T(512)S(1)} %add_rsqrt_fusion), kind=kLoop, calls=%fused_computation | loop fusion | flops 4718592 | bytes 9455104 | tf_op jit(solution)/shard_map/convert_element_type | solution.py:41
  28.1 0.0 copy-start.3
  28.1 2.1 %dynamic-slice_bitcast_fusion = (bf16[384,8,256]{0,2,1:T(8,128)(2,1)}, bf16[384,1,8,256]{0,3,2,1:T(8,128)(2,1)}) fusion(bf16[384,2,8,256]{0,3,2,1:T(8,128)(2,1)S(1)} %multiply_convert_fusion, s32[]{:T(128)S(6)} %select_n.8, s32[]{:T(128)S(6)} %select_n.7), kind=kLoop, calls=%fused_computation.7 | loop fusion | bytes 6291464 | tf_op jit(solution)/shard_map/jit(dynamic_index_in_dim)/squeeze | solution.py:52
  30.2 3.5 %collective-permute-start.9 = (bf16[384,8,256]{0,2,1:T(8,128)(2,1)}, bf16[384,8,256]{0,2,1:T(8,128)(2,1)S(1)}, u32[]{:S(2)}, u32[]{:S(2)}) collective-permute-start(bf16[384,8,256]{0,2,1:T(8,128)(2,1)} %get-tuple-element.43), channel_id=1, source_target_pairs={{0,8},{8,0},{1,9},{9,1},{2,10},{10,2},{3,11},{11,3},{4,12},{12,4},... | collective-permute-start | bytes 4718600 | tf_op jit(solution)/shard_map/ppermute | solution.py:53
  33.7 47.0 %all-gather.3.cloned.1.call-done = bf16[16,256,512]{2,1,0:T(8,128)(2,1)} async-done(((bf16[2,256,512]{2,1,0:T(8,128)(2,1)}), bf16[16,256,512]{2,1,0:T(8,128)(2,1)}) %all-gather.3.cloned.1.call-update) | async-done | bytes 4194320 | tf_op jit(solution)/shard_map/all_gather | solution.py:37
  80.7 0.0 copy-done.3
  80.7 6.8 %fusion.14 = bf16[384,512]{1,0:T(8,128)(2,1)S(1)} fusion(bf16[8,2,256,512]{3,2,1,0:T(8,128)(2,1)} %bitcast.43, bf16[1,384,512]{2,1,0:T(8,128)(2,1)S(1)} %copy-done.3, f32[2,8,256]{2,1,0:T(8,128)S(1)} %mul.42, f32[384,2,8,256]{0,3,2,1:T(8,128)} %bitcast.41, f32[384]{0:T(512)S(1)} %add_rsqrt_fusion), kind=kOutput, calls=%fused_computation.12 | convolution fusion | flops 1616314368 | bytes 11290112 | tf_op jit(solution)/shard_map/dot_general | solution.py:44
  87.5 3.4 %collective-permute-start.10 = (bf16[384,512]{1,0:T(8,128)(2,1)S(1)}, bf16[384,512]{1,0:T(8,128)(2,1)S(1)}, u32[]{:S(2)}, u32[]{:S(2)}) collective-permute-start(bf16[384,512]{1,0:T(8,128)(2,1)S(1)} %fusion.14), channel_id=1, source_target_pairs={{0,8},{8,0},{1,9},{9,1},{2,10},{10,2},{3,11},{11,3},{4,12},{12,4},... | collective-permute-start | bytes 1179656 | tf_op jit(solution)/shard_map/ppermute | solution.py:54
  91.0 1.2 convolution_convert_fusion.1
  92.2 0.0 collective-permute-done.9
  92.2 7.9 %collective-permute-done.10 = bf16[384,512]{1,0:T(8,128)(2,1)S(1)} collective-permute-done((bf16[384,512]{1,0:T(8,128)(2,1)S(1)}, bf16[384,512]{1,0:T(8,128)(2,1)S(1)}, u32[]{:S(2)}, u32[]{:S(2)}) %collective-permute-start.10) | collective-permute-done | bytes 393248 | tf_op jit(solution)/shard_map/ppermute | solution.py:54
  100.1 2.7 %add_convert_fusion = bf16[2048,512]{1,0:T(8,128)(2,1)} fusion(bf16[2048,512]{1,0:T(8,128)(2,1)S(1)} %convolution_convert_fusion.1, bf16[384,2048]{0,1:T(8,128)(2,1)S(1)} %bitcast.47, bf16[384,512]{1,0:T(8,128)(2,1)S(1)} %collective-permute-done.10), kind=kOutput, calls=%fused_computation.2 | convolution fusion | flops 810549248 | bytes 6160384 | tf_op jit(solution)/shard_map/dot_general | solution.py:57
  102.8 0.0 reduce-scatter.2.cloned.1.call-update
  103.5 25.5 %conditional.5 = (f32[256,512]{1,0:T(8,128)}, f32[1]{0:T(128)}) conditional(s32[]{:T(128)} %bitcast.13, (f32[256,512]{1,0:T(8,128)S(1)}, f32[1]{0:T(128)}) %tuple.58, (f32[256,512]{1,0:T(8,128)S(1)}, f32[1]{0:T(128)}) %tuple.59, (f32[256,512]{1,0:T(8,128)S(1)}, f32[1]{0:T(128)}) %tuple.60), branch_computations={%region_2.3_spmd, %region_3.4_spmd, %region_4.5_spmd} | conditional | bytes 2097264 | solution.py:25
  103.5 7.4 %collective-permute-start.4 = (f32[256,512]{1,0:T(8,128)S(1)}, f32[256,512]{1,0:T(8,128)}, u32[]{:S(2)}, u32[]{:S(2)}) collective-permute-start(f32[256,512]{1,0:T(8,128)S(1)} %get-tuple-element.29), channel_id=1, source_target_pairs={{0,64},{16,80},{32,96},{48,112},{64,128},{80,144},{96,160},{112,17... | collective-permute-start | bytes 1572872 | tf_op jit(solution)/shard_map/cond/branch_2_fun/ppermute | solution.py:16
  110.9 2.4 %collective-permute-start.5 = (f32[1]{0:T(128)}, f32[1]{0:T(128)}, u32[]{:S(2)}, u32[]{:S(2)}) collective-permute-start(f32[1]{0:T(128)} %get-tuple-element.30), channel_id=1, source_target_pairs={{0,64},{16,80},{32,96},{48,112},{64,128},{80,144},{96,160},{112,17... | collective-permute-start | bytes 20 | tf_op jit(solution)/shard_map/cond/branch_2_fun/ppermute | solution.py:16
  113.3 15.7 %collective-permute-done.5 = f32[1]{0:T(128)} collective-permute-done((f32[1]{0:T(128)}, f32[1]{0:T(128)}, u32[]{:S(2)}, u32[]{:S(2)}) %collective-permute-start.5) | collective-permute-done | bytes 36 | tf_op jit(solution)/shard_map/cond/branch_2_fun/ppermute | solution.py:16
  129.0 0.0 collective-permute-done.4
  129.7 17.4 %reduce-scatter.2.cloned.1.call-done = bf16[1,256,512]{2,1,0:T(8,128)(2,1)} async-done(((bf16[8,256,512]{2,1,0:T(8,128)(2,1)}), bf16[1,256,512]{2,1,0:T(8,128)(2,1)}) %reduce-scatter.2.cloned.1.call-update) | async-done | bytes 262160 | tf_op jit(solution)/shard_map/reduce_scatter | solution.py:62
  147.1 16.5 %conditional.6 = (bf16[256,512]{1,0:T(8,128)(2,1)}) conditional(s32[]{:T(128)} %bitcast.13, bf16[256,512]{1,0:T(8,128)(2,1)} %bitcast.49, bf16[256,512]{1,0:T(8,128)(2,1)} %bitcast.50, bf16[256,512]{1,0:T(8,128)(2,1)} %bitcast.51), branch_computations={%region_5.6_spmd, %region_6.7_spmd, %region_7.8_spmd} | conditional | bytes 1048624
  147.1 7.3 %collective-permute-start.8 = (bf16[256,512]{1,0:T(8,128)(2,1)}, bf16[256,512]{1,0:T(8,128)(2,1)}, u32[]{:S(2)}, u32[]{:S(2)}) collective-permute-start(bf16[256,512]{1,0:T(8,128)(2,1)} %param.5), channel_id=1, source_target_pairs={{0,64},{16,80},{32,96},{48,112},{64,128},{80,144},{96,160},{112,17... | collective-permute-start | bytes 786440 | tf_op jit(solution)/shard_map/cond/branch_2_fun/ppermute | solution.py:16
  154.4 9.1 %collective-permute-done.8 = bf16[256,512]{1,0:T(8,128)(2,1)} collective-permute-done((bf16[256,512]{1,0:T(8,128)(2,1)}, bf16[256,512]{1,0:T(8,128)(2,1)}, u32[]{:S(2)}, u32[]{:S(2)}) %collective-permute-start.8) | collective-permute-done | bytes 262176 | tf_op jit(solution)/shard_map/cond/branch_2_fun/ppermute | solution.py:16
  163.5 2.1 %multiply_bitcast_fusion = f32[1,256,512]{2,1,0:T(8,128)} fusion(f32[256,512]{1,0:T(8,128)} %get-tuple-element.41, bf16[256,512]{1,0:T(8,128)(2,1)} %get-tuple-element.51, bf16[1,256,512]{2,1,0:T(8,128)(2,1)} %reduce-scatter.2.cloned.1.call-done, f32[1,256,512]{2,1,0:T(8,128)S(1)} %copy-done.1), kind=kLoop, calls=%fused_computation.13 | loop fusion | flops 1048576 | bytes 2097152 | tf_op jit(solution)/shard_map/broadcast_in_dim | solution.py:68
  (6 shorter events, 0.0 us)
Async XLA Ops:
  7.2 73.6 %all-gather.3.cloned.1.call-start = ((), (), s32[]{:S(2)}) async-start(), calls=%async_computation.2 | async-start | bytes 4718592 | tf_op jit(solution)/shard_map/all_gather | solution.py:37
  17.8 129.3 %reduce-scatter.2.cloned.1.call-start = ((), (), s32[]{:S(2)}) async-start(), calls=%async_computation.1 | async-start | bytes 2359296 | tf_op jit(solution)/shard_map/reduce_scatter | solution.py:62
  18.6 5.6 %copy-start = (bf16[1,384,4096]{2,1,0:T(8,128)(2,1)S(1)}, bf16[1,384,4096]{2,1,0:T(8,128)(2,1)}, u32[]{:S(2)}) copy-start(bf16[1,384,4096]{2,1,0:T(8,128)(2,1)} %param.15) | copy-start | bytes 9437188
  28.1 52.6 %copy-start.3 = (bf16[1,384,512]{2,1,0:T(8,128)(2,1)S(1)}, bf16[1,384,512]{2,1,0:T(8,128)(2,1)}, u32[]{:S(2)}) copy-start(bf16[1,384,512]{2,1,0:T(8,128)(2,1)} %param.16) | copy-start | bytes 1179652
  30.2 62.0 %collective-permute-start.9 = (bf16[384,8,256]{0,2,1:T(8,128)(2,1)}, bf16[384,8,256]{0,2,1:T(8,128)(2,1)S(1)}, u32[]{:S(2)}, u32[]{:S(2)}) collective-permute-start(bf16[384,8,256]{0,2,1:T(8,128)(2,1)} %get-tuple-element.43), channel_id=1, source_target_pairs={{0,8},{8,0},{1,9},{9,1},{2,10},{10,2},{3,11},{11,3},{4,12},{12,4},... | collective-permute-start | bytes 4718600 | tf_op jit(solution)/shard_map/ppermute | solution.py:53
  80.7 10.2 %copy-start.2 = (bf16[384,1,8,256]{0,3,2,1:T(8,128)(2,1)S(1)}, bf16[384,1,8,256]{0,3,2,1:T(8,128)(2,1)}, u32[]{:S(2)}) copy-start(bf16[384,1,8,256]{0,3,2,1:T(8,128)(2,1)} %get-tuple-element.44) | copy-start | bytes 4718596
  87.5 12.6 %collective-permute-start.10 = (bf16[384,512]{1,0:T(8,128)(2,1)S(1)}, bf16[384,512]{1,0:T(8,128)(2,1)S(1)}, u32[]{:S(2)}, u32[]{:S(2)}) collective-permute-start(bf16[384,512]{1,0:T(8,128)(2,1)S(1)} %fusion.14), channel_id=1, source_target_pairs={{0,8},{8,0},{1,9},{9,1},{2,10},{10,2},{3,11},{11,3},{4,12},{12,4},... | collective-permute-start | bytes 1179656 | tf_op jit(solution)/shard_map/ppermute | solution.py:54
  100.1 3.4 %copy-start.1 = (f32[1,256,512]{2,1,0:T(8,128)S(1)}, f32[1,256,512]{2,1,0:T(8,128)}, u32[]{:S(2)}) copy-start(f32[1,256,512]{2,1,0:T(8,128)} %param.12) | copy-start | bytes 1572868
  103.5 25.5 %collective-permute-start.4 = (f32[256,512]{1,0:T(8,128)S(1)}, f32[256,512]{1,0:T(8,128)}, u32[]{:S(2)}, u32[]{:S(2)}) collective-permute-start(f32[256,512]{1,0:T(8,128)S(1)} %get-tuple-element.29), channel_id=1, source_target_pairs={{0,64},{16,80},{32,96},{48,112},{64,128},{80,144},{96,160},{112,17... | collective-permute-start | bytes 1572872 | tf_op jit(solution)/shard_map/cond/branch_2_fun/ppermute | solution.py:16
  110.9 18.1 %collective-permute-start.5 = (f32[1]{0:T(128)}, f32[1]{0:T(128)}, u32[]{:S(2)}, u32[]{:S(2)}) collective-permute-start(f32[1]{0:T(128)} %get-tuple-element.30), channel_id=1, source_target_pairs={{0,64},{16,80},{32,96},{48,112},{64,128},{80,144},{96,160},{112,17... | collective-permute-start | bytes 20 | tf_op jit(solution)/shard_map/cond/branch_2_fun/ppermute | solution.py:16
  147.1 16.5 %collective-permute-start.8 = (bf16[256,512]{1,0:T(8,128)(2,1)}, bf16[256,512]{1,0:T(8,128)(2,1)}, u32[]{:S(2)}, u32[]{:S(2)}) collective-permute-start(bf16[256,512]{1,0:T(8,128)(2,1)} %param.5), channel_id=1, source_target_pairs={{0,64},{16,80},{32,96},{48,112},{64,128},{80,144},{96,160},{112,17... | collective-permute-start | bytes 786440 | tf_op jit(solution)/shard_map/cond/branch_2_fun/ppermute | solution.py:16
Sparse Core Ops, SparseCore 0:
  17.9 62.7 all-gather.2
  103.0 44.0 reduce-scatter.1

commit v9 on v8

--- a/solution.py
+++ b/solution.py
@@ -34,23 +34,22 @@
     replica_tokens = activations.shape[1] * n_pair * n_ring
     params = (numer / push_weights[0]).astype(jnp.bfloat16)
     gathered = lax.all_gather(params, "fl", axis=0)
-    gathered = lax.all_gather(gathered, "fz", axis=0)
+    gathered = lax.all_gather(gathered, "fz", axis=1)
     full_params = gathered.reshape(-1, params.shape[1])
     act32 = activations[0].astype(jnp.float32)
     mean_sq = jnp.mean(act32 * act32, axis=1, keepdims=True)
     normed = (act32 * lax.rsqrt(mean_sq + 1e-05) * gain[None, :]).astype(jnp.bfloat16)
     tokens = normed.shape[0]
-    normed = normed.reshape(tokens, n_pair, n_ring, -1).transpose(0, 2, 1, 3).reshape(tokens, -1)
     keys = jnp.dot(normed, full_params, preferred_element_type=jnp.float32) / math.sqrt(features)
     errors = ((keys - targets[0].astype(jnp.float32)) / math.sqrt(replica_tokens)).astype(
         jnp.bfloat16
     )
     side = lax.axis_index("fl")
     flip = [(i, n_pair - 1 - i) for i in range(n_pair)]
-    by_block = normed.reshape(tokens, n_ring, n_pair, -1)
-    own_cols = lax.dynamic_index_in_dim(by_block, side, 2, keepdims=False).reshape(tokens, -1)
-    partner_cols = lax.dynamic_index_in_dim(by_block, n_pair - 1 - side, 2, keepdims=False)
-    their_cols = lax.ppermute(partner_cols, "fl", flip).reshape(tokens, -1)
+    row_width = features // n_pair
+    own_cols = lax.dynamic_slice_in_dim(normed, side * row_width, row_width, axis=1)
+    partner_cols = lax.dynamic_slice_in_dim(normed, (n_pair - 1 - side) * row_width, row_width, axis=1)
+    their_cols = lax.ppermute(partner_cols, "fl", flip)
     their_errors = lax.ppermute(errors, "fl", flip)
     contract = (((0,), (0,)), ((), ()))
     mine = lax.dot_general(own_cols, errors, contract, preferred_element_type=jnp.float32)

time: 175 us -> 173 us (0.989)
  waiting for transfers between devices: 97.2 us -> 103 us
  local copies, waits for them, and re-layouts: 8.44 us -> 2.95 us
  starting transfers between devices: 24 us -> 21.1 us
    all_gather x1, waiting for transfers between devices: 47 us -> 52.8 us  [body(): gathered = lax.all_gather(gathered, 'fz', axis=1)]
    convert_element_type x1 -> x0, local copies, waits for them, and re-layouts: 5.56 us -> none  [body(): act32 = activations[0].astype(jnp.float32)]
    ppermute x3, starting transfers between devices: 17.1 us -> 14.2 us  [passed_along(): return lax.ppermute(value, axis, pairs)]
    convert_element_type x1, other arithmetic: 3.24 us -> 1 us  [body(): (act32 * lax.rsqrt(mean_sq + 1e-05) * gain[None, :]).astype(jnp.bfloat16)]
    squeeze x1 -> x0, local copies, waits for them, and re-layouts: 2.14 us -> none  [body(): lax.dynamic_index_in_dim(by_block, n_pair - 1 - side, 2, keepdims=False)]
    dot_general x1, matrix products: 6.81 us -> 4.85 us  [body(): jnp.dot(normed, full_params, preferred_element_type=jnp.float32)]
    reduce_sum x1, other arithmetic: 0.69 us -> 2.58 us  [body(): mean_sq = jnp.mean(act32 * act32, axis=1, keepdims=True)]
  transfers between devices with their start and end apart: 7 -> 7, of which waited for: 5 -> 5; matrix products, arithmetic and copies ran while one was open for 12% -> 7% of each run, Pallas kernels for 0% -> 0%
where the time goes in v9:
time: 173 us; the launch traced here: 172 us
  waiting for transfers between devices  103 us (60%)
  starting transfers between devices  21.1 us (12%)
  between operations  17.4 us (10%)
  matrix products  11.7 us (7%)
  blocking collectives  8.82 us (5%)
  other arithmetic  6.93 us (4%)
  local copies, waits for them, and re-layouts  2.95 us (2%)
    all_gather x1, waiting for transfers between devices, body(): gathered = lax.all_gather(gathered, 'fz', axis=1)  52.8 us
    ppermute x3, waiting for transfers between devices, passed_along(): return lax.ppermute(value, axis, pairs)  26 us
    reduce_scatter x1, waiting for transfers between devices, body(): grad16 = lax.psum_scatter(blocks, 'fz', scatter_dimension=0)  17.6 us
    ppermute x3, starting transfers between devices, passed_along(): return lax.ppermute(value, axis, pairs)  14.2 us
    all_gather x1, blocking collectives, body(): gathered = lax.all_gather(params, 'fl', axis=0)  8.82 us
    ppermute x1, waiting for transfers between devices, body(): their_errors = lax.ppermute(errors, 'fl', flip)  6.59 us
    dot_general x1, matrix products, body(): jnp.dot(normed, full_params, preferred_element_type=jnp.float32)  4.85 us
    dot_general x1, matrix products, body(): lax.dot_general(their_cols, their_errors, contract, preferred_element_typ...  4.07 us
  transfers between devices with their start and end apart: 7, of which 5 were waited for; matrix products, arithmetic and copies ran while one was open for 7% of the time, Pallas kernels for 0%

profile of v9, /device:TPU:6, one launch (start us, length us, event | category | flops | bytes accessed | tf_op | source)
XLA Modules:
  0.0 172.1 jit_solution(14405225356768264064)
XLA Ops:
  7.2 0.0 copy-start
  7.2 0.0 all-gather.3.cloned.1.call-start
  8.0 1.2 divide_convert_fusion
  9.2 8.8 %all_gather.10 = bf16[2,256,512]{2,1,0:T(8,128)(2,1)} all-gather(bf16[1,256,512]{2,1,0:T(8,128)(2,1)S(1)} %divide_convert_fusion), channel_id=1, replica_groups=mesh['replica'=32,'fl'=2,'fz'=8] {'fl'}, dimensions={0}, use_global_device_ids=true | all-gather | bytes 786432 | tf_op jit(solution)/shard_map/all_gather | solution.py:36
  18.0 0.0 all-gather.3.cloned.1.call-update
  18.1 0.0 reduce-scatter.2.cloned.1.call-start
  18.1 2.6 %fusion.2 = f32[384]{0:T(512)S(1)} fusion(bf16[1,384,4096]{2,1,0:T(8,128)(2,1)} %param.15), kind=kLoop, calls=%fused_computation.4 | loop fusion | flops 4718208 | bytes 3147264 | tf_op jit(solution)/shard_map/reduce_sum | solution.py:40
  20.7 0.0 copy-done.3
  20.7 1.0 fusion.4
  21.8 1.7 copy-done.1
  23.4 1.3 constant_dynamic-slice_fusion
  24.7 3.5 %collective-permute-start.9 = (bf16[384,2048]{1,0:T(8,128)(2,1)}, bf16[384,2048]{1,0:T(8,128)(2,1)}, u32[]{:S(2)}, u32[]{:S(2)}) collective-permute-start(bf16[384,2048]{1,0:T(8,128)(2,1)} %constant_dynamic-slice_fusion), channel_id=1, source_target_pairs={{0,8},{8,0},{1,9},{9,1},{2,10},{10,2},{3,11},{11,3},{4,12},{12,4},... | collective-permute-start | bytes 4718600 | tf_op jit(solution)/shard_map/ppermute | solution.py:52
  28.2 52.8 %all-gather.3.cloned.1.call-done = bf16[2,2048,512]{2,1,0:T(8,128)(2,1)} async-done(((bf16[2,256,512]{2,1,0:T(8,128)(2,1)}), bf16[2,2048,512]{2,1,0:T(8,128)(2,1)}) %all-gather.3.cloned.1.call-update) | async-done | bytes 4194320 | tf_op jit(solution)/shard_map/all_gather | solution.py:37
  81.0 4.8 %fusion.22 = bf16[384,512]{1,0:T(8,128)(2,1)} fusion(bf16[4096,512]{1,0:T(8,128)(2,1)} %bitcast.48, bf16[1,384,4096]{2,1,0:T(8,128)(2,1)S(1)} %copy-done, f32[4096]{0:T(1024)S(1)} %copy-done.3, f32[384]{0:T(512)S(1)} %add_rsqrt_fusion, bf16[1,384,512]{2,1,0:T(8,128)(2,1)} %param.16), kind=kOutput, calls=%fused_computation.20 | convolution fusion | flops 1617887232 | bytes 8144384 | tf_op jit(solution)/shard_map/dot_general | solution.py:43
  85.9 3.4 %collective-permute-start.10 = (bf16[384,512]{1,0:T(8,128)(2,1)}, bf16[384,512]{1,0:T(8,128)(2,1)S(1)}, u32[]{:S(2)}, u32[]{:S(2)}) collective-permute-start(bf16[384,512]{1,0:T(8,128)(2,1)} %fusion.22), channel_id=1, source_target_pairs={{0,8},{8,0},{1,9},{9,1},{2,10},{10,2},{3,11},{11,3},{4,12},{12,4},... | collective-permute-start | bytes 1179656 | tf_op jit(solution)/shard_map/ppermute | solution.py:53
  89.3 2.8 %convolution_convert_fusion.1 = bf16[2048,512]{1,0:T(8,128)(2,1)S(1)} fusion(bf16[384,512]{1,0:T(8,128)(2,1)} %fusion.22, bf16[384,4096]{1,0:T(8,128)(2,1)} %copy-done.1, s32[]{:T(128)S(6)} %select_n.6), kind=kOutput, calls=%fused_computation.15 | convolution fusion | flops 806354944 | bytes 4063236 | tf_op jit(solution)/shard_map/dot_general | solution.py:55
  92.0 0.0 copy-start.2
  92.0 0.0 collective-permute-done.9
  92.1 6.6 %collective-permute-done.10 = bf16[384,512]{1,0:T(8,128)(2,1)S(1)} collective-permute-done((bf16[384,512]{1,0:T(8,128)(2,1)}, bf16[384,512]{1,0:T(8,128)(2,1)S(1)}, u32[]{:S(2)}, u32[]{:S(2)}) %collective-permute-start.10) | collective-permute-done | bytes 393248 | tf_op jit(solution)/shard_map/ppermute | solution.py:53
  98.6 4.1 %add_convert_fusion = bf16[2048,512]{1,0:T(8,128)(2,1)} fusion(bf16[2048,512]{1,0:T(8,128)(2,1)S(1)} %convolution_convert_fusion.1, bf16[384,2048]{1,0:T(8,128)(2,1)} %collective-permute-done.9, bf16[384,512]{1,0:T(8,128)(2,1)S(1)} %collective-permute-done.10), kind=kOutput, calls=%fused_computation.9 | convolution fusion | flops 810549248 | bytes 6160384 | tf_op jit(solution)/shard_map/dot_general | solution.py:56
  102.7 0.0 reduce-scatter.2.cloned.1.call-update
  103.4 0.0 copy-done.2
  103.4 25.1 %conditional.5 = (f32[256,512]{1,0:T(8,128)}, f32[1]{0:T(128)}) conditional(s32[]{:T(128)} %bitcast.8, (f32[256,512]{1,0:T(8,128)S(1)}, f32[1]{0:T(128)}) %tuple.57, (f32[256,512]{1,0:T(8,128)S(1)}, f32[1]{0:T(128)}) %tuple.58, (f32[256,512]{1,0:T(8,128)S(1)}, f32[1]{0:T(128)}) %tuple.59), branch_computations={%region_2.0_spmd, %region_3.0_spmd, %region_4.0_spmd} | conditional | bytes 2097264 | solution.py:25
  103.4 4.3 %collective-permute-start.2 = (f32[256,512]{1,0:T(8,128)S(1)}, f32[256,512]{1,0:T(8,128)}, u32[]{:S(2)}, u32[]{:S(2)}) collective-permute-start(f32[256,512]{1,0:T(8,128)S(1)} %get-tuple-element.27), channel_id=1, source_target_pairs={{0,32},{16,48},{32,64},{48,80},{64,96},{80,112},{96,128},{112,144}... | collective-permute-start | bytes 1572872 | tf_op jit(solution)/shard_map/cond/branch_1_fun/ppermute | solution.py:16
  107.7 5.5 %collective-permute-start.3 = (f32[1]{0:T(128)}, f32[1]{0:T(128)}, u32[]{:S(2)}, u32[]{:S(2)}) collective-permute-start(f32[1]{0:T(128)} %get-tuple-element.28), channel_id=1, source_target_pairs={{0,32},{16,48},{32,64},{48,80},{64,96},{80,112},{96,128},{112,144}... | collective-permute-start | bytes 20 | tf_op jit(solution)/shard_map/cond/branch_1_fun/ppermute | solution.py:16
  113.3 15.3 %collective-permute-done.3 = f32[1]{0:T(128)} collective-permute-done((f32[1]{0:T(128)}, f32[1]{0:T(128)}, u32[]{:S(2)}, u32[]{:S(2)}) %collective-permute-start.3) | collective-permute-done | bytes 36 | tf_op jit(solution)/shard_map/cond/branch_1_fun/ppermute | solution.py:16
  128.5 0.0 collective-permute-done.2
  129.2 17.6 %reduce-scatter.2.cloned.1.call-done = bf16[1,256,512]{2,1,0:T(8,128)(2,1)} async-done(((bf16[8,256,512]{2,1,0:T(8,128)(2,1)}), bf16[1,256,512]{2,1,0:T(8,128)(2,1)}) %reduce-scatter.2.cloned.1.call-update) | async-done | bytes 262160 | tf_op jit(solution)/shard_map/reduce_scatter | solution.py:61
  146.9 15.1 %conditional.6 = (bf16[256,512]{1,0:T(8,128)(2,1)}) conditional(s32[]{:T(128)} %bitcast.8, bf16[256,512]{1,0:T(8,128)(2,1)} %bitcast.45, bf16[256,512]{1,0:T(8,128)(2,1)} %bitcast.46, bf16[256,512]{1,0:T(8,128)(2,1)} %bitcast.47), branch_computations={%region_5.0_spmd, %region_6.0_spmd, %region_7.0_spmd} | conditional | bytes 1048624
  146.9 4.4 %collective-permute-start.7 = (bf16[256,512]{1,0:T(8,128)(2,1)}, bf16[256,512]{1,0:T(8,128)(2,1)}, u32[]{:S(2)}, u32[]{:S(2)}) collective-permute-start(bf16[256,512]{1,0:T(8,128)(2,1)} %param.4), channel_id=1, source_target_pairs={{0,32},{16,48},{32,64},{48,80},{64,96},{80,112},{96,128},{112,144}... | collective-permute-start | bytes 786440 | tf_op jit(solution)/shard_map/cond/branch_1_fun/ppermute | solution.py:16
  151.2 10.7 %collective-permute-done.7 = bf16[256,512]{1,0:T(8,128)(2,1)} collective-permute-done((bf16[256,512]{1,0:T(8,128)(2,1)}, bf16[256,512]{1,0:T(8,128)(2,1)}, u32[]{:S(2)}, u32[]{:S(2)}) %collective-permute-start.7) | collective-permute-done | bytes 262176 | tf_op jit(solution)/shard_map/cond/branch_1_fun/ppermute | solution.py:16
  162.0 2.1 %multiply_bitcast_fusion = f32[1,256,512]{2,1,0:T(8,128)} fusion(f32[256,512]{1,0:T(8,128)} %get-tuple-element.41, bf16[256,512]{1,0:T(8,128)(2,1)} %get-tuple-element.49, bf16[1,256,512]{2,1,0:T(8,128)(2,1)} %reduce-scatter.2.cloned.1.call-done, f32[1,256,512]{2,1,0:T(8,128)S(1)} %copy-done.2), kind=kLoop, calls=%fused_computation.21 | loop fusion | flops 1048576 | bytes 2097152 | tf_op jit(solution)/shard_map/broadcast_in_dim | solution.py:67
  (4 shorter events, 0.0 us)
Async XLA Ops:
  7.2 13.6 %copy-start = (bf16[1,384,4096]{2,1,0:T(8,128)(2,1)S(1)}, bf16[1,384,4096]{2,1,0:T(8,128)(2,1)}, u32[]{:S(2)}) copy-start(bf16[1,384,4096]{2,1,0:T(8,128)(2,1)} %param.15) | copy-start | bytes 9437188
  7.2 13.6 %copy-start.3 = (f32[4096]{0:T(1024)S(1)}, f32[4096]{0:T(1024)}, u32[]{:S(2)}) copy-start(f32[4096]{0:T(1024)} %param.17) | copy-start | bytes 49156
  7.2 73.8 %all-gather.3.cloned.1.call-start = ((), (), s32[]{:S(2)}) async-start(), calls=%async_computation.2 | async-start | bytes 4718592 | tf_op jit(solution)/shard_map/all_gather | solution.py:37
  18.1 128.8 %reduce-scatter.2.cloned.1.call-start = ((), (), s32[]{:S(2)}) async-start(), calls=%async_computation.1 | async-start | bytes 2359296 | tf_op jit(solution)/shard_map/reduce_scatter | solution.py:61
  21.7 1.7 copy-start.1
  24.7 67.4 %collective-permute-start.9 = (bf16[384,2048]{1,0:T(8,128)(2,1)}, bf16[384,2048]{1,0:T(8,128)(2,1)}, u32[]{:S(2)}, u32[]{:S(2)}) collective-permute-start(bf16[384,2048]{1,0:T(8,128)(2,1)} %constant_dynamic-slice_fusion), channel_id=1, source_target_pairs={{0,8},{8,0},{1,9},{9,1},{2,10},{10,2},{3,11},{11,3},{4,12},{12,4},... | collective-permute-start | bytes 4718600 | tf_op jit(solution)/shard_map/ppermute | solution.py:52
  85.9 12.8 %collective-permute-start.10 = (bf16[384,512]{1,0:T(8,128)(2,1)}, bf16[384,512]{1,0:T(8,128)(2,1)S(1)}, u32[]{:S(2)}, u32[]{:S(2)}) collective-permute-start(bf16[384,512]{1,0:T(8,128)(2,1)} %fusion.22), channel_id=1, source_target_pairs={{0,8},{8,0},{1,9},{9,1},{2,10},{10,2},{3,11},{11,3},{4,12},{12,4},... | collective-permute-start | bytes 1179656 | tf_op jit(solution)/shard_map/ppermute | solution.py:53
  92.0 11.4 %copy-start.2 = (f32[1,256,512]{2,1,0:T(8,128)S(1)}, f32[1,256,512]{2,1,0:T(8,128)}, u32[]{:S(2)}) copy-start(f32[1,256,512]{2,1,0:T(8,128)} %param.12) | copy-start | bytes 1572868
  103.4 25.1 %collective-permute-start.2 = (f32[256,512]{1,0:T(8,128)S(1)}, f32[256,512]{1,0:T(8,128)}, u32[]{:S(2)}, u32[]{:S(2)}) collective-permute-start(f32[256,512]{1,0:T(8,128)S(1)} %get-tuple-element.27), channel_id=1, source_target_pairs={{0,32},{16,48},{32,64},{48,80},{64,96},{80,112},{96,128},{112,144}... | collective-permute-start | bytes 1572872 | tf_op jit(solution)/shard_map/cond/branch_1_fun/ppermute | solution.py:16
  107.7 20.8 %collective-permute-start.3 = (f32[1]{0:T(128)}, f32[1]{0:T(128)}, u32[]{:S(2)}, u32[]{:S(2)}) collective-permute-start(f32[1]{0:T(128)} %get-tuple-element.28), channel_id=1, source_target_pairs={{0,32},{16,48},{32,64},{48,80},{64,96},{80,112},{96,128},{112,144}... | collective-permute-start | bytes 20 | tf_op jit(solution)/shard_map/cond/branch_1_fun/ppermute | solution.py:16
  146.9 15.1 %collective-permute-start.7 = (bf16[256,512]{1,0:T(8,128)(2,1)}, bf16[256,512]{1,0:T(8,128)(2,1)}, u32[]{:S(2)}, u32[]{:S(2)}) collective-permute-start(bf16[256,512]{1,0:T(8,128)(2,1)} %param.4), channel_id=1, source_target_pairs={{0,32},{16,48},{32,64},{48,80},{64,96},{80,112},{96,128},{112,144}... | collective-permute-start | bytes 786440 | tf_op jit(solution)/shard_map/cond/branch_1_fun/ppermute | solution.py:16
Sparse Core Ops, SparseCore 0:
  18.2 62.7 all-gather.2
  102.9 43.9 reduce-scatter.1

commit v10 on v9

--- a/solution.py
+++ b/solution.py
@@ -40,20 +40,28 @@
     mean_sq = jnp.mean(act32 * act32, axis=1, keepdims=True)
     normed = (act32 * lax.rsqrt(mean_sq + 1e-05) * gain[None, :]).astype(jnp.bfloat16)
     tokens = normed.shape[0]
-    keys = jnp.dot(normed, full_params, preferred_element_type=jnp.float32) / math.sqrt(features)
-    errors = ((keys - targets[0].astype(jnp.float32)) / math.sqrt(replica_tokens)).astype(
-        jnp.bfloat16
-    )
     side = lax.axis_index("fl")
     flip = [(i, n_pair - 1 - i) for i in range(n_pair)]
     row_width = features // n_pair
     own_cols = lax.dynamic_slice_in_dim(normed, side * row_width, row_width, axis=1)
     partner_cols = lax.dynamic_slice_in_dim(normed, (n_pair - 1 - side) * row_width, row_width, axis=1)
     their_cols = lax.ppermute(partner_cols, "fl", flip)
-    their_errors = lax.ppermute(errors, "fl", flip)
     contract = (((0,), (0,)), ((), ()))
-    mine = lax.dot_general(own_cols, errors, contract, preferred_element_type=jnp.float32)
-    theirs = lax.dot_general(their_cols, their_errors, contract, preferred_element_type=jnp.float32)
+    half = tokens // 2
+    mine = theirs = None
+    for part in range(2):
+        span = slice(part * half, (part + 1) * half)
+        keys = jnp.dot(normed[span], full_params, preferred_element_type=jnp.float32) / math.sqrt(features)
+        errors = ((keys - targets[0, span].astype(jnp.float32)) / math.sqrt(replica_tokens)).astype(
+            jnp.bfloat16
+        )
+        their_errors = lax.ppermute(errors, "fl", flip)
+        term = lax.dot_general(own_cols[span], errors, contract, preferred_element_type=jnp.float32)
+        their_term = lax.dot_general(
+            their_cols[span], their_errors, contract, preferred_element_type=jnp.float32
+        )
+        mine = term if mine is None else mine + term
+        theirs = their_term if theirs is None else theirs + their_term
     pair_sum = mine.astype(jnp.bfloat16).astype(jnp.float32) + theirs.astype(jnp.bfloat16).astype(jnp.float32)
     blocks = pair_sum.astype(jnp.bfloat16).reshape(n_ring, -1, pair_sum.shape[1])
     early, weight, blocks = lax.optimization_barrier((numer, push_weights, blocks))

time: 173 us -> 173 us (level)
  waiting for transfers between devices: 103 us -> 96.6 us
  starting transfers between devices: 21.1 us -> 26.6 us
    ppermute x1 -> x2, waiting for transfers between devices: 6.59 us -> 3.26 us  [body(): their_errors = lax.ppermute(errors, 'fl', flip)]
    reduce_scatter x1, waiting for transfers between devices: 17.6 us -> 14.5 us  [body(): grad16 = lax.psum_scatter(blocks, 'fz', scatter_dimension=0)]
    ppermute x3, starting transfers between devices: 14.2 us -> 17.2 us  [passed_along(): return lax.ppermute(value, axis, pairs)]
    ppermute x1 -> x2, starting transfers between devices: 3.39 us -> 5.84 us  [body(): their_errors = lax.ppermute(errors, 'fl', flip)]
    dot_general x3 -> x6, matrix products: 11.7 us -> 11.4 us  [the longest x2 6.97 us: body(): jnp.dot(normed[span], full_params, preferred_element_type=jnp.float32)]
  transfers between devices with their start and end apart: 7 -> 8, of which waited for: 5 -> 5; matrix products, arithmetic and copies ran while one was open for 7% -> 8% of each run, Pallas kernels for 0% -> 0%
where the time goes in v10:
time: 173 us; the launch traced here: 171 us
  waiting for transfers between devices  96.6 us (56%)
  starting transfers between devices  26.6 us (15%)
  between operations  17.3 us (10%)
  matrix products  11.4 us (7%)
  blocking collectives  8.82 us (5%)
  other arithmetic  6.93 us (4%)
  local copies, waits for them, and re-layouts  3.03 us (2%)
    all_gather x1, waiting for transfers between devices, body(): gathered = lax.all_gather(gathered, 'fz', axis=1)  52.8 us
    ppermute x3, waiting for transfers between devices, passed_along(): return lax.ppermute(value, axis, pairs)  26 us
    ppermute x3, starting transfers between devices, passed_along(): return lax.ppermute(value, axis, pairs)  17.2 us
    reduce_scatter x1, waiting for transfers between devices, body(): grad16 = lax.psum_scatter(blocks, 'fz', scatter_dimension=0)  14.5 us
    all_gather x1, blocking collectives, body(): gathered = lax.all_gather(params, 'fl', axis=0)  8.82 us
    dot_general x2, matrix products, body(): jnp.dot(normed[span], full_params, preferred_element_type=jnp.float32)  6.97 us
    ppermute x2, starting transfers between devices, body(): their_errors = lax.ppermute(errors, 'fl', flip)  5.84 us
    ppermute x1, starting transfers between devices, body(): their_cols = lax.ppermute(partner_cols, 'fl', flip)  3.47 us
  transfers between devices with their start and end apart: 8, of which 5 were waited for; matrix products, arithmetic and copies ran while one was open for 8% of the time, Pallas kernels for 0%

profile of v10, /device:TPU:6, one launch (start us, length us, event | category | flops | bytes accessed | tf_op | source)
XLA Modules:
  0.0 170.8 jit_solution(11363790467298834916)
XLA Ops:
  7.2 0.0 copy-start
  7.2 0.0 all-gather.3.cloned.1.call-start
  8.0 1.2 divide_convert_fusion
  9.2 8.8 %all_gather.10 = bf16[2,256,512]{2,1,0:T(8,128)(2,1)} all-gather(bf16[1,256,512]{2,1,0:T(8,128)(2,1)S(1)} %divide_convert_fusion), channel_id=1, replica_groups=mesh['replica'=32,'fl'=2,'fz'=8] {'fl'}, dimensions={0}, use_global_device_ids=true | all-gather | bytes 786432 | tf_op jit(solution)/shard_map/all_gather | solution.py:36
  18.0 0.0 all-gather.3.cloned.1.call-update
  18.1 0.0 reduce-scatter.2.cloned.1.call-start
  18.1 2.6 %fusion = f32[384]{0:T(512)S(1)} fusion(bf16[1,384,4096]{2,1,0:T(8,128)(2,1)} %param.15), kind=kLoop, calls=%fused_computation.2 | loop fusion | flops 4718208 | bytes 3147264 | tf_op jit(solution)/shard_map/reduce_sum | solution.py:40
  20.7 1.0 fusion.2
  21.8 1.7 copy-done.1
  23.4 1.3 constant_dynamic-slice_fusion
  24.8 3.5 %collective-permute-start.9 = (bf16[384,2048]{1,0:T(8,128)(2,1)}, bf16[384,2048]{1,0:T(8,128)(2,1)S(1)}, u32[]{:S(2)}, u32[]{:S(2)}) collective-permute-start(bf16[384,2048]{1,0:T(8,128)(2,1)} %constant_dynamic-slice_fusion), channel_id=1, source_target_pairs={{0,8},{8,0},{1,9},{9,1},{2,10},{10,2},{3,11},{11,3},{4,12},{12,4},... | collective-permute-start | bytes 4718600 | tf_op jit(solution)/shard_map/ppermute | solution.py:48
  28.2 52.8 %all-gather.3.cloned.1.call-done = bf16[2,2048,512]{2,1,0:T(8,128)(2,1)} async-done(((bf16[2,256,512]{2,1,0:T(8,128)(2,1)}), bf16[2,2048,512]{2,1,0:T(8,128)(2,1)}) %all-gather.3.cloned.1.call-update) | async-done | bytes 4194320 | tf_op jit(solution)/shard_map/all_gather | solution.py:37
  81.0 3.8 %fusion.28 = bf16[192,512]{1,0:T(8,128)(2,1)S(1)} fusion(bf16[4096,512]{1,0:T(8,128)(2,1)} %bitcast.34, bf16[384,4096]{1,0:T(8,128)(2,1)} %copy-done.1, bf16[1,384,512]{2,1,0:T(8,128)(2,1)S(1)} %copy-done.5), kind=kOutput, calls=%fused_computation.19 | convolution fusion | flops 805797888 | bytes 6160384 | tf_op jit(solution)/shard_map/dot_general | solution.py:54
  84.8 3.4 %collective-permute-start.11 = (bf16[192,512]{1,0:T(8,128)(2,1)S(1)}, bf16[192,512]{1,0:T(8,128)(2,1)S(1)}, u32[]{:S(2)}, u32[]{:S(2)}) collective-permute-start(bf16[192,512]{1,0:T(8,128)(2,1)S(1)} %fusion.28), channel_id=1, source_target_pairs={{0,8},{8,0},{1,9},{9,1},{2,10},{10,2},{3,11},{11,3},{4,12},{12,4},... | collective-permute-start | bytes 589832 | tf_op jit(solution)/shard_map/ppermute | solution.py:58
  88.2 3.2 %fusion.25 = bf16[192,512]{1,0:T(8,128)(2,1)S(1)} fusion(bf16[4096,512]{1,0:T(8,128)(2,1)} %bitcast.35, bf16[384,4096]{1,0:T(8,128)(2,1)S(1)} %copy-done.2, bf16[1,384,512]{2,1,0:T(8,128)(2,1)S(1)} %copy-done.5), kind=kOutput, calls=%fused_computation.18 | convolution fusion | flops 805797888 | bytes 6160384 | tf_op jit(solution)/shard_map/dot_general | solution.py:54
  91.4 2.4 %collective-permute-start.10 = (bf16[192,512]{1,0:T(8,128)(2,1)S(1)}, bf16[192,512]{1,0:T(8,128)(2,1)S(1)}, u32[]{:S(2)}, u32[]{:S(2)}) collective-permute-start(bf16[192,512]{1,0:T(8,128)(2,1)S(1)} %fusion.25), channel_id=1, source_target_pairs={{0,8},{8,0},{1,9},{9,1},{2,10},{10,2},{3,11},{11,3},{4,12},{12,4},... | collective-permute-start | bytes 589832 | tf_op jit(solution)/shard_map/ppermute | solution.py:58
  93.9 0.8 fusion.35
  94.6 0.8 add_convert_fusion.2
  95.5 0.8 fusion.31
  96.2 0.0 copy-start.3
  96.2 3.3 %collective-permute-done.10 = bf16[192,512]{1,0:T(8,128)(2,1)S(1)} collective-permute-done((bf16[192,512]{1,0:T(8,128)(2,1)S(1)}, bf16[192,512]{1,0:T(8,128)(2,1)S(1)}, u32[]{:S(2)}, u32[]{:S(2)}) %collective-permute-start.10) | collective-permute-done | bytes 196640 | tf_op jit(solution)/shard_map/ppermute | solution.py:58
  99.5 2.1 %add_convert_fusion = bf16[2048,512]{1,0:T(8,128)(2,1)} fusion(bf16[2048,512]{1,0:T(8,128)(2,1)S(1)} %add_convert_fusion.2, f32[2048,512]{1,0:T(8,128)S(1)} %fusion.31, bf16[192,512]{1,0:T(8,128)(2,1)S(1)} %collective-permute-done.10, bf16[384,2048]{1,0:T(8,128)(2,1)S(1)} %collective-permute-done.9), kind=kOutput, calls=%fused_computation.5 | convolution fusion | flops 408944640 | bytes 9371648 | tf_op jit(solution)/shard_map/dot_general | solution.py:60
  101.6 0.0 reduce-scatter.2.cloned.1.call-update
  102.3 27.5 %conditional.5 = (f32[256,512]{1,0:T(8,128)}, f32[1]{0:T(128)}) conditional(s32[]{:T(128)} %bitcast.9, (f32[256,512]{1,0:T(8,128)S(1)}, f32[1]{0:T(128)}) %tuple.57, (f32[256,512]{1,0:T(8,128)S(1)}, f32[1]{0:T(128)}) %tuple.58, (f32[256,512]{1,0:T(8,128)S(1)}, f32[1]{0:T(128)}) %tuple.59), branch_computations={%region_2.0_spmd, %region_3.0_spmd, %region_4.0_spmd} | conditional | bytes 2097264 | solution.py:25
  102.3 6.5 %collective-permute-start.4 = (f32[256,512]{1,0:T(8,128)S(1)}, f32[256,512]{1,0:T(8,128)}, u32[]{:S(2)}, u32[]{:S(2)}) collective-permute-start(f32[256,512]{1,0:T(8,128)S(1)} %get-tuple-element.29), channel_id=1, source_target_pairs={{0,64},{16,80},{32,96},{48,112},{64,128},{80,144},{96,160},{112,17... | collective-permute-start | bytes 1572872 | tf_op jit(solution)/shard_map/cond/branch_2_fun/ppermute | solution.py:16
  108.8 3.3 %collective-permute-start.5 = (f32[1]{0:T(128)}, f32[1]{0:T(128)}, u32[]{:S(2)}, u32[]{:S(2)}) collective-permute-start(f32[1]{0:T(128)} %get-tuple-element.30), channel_id=1, source_target_pairs={{0,64},{16,80},{32,96},{48,112},{64,128},{80,144},{96,160},{112,17... | collective-permute-start | bytes 20 | tf_op jit(solution)/shard_map/cond/branch_2_fun/ppermute | solution.py:16
  112.1 17.7 %collective-permute-done.5 = f32[1]{0:T(128)} collective-permute-done((f32[1]{0:T(128)}, f32[1]{0:T(128)}, u32[]{:S(2)}, u32[]{:S(2)}) %collective-permute-start.5) | collective-permute-done | bytes 36 | tf_op jit(solution)/shard_map/cond/branch_2_fun/ppermute | solution.py:16
  130.3 14.5 %reduce-scatter.2.cloned.1.call-done = bf16[1,256,512]{2,1,0:T(8,128)(2,1)} async-done(((bf16[8,256,512]{2,1,0:T(8,128)(2,1)}), bf16[1,256,512]{2,1,0:T(8,128)(2,1)}) %reduce-scatter.2.cloned.1.call-update) | async-done | bytes 262160 | tf_op jit(solution)/shard_map/reduce_scatter | solution.py:69
  144.9 15.8 %conditional.6 = (bf16[256,512]{1,0:T(8,128)(2,1)}) conditional(s32[]{:T(128)} %bitcast.9, bf16[256,512]{1,0:T(8,128)(2,1)} %bitcast.31, bf16[256,512]{1,0:T(8,128)(2,1)} %bitcast.32, bf16[256,512]{1,0:T(8,128)(2,1)} %bitcast.33), branch_computations={%region_5.0_spmd, %region_6.0_spmd, %region_7.0_spmd} | conditional | bytes 1048624
  144.9 7.5 %collective-permute-start.8 = (bf16[256,512]{1,0:T(8,128)(2,1)}, bf16[256,512]{1,0:T(8,128)(2,1)}, u32[]{:S(2)}, u32[]{:S(2)}) collective-permute-start(bf16[256,512]{1,0:T(8,128)(2,1)} %param.5), channel_id=1, source_target_pairs={{0,64},{16,80},{32,96},{48,112},{64,128},{80,144},{96,160},{112,17... | collective-permute-start | bytes 786440 | tf_op jit(solution)/shard_map/cond/branch_2_fun/ppermute | solution.py:16
  152.4 8.3 %collective-permute-done.8 = bf16[256,512]{1,0:T(8,128)(2,1)} collective-permute-done((bf16[256,512]{1,0:T(8,128)(2,1)}, bf16[256,512]{1,0:T(8,128)(2,1)}, u32[]{:S(2)}, u32[]{:S(2)}) %collective-permute-start.8) | collective-permute-done | bytes 262176 | tf_op jit(solution)/shard_map/cond/branch_2_fun/ppermute | solution.py:16
  160.7 2.1 %multiply_bitcast_fusion = f32[1,256,512]{2,1,0:T(8,128)} fusion(f32[256,512]{1,0:T(8,128)} %get-tuple-element.41, bf16[256,512]{1,0:T(8,128)(2,1)} %get-tuple-element.49, bf16[1,256,512]{2,1,0:T(8,128)(2,1)} %reduce-scatter.2.cloned.1.call-done, f32[1,256,512]{2,1,0:T(8,128)S(1)} %copy-done.3), kind=kLoop, calls=%fused_computation.26 | loop fusion | flops 1048576 | bytes 2097152 | tf_op jit(solution)/shard_map/broadcast_in_dim | solution.py:75
  (13 shorter events, 0.0 us)
Async XLA Ops:
  7.2 13.6 %copy-start = (bf16[1,384,4096]{2,1,0:T(8,128)(2,1)S(1)}, bf16[1,384,4096]{2,1,0:T(8,128)(2,1)}, u32[]{:S(2)}) copy-start(bf16[1,384,4096]{2,1,0:T(8,128)(2,1)} %param.15) | copy-start | bytes 9437188
  7.2 13.6 %copy-start.4 = (f32[4096]{0:T(1024)S(1)}, f32[4096]{0:T(1024)}, u32[]{:S(2)}) copy-start(f32[4096]{0:T(1024)} %param.17) | copy-start | bytes 49156
  7.2 73.8 %all-gather.3.cloned.1.call-start = ((), (), s32[]{:S(2)}) async-start(), calls=%async_computation.2 | async-start | bytes 4718592 | tf_op jit(solution)/shard_map/all_gather | solution.py:37
  18.1 126.8 %reduce-scatter.2.cloned.1.call-start = ((), (), s32[]{:S(2)}) async-start(), calls=%async_computation.1 | async-start | bytes 2359296 | tf_op jit(solution)/shard_map/reduce_scatter | solution.py:69
  21.7 1.7 copy-start.1
  23.4 57.6 %copy-start.5 = (bf16[1,384,512]{2,1,0:T(8,128)(2,1)S(1)}, bf16[1,384,512]{2,1,0:T(8,128)(2,1)}, u32[]{:S(2)}) copy-start(bf16[1,384,512]{2,1,0:T(8,128)(2,1)} %param.16) | copy-start | bytes 1179652
  24.8 70.7 %collective-permute-start.9 = (bf16[384,2048]{1,0:T(8,128)(2,1)}, bf16[384,2048]{1,0:T(8,128)(2,1)S(1)}, u32[]{:S(2)}, u32[]{:S(2)}) collective-permute-start(bf16[384,2048]{1,0:T(8,128)(2,1)} %constant_dynamic-slice_fusion), channel_id=1, source_target_pairs={{0,8},{8,0},{1,9},{9,1},{2,10},{10,2},{3,11},{11,3},{4,12},{12,4},... | collective-permute-start | bytes 4718600 | tf_op jit(solution)/shard_map/ppermute | solution.py:48
  81.0 7.2 %copy-start.2 = (bf16[384,4096]{1,0:T(8,128)(2,1)S(1)}, bf16[384,4096]{1,0:T(8,128)(2,1)}, u32[]{:S(2)}) copy-start(bf16[384,4096]{1,0:T(8,128)(2,1)} %copy-done.1) | copy-start | bytes 9437188
  84.8 10.6 %collective-permute-start.11 = (bf16[192,512]{1,0:T(8,128)(2,1)S(1)}, bf16[192,512]{1,0:T(8,128)(2,1)S(1)}, u32[]{:S(2)}, u32[]{:S(2)}) collective-permute-start(bf16[192,512]{1,0:T(8,128)(2,1)S(1)} %fusion.28), channel_id=1, source_target_pairs={{0,8},{8,0},{1,9},{9,1},{2,10},{10,2},{3,11},{11,3},{4,12},{12,4},... | collective-permute-start | bytes 589832 | tf_op jit(solution)/shard_map/ppermute | solution.py:58
  91.4 8.1 %collective-permute-start.10 = (bf16[192,512]{1,0:T(8,128)(2,1)S(1)}, bf16[192,512]{1,0:T(8,128)(2,1)S(1)}, u32[]{:S(2)}, u32[]{:S(2)}) collective-permute-start(bf16[192,512]{1,0:T(8,128)(2,1)S(1)} %fusion.25), channel_id=1, source_target_pairs={{0,8},{8,0},{1,9},{9,1},{2,10},{10,2},{3,11},{11,3},{4,12},{12,4},... | collective-permute-start | bytes 589832 | tf_op jit(solution)/shard_map/ppermute | solution.py:58
  96.2 6.1 %copy-start.3 = (f32[1,256,512]{2,1,0:T(8,128)S(1)}, f32[1,256,512]{2,1,0:T(8,128)}, u32[]{:S(2)}) copy-start(f32[1,256,512]{2,1,0:T(8,128)} %param.12) | copy-start | bytes 1572868
  102.3 27.4 %collective-permute-start.4 = (f32[256,512]{1,0:T(8,128)S(1)}, f32[256,512]{1,0:T(8,128)}, u32[]{:S(2)}, u32[]{:S(2)}) collective-permute-start(f32[256,512]{1,0:T(8,128)S(1)} %get-tuple-element.29), channel_id=1, source_target_pairs={{0,64},{16,80},{32,96},{48,112},{64,128},{80,144},{96,160},{112,17... | collective-permute-start | bytes 1572872 | tf_op jit(solution)/shard_map/cond/branch_2_fun/ppermute | solution.py:16
  108.8 21.0 %collective-permute-start.5 = (f32[1]{0:T(128)}, f32[1]{0:T(128)}, u32[]{:S(2)}, u32[]{:S(2)}) collective-permute-start(f32[1]{0:T(128)} %get-tuple-element.30), channel_id=1, source_target_pairs={{0,64},{16,80},{32,96},{48,112},{64,128},{80,144},{96,160},{112,17... | collective-permute-start | bytes 20 | tf_op jit(solution)/shard_map/cond/branch_2_fun/ppermute | solution.py:16
  144.9 15.8 %collective-permute-start.8 = (bf16[256,512]{1,0:T(8,128)(2,1)}, bf16[256,512]{1,0:T(8,128)(2,1)}, u32[]{:S(2)}, u32[]{:S(2)}) collective-permute-start(bf16[256,512]{1,0:T(8,128)(2,1)} %param.5), channel_id=1, source_target_pairs={{0,64},{16,80},{32,96},{48,112},{64,128},{80,144},{96,160},{112,17... | collective-permute-start | bytes 786440 | tf_op jit(solution)/shard_map/cond/branch_2_fun/ppermute | solution.py:16
Sparse Core Ops, SparseCore 0:
  18.2 62.7 all-gather.2
  101.8 43.0 reduce-scatter.1

commit v11 on v10

--- a/solution.py
+++ b/solution.py
@@ -33,15 +33,14 @@
     n_ring = lax.axis_size("fz")
     replica_tokens = activations.shape[1] * n_pair * n_ring
     params = (numer / push_weights[0]).astype(jnp.bfloat16)
-    gathered = lax.all_gather(params, "fl", axis=0)
-    gathered = lax.all_gather(gathered, "fz", axis=1)
-    full_params = gathered.reshape(-1, params.shape[1])
+    side = lax.axis_index("fl")
+    flip = [(i, n_pair - 1 - i) for i in range(n_pair)]
+    pair = jnp.stack([params, lax.ppermute(params, "fl", flip)])
+    rows_by_side = lax.all_gather(pair, "fz", axis=1).reshape(n_pair, -1, params.shape[1])
     act32 = activations[0].astype(jnp.float32)
     mean_sq = jnp.mean(act32 * act32, axis=1, keepdims=True)
     normed = (act32 * lax.rsqrt(mean_sq + 1e-05) * gain[None, :]).astype(jnp.bfloat16)
     tokens = normed.shape[0]
-    side = lax.axis_index("fl")
-    flip = [(i, n_pair - 1 - i) for i in range(n_pair)]
     row_width = features // n_pair
     own_cols = lax.dynamic_slice_in_dim(normed, side * row_width, row_width, axis=1)
     partner_cols = lax.dynamic_slice_in_dim(normed, (n_pair - 1 - side) * row_width, row_width, axis=1)
@@ -51,7 +50,9 @@
     mine = theirs = None
     for part in range(2):
         span = slice(part * half, (part + 1) * half)
-        keys = jnp.dot(normed[span], full_params, preferred_element_type=jnp.float32) / math.sqrt(features)
+        keys = jnp.dot(own_cols[span], rows_by_side[0], preferred_element_type=jnp.float32)
+        keys = keys + jnp.dot(partner_cols[span], rows_by_side[1], preferred_element_type=jnp.float32)
+        keys = keys / math.sqrt(features)
         errors = ((keys - targets[0, span].astype(jnp.float32)) / math.sqrt(replica_tokens)).astype(
             jnp.bfloat16
         )

time: 173 us -> 176 us (1.017)
  blocking collectives: 8.82 us -> 0 us
  waiting for transfers between devices: 96.6 us -> 104 us
  starting transfers between devices: 26.6 us -> 30.2 us
    all_gather x1 -> x0, blocking collectives: 8.82 us -> none  [body(): gathered = lax.all_gather(params, 'fl', axis=0)]
    ppermute x0 -> x1, waiting for transfers between devices: none -> 5.36 us  [body(): pair = jnp.stack([params, lax.ppermute(params, 'fl', flip)])]
    ppermute x0 -> x1, starting transfers between devices: none -> 3.48 us  [body(): pair = jnp.stack([params, lax.ppermute(params, 'fl', flip)])]
    reduce_scatter x1, waiting for transfers between devices: 14.5 us -> 17.5 us  [body(): grad16 = lax.psum_scatter(blocks, 'fz', scatter_dimension=0)]
    dot_general x2, matrix products: 2.88 us -> 5.16 us  [body(): lax.dot_general(their_cols[span], their_errors, contract, preferred_eleme...]
    reduce_sum x1, other arithmetic: 2.58 us -> 0.69 us  [body(): mean_sq = jnp.mean(act32 * act32, axis=1, keepdims=True)]
    ppermute x3, waiting for transfers between devices: 26 us -> 24.2 us  [passed_along(): return lax.ppermute(value, axis, pairs)]
    dot_general x2 -> x4, matrix products: 6.97 us -> 5.99 us  [the longest x2 3.01 us: body(): jnp.dot(partner_cols[span], rows_by_side[1], preferred_element_type=jnp.f...]
  transfers between devices with their start and end apart: 8 -> 9, of which waited for: 5 -> 6; matrix products, arithmetic and copies ran while one was open for 8% -> 8% of each run, Pallas kernels for 0% -> 0%
where the time goes in v11:
time: 176 us; the launch traced here: 174 us
  waiting for transfers between devices  104 us (59%)
  starting transfers between devices  30.2 us (17%)
  between operations  17.5 us (10%)
  matrix products  12.7 us (7%)
  other arithmetic  6.97 us (4%)
  local copies, waits for them, and re-layouts  2.95 us (2%)
    all_gather x1, waiting for transfers between devices, body(): lax.all_gather(pair, 'fz', axis=1).reshape(n_pair, -1, params.shape[1])  54.5 us
    ppermute x3, waiting for transfers between devices, passed_along(): return lax.ppermute(value, axis, pairs)  24.2 us
    reduce_scatter x1, waiting for transfers between devices, body(): grad16 = lax.psum_scatter(blocks, 'fz', scatter_dimension=0)  17.5 us
    ppermute x3, starting transfers between devices, passed_along(): return lax.ppermute(value, axis, pairs)  17.1 us
    ppermute x2, starting transfers between devices, body(): their_errors = lax.ppermute(errors, 'fl', flip)  5.84 us
    ppermute x1, waiting for transfers between devices, body(): pair = jnp.stack([params, lax.ppermute(params, 'fl', flip)])  5.36 us
    dot_general x2, matrix products, body(): lax.dot_general(their_cols[span], their_errors, contract, preferred_eleme...  5.16 us
    ppermute x1, starting transfers between devices, body(): their_cols = lax.ppermute(partner_cols, 'fl', flip)  3.74 us
  transfers between devices with their start and end apart: 9, of which 6 were waited for; matrix products, arithmetic and copies ran while one was open for 8% of the time, Pallas kernels for 0%

profile of v11, /device:TPU:6, one launch (start us, length us, event | category | flops | bytes accessed | tf_op | source)
XLA Modules:
  0.0 174.0 jit_solution(6239075853195939553)
XLA Ops:
  8.0 1.2 divide_convert_fusion
  9.2 3.5 %collective-permute-start.9 = (bf16[256,512]{1,0:T(8,128)(2,1)S(1)}, bf16[256,512]{1,0:T(8,128)(2,1)S(1)}, u32[]{:S(2)}, u32[]{:S(2)}) collective-permute-start(bf16[256,512]{1,0:T(8,128)(2,1)S(1)} %divide_convert_fusion), channel_id=1, source_target_pairs={{0,8},{8,0},{1,9},{9,1},{2,10},{10,2},{3,11},{11,3},{4,12},{12,4},... | collective-permute-start | bytes 786440 | tf_op jit(solution)/shard_map/ppermute | solution.py:38
  12.7 1.1 divide_convert_fusion.1
  13.8 5.4 %collective-permute-done.9 = bf16[256,512]{1,0:T(8,128)(2,1)S(1)} collective-permute-done((bf16[256,512]{1,0:T(8,128)(2,1)S(1)}, bf16[256,512]{1,0:T(8,128)(2,1)S(1)}, u32[]{:S(2)}, u32[]{:S(2)}) %collective-permute-start.9) | collective-permute-done | bytes 262176 | tf_op jit(solution)/shard_map/ppermute | solution.py:38
  19.2 0.8 pad_maximum_fusion
  20.0 0.0 reduce-scatter.2.cloned.1.call-start
  20.1 0.7 fusion
  20.8 1.0 fusion.2
  21.8 1.7 copy-done.1
  23.5 1.3 constant_dynamic-slice_fusion
  24.8 3.7 %collective-permute-start.10 = (bf16[384,2048]{1,0:T(8,128)(2,1)}, bf16[384,2048]{1,0:T(8,128)(2,1)}, u32[]{:S(2)}, u32[]{:S(2)}) collective-permute-start(bf16[384,2048]{1,0:T(8,128)(2,1)} %constant_dynamic-slice_fusion), channel_id=1, source_target_pairs={{0,8},{8,0},{1,9},{9,1},{2,10},{10,2},{3,11},{11,3},{4,12},{12,4},... | collective-permute-start | bytes 4718600 | tf_op jit(solution)/shard_map/ppermute | solution.py:47
  28.5 54.5 %all-gather.3.cloned.1.call-done = bf16[2,2048,512]{2,1,0:T(8,128)(2,1)} async-done(((bf16[2,256,512]{2,1,0:T(8,128)(2,1)}), bf16[2,2048,512]{2,1,0:T(8,128)(2,1)}) %all-gather.3.cloned.1.call-update) | async-done | bytes 4194320 | tf_op jit(solution)/shard_map/all_gather | solution.py:39
  83.0 2.4 %fusion.5 = f32[192,512]{1,0:T(8,128)S(1)} fusion(bf16[2,2048,512]{2,1,0:T(8,128)(2,1)} %all-gather.3.cloned.1.call-done, bf16[384,4096]{1,0:T(8,128)(2,1)} %copy-done.1, s32[]{:T(128)S(6)} %add.51, s32[]{:T(128)S(6)} %select_n.7), kind=kOutput, calls=%fused_computation.12 | convolution fusion | flops 402653184 | bytes 3276808 | tf_op jit(solution)/shard_map/dot_general | solution.py:54
  85.4 2.3 %fusion.15 = bf16[192,512]{1,0:T(8,128)(2,1)S(1)} fusion(f32[192,512]{1,0:T(8,128)S(1)} %fusion.5, bf16[2,2048,512]{2,1,0:T(8,128)(2,1)} %all-gather.3.cloned.1.call-done, bf16[384,4096]{1,0:T(8,128)(2,1)S(1)} %copy-done.2, s32[]{:T(128)S(6)} %add.51, s32[]{:T(128)S(6)} %select_n.6, bf16[1,384,512]{2,1,0:T(8,128)(2,1)S(1)} %copy-done.6), kind=kOutput, calls=%fused_computation.22 | convolution fusion | flops 403243008 | bytes 3670024 | tf_op jit(solution)/shard_map/dot_general | solution.py:53
  87.8 3.4 %collective-permute-start.12 = (bf16[192,512]{1,0:T(8,128)(2,1)S(1)}, bf16[192,512]{1,0:T(8,128)(2,1)S(1)}, u32[]{:S(2)}, u32[]{:S(2)}) collective-permute-start(bf16[192,512]{1,0:T(8,128)(2,1)S(1)} %fusion.15), channel_id=1, source_target_pairs={{0,8},{8,0},{1,9},{9,1},{2,10},{10,2},{3,11},{11,3},{4,12},{12,4},... | collective-permute-start | bytes 589832 | tf_op jit(solution)/shard_map/ppermute | solution.py:59
  91.2 0.6 fusion.6
  91.8 0.6 fusion.16
  92.4 2.4 %collective-permute-start.11 = (bf16[192,512]{1,0:T(8,128)(2,1)S(1)}, bf16[192,512]{1,0:T(8,128)(2,1)S(1)}, u32[]{:S(2)}, u32[]{:S(2)}) collective-permute-start(bf16[192,512]{1,0:T(8,128)(2,1)S(1)} %fusion.16), channel_id=1, source_target_pairs={{0,8},{8,0},{1,9},{9,1},{2,10},{10,2},{3,11},{11,3},{4,12},{12,4},... | collective-permute-start | bytes 589832 | tf_op jit(solution)/shard_map/ppermute | solution.py:59
  94.9 0.8 fusion.22
  95.6 0.8 add_convert_fusion.2
  96.5 1.9 %fusion.17 = f32[2048,512]{1,0:T(8,128)S(1)} fusion(bf16[192,512]{1,0:T(8,128)(2,1)S(1)} %collective-permute-done.12, bf16[384,2048]{1,0:T(8,128)(2,1)} %collective-permute-done.10), kind=kOutput, calls=%fused_computation.24 | convolution fusion | flops 402653184 | bytes 5177344 | tf_op jit(solution)/shard_map/dot_general | solution.py:61
  98.4 2.1 %collective-permute-done.11 = bf16[192,512]{1,0:T(8,128)(2,1)S(1)} collective-permute-done((bf16[192,512]{1,0:T(8,128)(2,1)S(1)}, bf16[192,512]{1,0:T(8,128)(2,1)S(1)}, u32[]{:S(2)}, u32[]{:S(2)}) %collective-permute-start.11) | collective-permute-done | bytes 196640 | tf_op jit(solution)/shard_map/ppermute | solution.py:59
  100.5 3.3 %add_convert_fusion = bf16[2048,512]{1,0:T(8,128)(2,1)} fusion(bf16[2048,512]{1,0:T(8,128)(2,1)S(1)} %add_convert_fusion.2, f32[2048,512]{1,0:T(8,128)S(1)} %fusion.17, bf16[192,512]{1,0:T(8,128)(2,1)S(1)} %collective-permute-done.11, bf16[384,2048]{1,0:T(8,128)(2,1)} %collective-permute-done.10), kind=kOutput, calls=%fused_computation.5 | convolution fusion | flops 408944640 | bytes 9371648 | tf_op jit(solution)/shard_map/dot_general | solution.py:61
  104.5 25.2 %conditional.5 = (f32[256,512]{1,0:T(8,128)}, f32[1]{0:T(128)}) conditional(s32[]{:T(128)} %bitcast.11, (f32[256,512]{1,0:T(8,128)S(1)}, f32[1]{0:T(128)}) %tuple.57, (f32[256,512]{1,0:T(8,128)S(1)}, f32[1]{0:T(128)}) %tuple.58, (f32[256,512]{1,0:T(8,128)S(1)}, f32[1]{0:T(128)}) %tuple.59), branch_computations={%region_2.0_spmd, %region_3.0_spmd, %region_4.0_spmd} | conditional | bytes 2097264 | solution.py:25
  104.5 7.2 %collective-permute-start.4 = (f32[256,512]{1,0:T(8,128)S(1)}, f32[256,512]{1,0:T(8,128)}, u32[]{:S(2)}, u32[]{:S(2)}) collective-permute-start(f32[256,512]{1,0:T(8,128)S(1)} %get-tuple-element.29), channel_id=1, source_target_pairs={{0,64},{16,80},{32,96},{48,112},{64,128},{80,144},{96,160},{112,17... | collective-permute-start | bytes 1572872 | tf_op jit(solution)/shard_map/cond/branch_2_fun/ppermute | solution.py:16
  111.7 2.5 %collective-permute-start.5 = (f32[1]{0:T(128)}, f32[1]{0:T(128)}, u32[]{:S(2)}, u32[]{:S(2)}) collective-permute-start(f32[1]{0:T(128)} %get-tuple-element.30), channel_id=1, source_target_pairs={{0,64},{16,80},{32,96},{48,112},{64,128},{80,144},{96,160},{112,17... | collective-permute-start | bytes 20 | tf_op jit(solution)/shard_map/cond/branch_2_fun/ppermute | solution.py:16
  114.2 15.4 %collective-permute-done.5 = f32[1]{0:T(128)} collective-permute-done((f32[1]{0:T(128)}, f32[1]{0:T(128)}, u32[]{:S(2)}, u32[]{:S(2)}) %collective-permute-start.5) | collective-permute-done | bytes 36 | tf_op jit(solution)/shard_map/cond/branch_2_fun/ppermute | solution.py:16
  130.3 17.5 %reduce-scatter.2.cloned.1.call-done = bf16[1,256,512]{2,1,0:T(8,128)(2,1)} async-done(((bf16[8,256,512]{2,1,0:T(8,128)(2,1)}), bf16[1,256,512]{2,1,0:T(8,128)(2,1)}) %reduce-scatter.2.cloned.1.call-update) | async-done | bytes 262160 | tf_op jit(solution)/shard_map/reduce_scatter | solution.py:70
  147.8 16.1 %conditional.6 = (bf16[256,512]{1,0:T(8,128)(2,1)}) conditional(s32[]{:T(128)} %bitcast.11, bf16[256,512]{1,0:T(8,128)(2,1)} %bitcast.60, bf16[256,512]{1,0:T(8,128)(2,1)} %bitcast.61, bf16[256,512]{1,0:T(8,128)(2,1)} %bitcast.62), branch_computations={%region_5.0_spmd, %region_6.0_spmd, %region_7.0_spmd} | conditional | bytes 1048624
  147.8 7.3 %collective-permute-start.8 = (bf16[256,512]{1,0:T(8,128)(2,1)}, bf16[256,512]{1,0:T(8,128)(2,1)}, u32[]{:S(2)}, u32[]{:S(2)}) collective-permute-start(bf16[256,512]{1,0:T(8,128)(2,1)} %param.5), channel_id=1, source_target_pairs={{0,64},{16,80},{32,96},{48,112},{64,128},{80,144},{96,160},{112,17... | collective-permute-start | bytes 786440 | tf_op jit(solution)/shard_map/cond/branch_2_fun/ppermute | solution.py:16
  155.2 8.8 %collective-permute-done.8 = bf16[256,512]{1,0:T(8,128)(2,1)} collective-permute-done((bf16[256,512]{1,0:T(8,128)(2,1)}, bf16[256,512]{1,0:T(8,128)(2,1)}, u32[]{:S(2)}, u32[]{:S(2)}) %collective-permute-start.8) | collective-permute-done | bytes 262176 | tf_op jit(solution)/shard_map/cond/branch_2_fun/ppermute | solution.py:16
  163.9 2.1 %multiply_bitcast_fusion = f32[1,256,512]{2,1,0:T(8,128)} fusion(f32[256,512]{1,0:T(8,128)} %get-tuple-element.41, bf16[256,512]{1,0:T(8,128)(2,1)} %get-tuple-element.49, bf16[1,256,512]{2,1,0:T(8,128)(2,1)} %reduce-scatter.2.cloned.1.call-done, f32[1,256,512]{2,1,0:T(8,128)S(1)} %copy-done.3), kind=kLoop, calls=%fused_computation.35 | loop fusion | flops 1048576 | bytes 2097152 | tf_op jit(solution)/shard_map/broadcast_in_dim | solution.py:76
  (20 shorter events, 0.1 us)
Async XLA Ops:
  7.2 12.9 %copy-start = (bf16[1,384,4096]{2,1,0:T(8,128)(2,1)S(1)}, bf16[1,384,4096]{2,1,0:T(8,128)(2,1)}, u32[]{:S(2)}) copy-start(bf16[1,384,4096]{2,1,0:T(8,128)(2,1)} %param.15) | copy-start | bytes 9437188
  7.2 75.8 %all-gather.3.cloned.1.call-start = ((), (), s32[]{:S(2)}) async-start(), calls=%async_computation.2 | async-start | bytes 4718592 | tf_op jit(solution)/shard_map/all_gather | solution.py:39
  8.0 12.8 %copy-start.4 = (f32[4096]{0:T(1024)S(1)}, f32[4096]{0:T(1024)}, u32[]{:S(2)}) copy-start(f32[4096]{0:T(1024)} %param.17) | copy-start | bytes 49156
  9.2 9.9 %collective-permute-start.9 = (bf16[256,512]{1,0:T(8,128)(2,1)S(1)}, bf16[256,512]{1,0:T(8,128)(2,1)S(1)}, u32[]{:S(2)}, u32[]{:S(2)}) collective-permute-start(bf16[256,512]{1,0:T(8,128)(2,1)S(1)} %divide_convert_fusion), channel_id=1, source_target_pairs={{0,8},{8,0},{1,9},{9,1},{2,10},{10,2},{3,11},{11,3},{4,12},{12,4},... | collective-permute-start | bytes 786440 | tf_op jit(solution)/shard_map/ppermute | solution.py:38
  20.0 127.8 %reduce-scatter.2.cloned.1.call-start = ((), (), s32[]{:S(2)}) async-start(), calls=%async_computation.1 | async-start | bytes 2359296 | tf_op jit(solution)/shard_map/reduce_scatter | solution.py:70
  21.8 1.7 copy-start.1
  23.5 61.9 %copy-start.6 = (bf16[1,384,512]{2,1,0:T(8,128)(2,1)S(1)}, bf16[1,384,512]{2,1,0:T(8,128)(2,1)}, u32[]{:S(2)}) copy-start(bf16[1,384,512]{2,1,0:T(8,128)(2,1)} %param.16) | copy-start | bytes 1179652
  24.8 60.6 %copy-start.2 = (bf16[384,4096]{1,0:T(8,128)(2,1)S(1)}, bf16[384,4096]{1,0:T(8,128)(2,1)}, u32[]{:S(2)}) copy-start(bf16[384,4096]{1,0:T(8,128)(2,1)} %copy-done.1) | copy-start | bytes 9437188
  24.8 71.7 %collective-permute-start.10 = (bf16[384,2048]{1,0:T(8,128)(2,1)}, bf16[384,2048]{1,0:T(8,128)(2,1)}, u32[]{:S(2)}, u32[]{:S(2)}) collective-permute-start(bf16[384,2048]{1,0:T(8,128)(2,1)} %constant_dynamic-slice_fusion), channel_id=1, source_target_pairs={{0,8},{8,0},{1,9},{9,1},{2,10},{10,2},{3,11},{11,3},{4,12},{12,4},... | collective-permute-start | bytes 4718600 | tf_op jit(solution)/shard_map/ppermute | solution.py:47
  85.4 5.8 %copy-start.5 = (bf16[2,2048,512]{2,1,0:T(8,128)(2,1)S(1)}, bf16[2,2048,512]{2,1,0:T(8,128)(2,1)}, u32[]{:S(2)}) copy-start(bf16[2,2048,512]{2,1,0:T(8,128)(2,1)} %all-gather.3.cloned.1.call-done) | copy-start | bytes 12582916
  87.8 8.7 %collective-permute-start.12 = (bf16[192,512]{1,0:T(8,128)(2,1)S(1)}, bf16[192,512]{1,0:T(8,128)(2,1)S(1)}, u32[]{:S(2)}, u32[]{:S(2)}) collective-permute-start(bf16[192,512]{1,0:T(8,128)(2,1)S(1)} %fusion.15), channel_id=1, source_target_pairs={{0,8},{8,0},{1,9},{9,1},{2,10},{10,2},{3,11},{11,3},{4,12},{12,4},... | collective-permute-start | bytes 589832 | tf_op jit(solution)/shard_map/ppermute | solution.py:59
  92.4 8.1 %collective-permute-start.11 = (bf16[192,512]{1,0:T(8,128)(2,1)S(1)}, bf16[192,512]{1,0:T(8,128)(2,1)S(1)}, u32[]{:S(2)}, u32[]{:S(2)}) collective-permute-start(bf16[192,512]{1,0:T(8,128)(2,1)S(1)} %fusion.16), channel_id=1, source_target_pairs={{0,8},{8,0},{1,9},{9,1},{2,10},{10,2},{3,11},{11,3},{4,12},{12,4},... | collective-permute-start | bytes 589832 | tf_op jit(solution)/shard_map/ppermute | solution.py:59
  98.4 6.1 %copy-start.3 = (f32[1,256,512]{2,1,0:T(8,128)S(1)}, f32[1,256,512]{2,1,0:T(8,128)}, u32[]{:S(2)}) copy-start(f32[1,256,512]{2,1,0:T(8,128)} %param.12) | copy-start | bytes 1572868
  104.5 25.2 %collective-permute-start.4 = (f32[256,512]{1,0:T(8,128)S(1)}, f32[256,512]{1,0:T(8,128)}, u32[]{:S(2)}, u32[]{:S(2)}) collective-permute-start(f32[256,512]{1,0:T(8,128)S(1)} %get-tuple-element.29), channel_id=1, source_target_pairs={{0,64},{16,80},{32,96},{48,112},{64,128},{80,144},{96,160},{112,17... | collective-permute-start | bytes 1572872 | tf_op jit(solution)/shard_map/cond/branch_2_fun/ppermute | solution.py:16
  111.7 18.0 %collective-permute-start.5 = (f32[1]{0:T(128)}, f32[1]{0:T(128)}, u32[]{:S(2)}, u32[]{:S(2)}) collective-permute-start(f32[1]{0:T(128)} %get-tuple-element.30), channel_id=1, source_target_pairs={{0,64},{16,80},{32,96},{48,112},{64,128},{80,144},{96,160},{112,17... | collective-permute-start | bytes 20 | tf_op jit(solution)/shard_map/cond/branch_2_fun/ppermute | solution.py:16
  147.8 16.1 %collective-permute-start.8 = (bf16[256,512]{1,0:T(8,128)(2,1)}, bf16[256,512]{1,0:T(8,128)(2,1)}, u32[]{:S(2)}, u32[]{:S(2)}) collective-permute-start(bf16[256,512]{1,0:T(8,128)(2,1)} %param.5), channel_id=1, source_target_pairs={{0,64},{16,80},{32,96},{48,112},{64,128},{80,144},{96,160},{112,17... | collective-permute-start | bytes 786440 | tf_op jit(solution)/shard_map/cond/branch_2_fun/ppermute | solution.py:16
Sparse Core Ops, SparseCore 0:
  20.2 62.7 all-gather.2
  103.9 43.8 reduce-scatter.1

commit v12 on v10

--- a/solution.py
+++ b/solution.py
@@ -47,22 +47,21 @@
     partner_cols = lax.dynamic_slice_in_dim(normed, (n_pair - 1 - side) * row_width, row_width, axis=1)
     their_cols = lax.ppermute(partner_cols, "fl", flip)
     contract = (((0,), (0,)), ((), ()))
-    half = tokens // 2
-    mine = theirs = None
+    width = full_params.shape[1] // 2
+    sums = []
     for part in range(2):
-        span = slice(part * half, (part + 1) * half)
-        keys = jnp.dot(normed[span], full_params, preferred_element_type=jnp.float32) / math.sqrt(features)
-        errors = ((keys - targets[0, span].astype(jnp.float32)) / math.sqrt(replica_tokens)).astype(
+        span = slice(part * width, (part + 1) * width)
+        keys = jnp.dot(normed, full_params[:, span], preferred_element_type=jnp.float32) / math.sqrt(features)
+        errors = ((keys - targets[0][:, span].astype(jnp.float32)) / math.sqrt(replica_tokens)).astype(
             jnp.bfloat16
         )
         their_errors = lax.ppermute(errors, "fl", flip)
-        term = lax.dot_general(own_cols[span], errors, contract, preferred_element_type=jnp.float32)
-        their_term = lax.dot_general(
-            their_cols[span], their_errors, contract, preferred_element_type=jnp.float32
+        mine = lax.dot_general(own_cols, errors, contract, preferred_element_type=jnp.float32)
+        theirs = lax.dot_general(their_cols, their_errors, contract, preferred_element_type=jnp.float32)
+        sums.append(
+            mine.astype(jnp.bfloat16).astype(jnp.float32) + theirs.astype(jnp.bfloat16).astype(jnp.float32)
         )
-        mine = term if mine is None else mine + term
-        theirs = their_term if theirs is None else theirs + their_term
-    pair_sum = mine.astype(jnp.bfloat16).astype(jnp.float32) + theirs.astype(jnp.bfloat16).astype(jnp.float32)
+    pair_sum = jnp.concatenate(sums, axis=1)
     blocks = pair_sum.astype(jnp.bfloat16).reshape(n_ring, -1, pair_sum.shape[1])
     early, weight, blocks = lax.optimization_barrier((numer, push_weights, blocks))
     peer_numer, peer_weight = to_peer(send_to_peer, (early, weight), power)

time: 173 us -> 172 us (level)
  other arithmetic: 6.93 us -> 10.3 us
  waiting for transfers between devices: 96.6 us -> 99.9 us
  starting transfers between devices: 26.6 us -> 23.6 us
  matrix products: 11.4 us -> 9.61 us
    ppermute x3, waiting for transfers between devices: 26 us -> 29.7 us  [passed_along(): return lax.ppermute(value, axis, pairs)]
    ppermute x3, starting transfers between devices: 17.2 us -> 14.2 us  [passed_along(): return lax.ppermute(value, axis, pairs)]
    convert_element_type x1, other arithmetic: 1 us -> 2.95 us  [body(): (act32 * lax.rsqrt(mean_sq + 1e-05) * gain[None, :]).astype(jnp.bfloat16)]
    dot_general x6, matrix products: 11.4 us -> 9.61 us  [the longest x2 4.36 us: body(): lax.dot_general(their_cols, their_errors, contract, preferred_element_typ...]
where the time goes in v12:
time: 172 us; the launch traced here: 171 us
  waiting for transfers between devices  99.9 us (58%)
  starting transfers between devices  23.6 us (14%)
  between operations  17.3 us (10%)
  other arithmetic  10.3 us (6%)
  matrix products  9.61 us (6%)
  blocking collectives  8.82 us (5%)
  local copies, waits for them, and re-layouts  1.73 us (1%)
    all_gather x1, waiting for transfers between devices, body(): gathered = lax.all_gather(gathered, 'fz', axis=1)  52.4 us
    ppermute x3, waiting for transfers between devices, passed_along(): return lax.ppermute(value, axis, pairs)  29.7 us
    ppermute x3, starting transfers between devices, passed_along(): return lax.ppermute(value, axis, pairs)  14.2 us
    reduce_scatter x1, waiting for transfers between devices, body(): grad16 = lax.psum_scatter(blocks, 'fz', scatter_dimension=0)  13.6 us
    all_gather x1, blocking collectives, body(): gathered = lax.all_gather(params, 'fl', axis=0)  8.82 us
    ppermute x2, starting transfers between devices, body(): their_errors = lax.ppermute(errors, 'fl', flip)  5.85 us
    dot_general x2, matrix products, body(): lax.dot_general(their_cols, their_errors, contract, preferred_element_typ...  4.36 us
    ppermute x2, waiting for transfers between devices, body(): their_errors = lax.ppermute(errors, 'fl', flip)  4.16 us
  transfers between devices with their start and end apart: 8, of which 5 were waited for; matrix products, arithmetic and copies ran while one was open for 8% of the time, Pallas kernels for 0%

profile of v12, /device:TPU:6, one launch (start us, length us, event | category | flops | bytes accessed | tf_op | source)
XLA Modules:
  0.0 171.3 jit_solution(11992484429087753954)
XLA Ops:
  7.2 0.0 all-gather.3.cloned.1.call-start
  7.9 1.1 divide_convert_fusion
  8.9 0.0 copy-start.1
  9.0 8.8 %all_gather.10 = bf16[2,256,512]{2,1,0:T(8,128)(2,1)} all-gather(bf16[1,256,512]{2,1,0:T(8,128)(2,1)S(1)} %divide_convert_fusion), channel_id=1, replica_groups=mesh['replica'=32,'fl'=2,'fz'=8] {'fl'}, dimensions={0}, use_global_device_ids=true | all-gather | bytes 786432 | tf_op jit(solution)/shard_map/all_gather | solution.py:36
  17.8 0.0 all-gather.3.cloned.1.call-update
  17.8 0.0 reduce-scatter.2.cloned.1.call-start
  17.9 2.6 %fusion = f32[384]{0:T(512)S(1)} fusion(bf16[1,384,4096]{2,1,0:T(8,128)(2,1)} %param.15), kind=kLoop, calls=%fused_computation.2 | loop fusion | flops 4718208 | bytes 3147264 | tf_op jit(solution)/shard_map/reduce_sum | solution.py:40
  20.5 3.0 %fusion.2 = bf16[384,4096]{1,0:T(8,128)(2,1)S(1)} fusion(bf16[1,384,4096]{2,1,0:T(8,128)(2,1)} %param.15, f32[4096]{0:T(1024)S(1)} %copy-done.1, f32[384]{0:T(512)S(1)} %add_rsqrt_fusion), kind=kLoop, calls=%fused_computation.4 | loop fusion | flops 6291456 | bytes 6309376 | tf_op jit(solution)/shard_map/convert_element_type | solution.py:41
  23.4 1.4 constant_dynamic-slice_fusion
  24.8 3.5 %collective-permute-start.9 = (bf16[384,2048]{1,0:T(8,128)(2,1)}, bf16[384,2048]{1,0:T(8,128)(2,1)}, u32[]{:S(2)}, u32[]{:S(2)}) collective-permute-start(bf16[384,2048]{1,0:T(8,128)(2,1)} %constant_dynamic-slice_fusion), channel_id=1, source_target_pairs={{0,8},{8,0},{1,9},{9,1},{2,10},{10,2},{3,11},{11,3},{4,12},{12,4},... | collective-permute-start | bytes 4718600 | tf_op jit(solution)/shard_map/ppermute | solution.py:48
  28.3 52.4 %all-gather.3.cloned.1.call-done = bf16[2,2048,512]{2,1,0:T(8,128)(2,1)} async-done(((bf16[2,256,512]{2,1,0:T(8,128)(2,1)}), bf16[2,2048,512]{2,1,0:T(8,128)(2,1)}) %all-gather.3.cloned.1.call-update) | async-done | bytes 4194320 | tf_op jit(solution)/shard_map/all_gather | solution.py:37
  80.7 2.7 %fusion.35 = bf16[384,256]{1,0:T(8,128)(2,1)S(1)} fusion(bf16[384,4096]{1,0:T(8,128)(2,1)S(1)} %fusion.2, bf16[4096,512]{1,0:T(8,128)(2,1)} %bitcast.33, bf16[384,512]{1,0:T(8,128)(2,1)S(1)} %bitcast.35), kind=kOutput, calls=%fused_computation.30 | convolution fusion | flops 805797888 | bytes 5636096 | tf_op jit(solution)/shard_map/dot_general | solution.py:54
  83.5 3.4 %collective-permute-start.10 = (bf16[384,256]{1,0:T(8,128)(2,1)S(1)}, bf16[384,256]{1,0:T(8,128)(2,1)S(1)}, u32[]{:S(2)}, u32[]{:S(2)}) collective-permute-start(bf16[384,256]{1,0:T(8,128)(2,1)S(1)} %fusion.35), channel_id=1, source_target_pairs={{0,8},{8,0},{1,9},{9,1},{2,10},{10,2},{3,11},{11,3},{4,12},{12,4},... | collective-permute-start | bytes 589832 | tf_op jit(solution)/shard_map/ppermute | solution.py:58
  86.9 1.0 fusion.38
  87.9 2.5 %collective-permute-start.11 = (bf16[384,256]{1,0:T(8,128)(2,1)S(1)}, bf16[384,256]{1,0:T(8,128)(2,1)S(1)}, u32[]{:S(2)}, u32[]{:S(2)}) collective-permute-start(bf16[384,256]{1,0:T(8,128)(2,1)S(1)} %fusion.38), channel_id=1, source_target_pairs={{0,8},{8,0},{1,9},{9,1},{2,10},{10,2},{3,11},{11,3},{4,12},{12,4},... | collective-permute-start | bytes 589832 | tf_op jit(solution)/shard_map/ppermute | solution.py:58
  90.4 0.8 fusion.3
  91.1 0.8 fusion.6
  91.9 4.2 %collective-permute-done.11 = bf16[384,256]{1,0:T(8,128)(2,1)S(1)} collective-permute-done((bf16[384,256]{1,0:T(8,128)(2,1)S(1)}, bf16[384,256]{1,0:T(8,128)(2,1)S(1)}, u32[]{:S(2)}, u32[]{:S(2)}) %collective-permute-start.11) | collective-permute-done | bytes 196640 | tf_op jit(solution)/shard_map/ppermute | solution.py:58
  96.0 2.2 %fusion.9 = bf16[2048,256]{1,0:T(8,128)(2,1)S(1)} fusion(f32[2048,256]{1,0:T(8,128)S(1)} %fusion.6, bf16[384,2048]{1,0:T(8,128)(2,1)} %collective-permute-done.9, bf16[384,256]{1,0:T(8,128)(2,1)S(1)} %collective-permute-done.11), kind=kOutput, calls=%fused_computation.15 | convolution fusion | flops 404750336 | bytes 4915200 | tf_op jit(solution)/shard_map/dot_general | solution.py:60
  98.2 2.2 %fusion.10 = bf16[2048,256]{1,0:T(8,128)(2,1)S(1)} fusion(f32[2048,256]{1,0:T(8,128)S(1)} %fusion.3, bf16[384,2048]{1,0:T(8,128)(2,1)} %collective-permute-done.9, bf16[384,256]{1,0:T(8,128)(2,1)S(1)} %collective-permute-done.10), kind=kOutput, calls=%fused_computation.16 | convolution fusion | flops 404750336 | bytes 4915200 | tf_op jit(solution)/shard_map/dot_general | solution.py:60
  100.4 1.5 pad_maximum_fusion
  102.0 0.0 reduce-scatter.2.cloned.1.call-update
  102.7 0.3 copy-done
  103.0 28.8 %conditional.5 = (f32[256,512]{1,0:T(8,128)}, f32[1]{0:T(128)}) conditional(s32[]{:T(128)} %bitcast.9, (f32[256,512]{1,0:T(8,128)S(1)}, f32[1]{0:T(128)}) %tuple.57, (f32[256,512]{1,0:T(8,128)S(1)}, f32[1]{0:T(128)}) %tuple.58, (f32[256,512]{1,0:T(8,128)S(1)}, f32[1]{0:T(128)}) %tuple.59), branch_computations={%region_2.0_spmd, %region_3.0_spmd, %region_4.0_spmd} | conditional | bytes 2097264 | solution.py:25
  103.0 4.3 %collective-permute-start.2 = (f32[256,512]{1,0:T(8,128)S(1)}, f32[256,512]{1,0:T(8,128)}, u32[]{:S(2)}, u32[]{:S(2)}) collective-permute-start(f32[256,512]{1,0:T(8,128)S(1)} %get-tuple-element.27), channel_id=1, source_target_pairs={{0,32},{16,48},{32,64},{48,80},{64,96},{80,112},{96,128},{112,144}... | collective-permute-start | bytes 1572872 | tf_op jit(solution)/shard_map/cond/branch_1_fun/ppermute | solution.py:16
  107.3 5.5 %collective-permute-start.3 = (f32[1]{0:T(128)}, f32[1]{0:T(128)}, u32[]{:S(2)}, u32[]{:S(2)}) collective-permute-start(f32[1]{0:T(128)} %get-tuple-element.28), channel_id=1, source_target_pairs={{0,32},{16,48},{32,64},{48,80},{64,96},{80,112},{96,128},{112,144}... | collective-permute-start | bytes 20 | tf_op jit(solution)/shard_map/cond/branch_1_fun/ppermute | solution.py:16
  112.9 19.0 %collective-permute-done.3 = f32[1]{0:T(128)} collective-permute-done((f32[1]{0:T(128)}, f32[1]{0:T(128)}, u32[]{:S(2)}, u32[]{:S(2)}) %collective-permute-start.3) | collective-permute-done | bytes 36 | tf_op jit(solution)/shard_map/cond/branch_1_fun/ppermute | solution.py:16
  132.5 13.6 %reduce-scatter.2.cloned.1.call-done = bf16[1,256,512]{2,1,0:T(8,128)(2,1)} async-done(((bf16[8,256,512]{2,1,0:T(8,128)(2,1)}), bf16[1,256,512]{2,1,0:T(8,128)(2,1)}) %reduce-scatter.2.cloned.1.call-update) | async-done | bytes 262160 | tf_op jit(solution)/shard_map/reduce_scatter | solution.py:68
  146.1 15.1 %conditional.6 = (bf16[256,512]{1,0:T(8,128)(2,1)}) conditional(s32[]{:T(128)} %bitcast.9, bf16[256,512]{1,0:T(8,128)(2,1)} %bitcast.30, bf16[256,512]{1,0:T(8,128)(2,1)} %bitcast.31, bf16[256,512]{1,0:T(8,128)(2,1)} %bitcast.32), branch_computations={%region_5.0_spmd, %region_6.0_spmd, %region_7.0_spmd} | conditional | bytes 1048624
  146.1 4.4 %collective-permute-start.7 = (bf16[256,512]{1,0:T(8,128)(2,1)}, bf16[256,512]{1,0:T(8,128)(2,1)}, u32[]{:S(2)}, u32[]{:S(2)}) collective-permute-start(bf16[256,512]{1,0:T(8,128)(2,1)} %param.4), channel_id=1, source_target_pairs={{0,32},{16,48},{32,64},{48,80},{64,96},{80,112},{96,128},{112,144}... | collective-permute-start | bytes 786440 | tf_op jit(solution)/shard_map/cond/branch_1_fun/ppermute | solution.py:16
  150.5 10.7 %collective-permute-done.7 = bf16[256,512]{1,0:T(8,128)(2,1)} collective-permute-done((bf16[256,512]{1,0:T(8,128)(2,1)}, bf16[256,512]{1,0:T(8,128)(2,1)}, u32[]{:S(2)}, u32[]{:S(2)}) %collective-permute-start.7) | collective-permute-done | bytes 262176 | tf_op jit(solution)/shard_map/cond/branch_1_fun/ppermute | solution.py:16
  161.2 2.1 %multiply_bitcast_fusion = f32[1,256,512]{2,1,0:T(8,128)} fusion(f32[256,512]{1,0:T(8,128)} %get-tuple-element.41, bf16[256,512]{1,0:T(8,128)(2,1)} %get-tuple-element.49, bf16[1,256,512]{2,1,0:T(8,128)(2,1)} %reduce-scatter.2.cloned.1.call-done, f32[1,256,512]{2,1,0:T(8,128)S(1)} %copy-done), kind=kLoop, calls=%fused_computation.32 | loop fusion | flops 1048576 | bytes 2097152 | tf_op jit(solution)/shard_map/broadcast_in_dim | solution.py:74
  (10 shorter events, 0.0 us)
Async XLA Ops:
  7.2 73.6 %all-gather.3.cloned.1.call-start = ((), (), s32[]{:S(2)}) async-start(), calls=%async_computation.2 | async-start | bytes 4718592 | tf_op jit(solution)/shard_map/all_gather | solution.py:37
  8.9 11.5 %copy-start.1 = (f32[4096]{0:T(1024)S(1)}, f32[4096]{0:T(1024)}, u32[]{:S(2)}) copy-start(f32[4096]{0:T(1024)} %param.17) | copy-start | bytes 49156
  17.8 128.3 %reduce-scatter.2.cloned.1.call-start = ((), (), s32[]{:S(2)}) async-start(), calls=%async_computation.1 | async-start | bytes 2359296 | tf_op jit(solution)/shard_map/reduce_scatter | solution.py:68
  23.4 57.3 %copy-start.3 = (bf16[1,384,512]{2,1,0:T(8,128)(2,1)S(1)}, bf16[1,384,512]{2,1,0:T(8,128)(2,1)}, u32[]{:S(2)}) copy-start(bf16[1,384,512]{2,1,0:T(8,128)(2,1)} %param.16) | copy-start | bytes 1179652
  24.8 67.1 %collective-permute-start.9 = (bf16[384,2048]{1,0:T(8,128)(2,1)}, bf16[384,2048]{1,0:T(8,128)(2,1)}, u32[]{:S(2)}, u32[]{:S(2)}) collective-permute-start(bf16[384,2048]{1,0:T(8,128)(2,1)} %constant_dynamic-slice_fusion), channel_id=1, source_target_pairs={{0,8},{8,0},{1,9},{9,1},{2,10},{10,2},{3,11},{11,3},{4,12},{12,4},... | collective-permute-start | bytes 4718600 | tf_op jit(solution)/shard_map/ppermute | solution.py:48
  80.7 6.1 %copy-start.2 = (bf16[2,2048,512]{2,1,0:T(8,128)(2,1)S(1)}, bf16[2,2048,512]{2,1,0:T(8,128)(2,1)}, u32[]{:S(2)}) copy-start(bf16[2,2048,512]{2,1,0:T(8,128)(2,1)} %all-gather.3.cloned.1.call-done) | copy-start | bytes 12582916
  83.5 14.8 %collective-permute-start.10 = (bf16[384,256]{1,0:T(8,128)(2,1)S(1)}, bf16[384,256]{1,0:T(8,128)(2,1)S(1)}, u32[]{:S(2)}, u32[]{:S(2)}) collective-permute-start(bf16[384,256]{1,0:T(8,128)(2,1)S(1)} %fusion.35), channel_id=1, source_target_pairs={{0,8},{8,0},{1,9},{9,1},{2,10},{10,2},{3,11},{11,3},{4,12},{12,4},... | collective-permute-start | bytes 589832 | tf_op jit(solution)/shard_map/ppermute | solution.py:58
  87.9 8.1 %collective-permute-start.11 = (bf16[384,256]{1,0:T(8,128)(2,1)S(1)}, bf16[384,256]{1,0:T(8,128)(2,1)S(1)}, u32[]{:S(2)}, u32[]{:S(2)}) collective-permute-start(bf16[384,256]{1,0:T(8,128)(2,1)S(1)} %fusion.38), channel_id=1, source_target_pairs={{0,8},{8,0},{1,9},{9,1},{2,10},{10,2},{3,11},{11,3},{4,12},{12,4},... | collective-permute-start | bytes 589832 | tf_op jit(solution)/shard_map/ppermute | solution.py:58
  101.9 1.1 copy-start
  103.0 28.8 %collective-permute-start.2 = (f32[256,512]{1,0:T(8,128)S(1)}, f32[256,512]{1,0:T(8,128)}, u32[]{:S(2)}, u32[]{:S(2)}) collective-permute-start(f32[256,512]{1,0:T(8,128)S(1)} %get-tuple-element.27), channel_id=1, source_target_pairs={{0,32},{16,48},{32,64},{48,80},{64,96},{80,112},{96,128},{112,144}... | collective-permute-start | bytes 1572872 | tf_op jit(solution)/shard_map/cond/branch_1_fun/ppermute | solution.py:16
  107.3 24.5 %collective-permute-start.3 = (f32[1]{0:T(128)}, f32[1]{0:T(128)}, u32[]{:S(2)}, u32[]{:S(2)}) collective-permute-start(f32[1]{0:T(128)} %get-tuple-element.28), channel_id=1, source_target_pairs={{0,32},{16,48},{32,64},{48,80},{64,96},{80,112},{96,128},{112,144}... | collective-permute-start | bytes 20 | tf_op jit(solution)/shard_map/cond/branch_1_fun/ppermute | solution.py:16
  146.1 15.1 %collective-permute-start.7 = (bf16[256,512]{1,0:T(8,128)(2,1)}, bf16[256,512]{1,0:T(8,128)(2,1)}, u32[]{:S(2)}, u32[]{:S(2)}) collective-permute-start(bf16[256,512]{1,0:T(8,128)(2,1)} %param.4), channel_id=1, source_target_pairs={{0,32},{16,48},{32,64},{48,80},{64,96},{80,112},{96,128},{112,144}... | collective-permute-start | bytes 786440 | tf_op jit(solution)/shard_map/cond/branch_1_fun/ppermute | solution.py:16
Sparse Core Ops, SparseCore 0:
  17.9 62.7 all-gather.2
  102.1 43.9 reduce-scatter.1

commit v13 on v10

--- a/solution.py
+++ b/solution.py
@@ -38,14 +38,18 @@
     full_params = gathered.reshape(-1, params.shape[1])
     act32 = activations[0].astype(jnp.float32)
     mean_sq = jnp.mean(act32 * act32, axis=1, keepdims=True)
-    normed = (act32 * lax.rsqrt(mean_sq + 1e-05) * gain[None, :]).astype(jnp.bfloat16)
+    scale = lax.rsqrt(mean_sq + 1e-05)
+    normed = (act32 * scale * gain[None, :]).astype(jnp.bfloat16)
     tokens = normed.shape[0]
     side = lax.axis_index("fl")
     flip = [(i, n_pair - 1 - i) for i in range(n_pair)]
     row_width = features // n_pair
     own_cols = lax.dynamic_slice_in_dim(normed, side * row_width, row_width, axis=1)
-    partner_cols = lax.dynamic_slice_in_dim(normed, (n_pair - 1 - side) * row_width, row_width, axis=1)
-    their_cols = lax.ppermute(partner_cols, "fl", flip)
+    raw_partner = lax.dynamic_slice_in_dim(activations[0], (n_pair - 1 - side) * row_width, row_width, axis=1)
+    their_raw = lax.ppermute(raw_partner, "fl", flip)
+    their_scale = lax.ppermute(scale, "fl", flip)
+    own_gain = lax.dynamic_slice_in_dim(gain, side * row_width, row_width)
+    their_cols = (their_raw.astype(jnp.float32) * their_scale * own_gain[None, :]).astype(jnp.bfloat16)
     contract = (((0,), (0,)), ((), ()))
     half = tokens // 2
     mine = theirs = None

time: 173 us -> 172 us (level)
  starting transfers between devices: 26.6 us -> 20.1 us
  waiting for transfers between devices: 96.6 us -> 101 us
  other arithmetic: 6.93 us -> 9.84 us
  matrix products: 11.4 us -> 8.71 us
    all_gather x1, waiting for transfers between devices: 52.8 us -> 19.4 us  [body(): gathered = lax.all_gather(gathered, 'fz', axis=1)]
    ppermute x1 -> x2, waiting for transfers between devices: 0.01 us -> 28.2 us  [the longest x1 28.2 us: body(): their_scale = lax.ppermute(scale, 'fl', flip)]
    reduce_scatter x1, waiting for transfers between devices: 14.5 us -> 26.2 us  [body(): grad16 = lax.psum_scatter(blocks, 'fz', scatter_dimension=0)]
    ppermute x3, starting transfers between devices: 17.2 us -> 8.25 us  [passed_along(): return lax.ppermute(value, axis, pairs)]
    convert_element_type x1 -> x2, other arithmetic: 1 us -> 5.78 us  [the longest x1 3.09 us: body(): (their_raw.astype(jnp.float32) * their_scale * own_gain[None, :]).astype(...]
    ppermute x3, waiting for transfers between devices: 26 us -> 21.5 us  [passed_along(): return lax.ppermute(value, axis, pairs)]
    ppermute x2, waiting for transfers between devices: 3.26 us -> 5.94 us  [body(): their_errors = lax.ppermute(errors, 'fl', flip)]
    dot_general x2, matrix products: 6.97 us -> 4.31 us  [body(): jnp.dot(normed[span], full_params, preferred_element_type=jnp.float32)]
  transfers between devices with their start and end apart: 8 -> 9, of which waited for: 5 -> 6; matrix products, arithmetic and copies ran while one was open for 8% -> 6% of each run, Pallas kernels for 0% -> 0%
where the time goes in v13:
time: 172 us; the launch traced here: 169 us
  waiting for transfers between devices  101 us (59%)
  starting transfers between devices  20.1 us (12%)
  between operations  17.3 us (10%)
  other arithmetic  9.84 us (6%)
  blocking collectives  8.82 us (5%)
  matrix products  8.71 us (5%)
  local copies, waits for them, and re-layouts  3.11 us (2%)
    ppermute x1, waiting for transfers between devices, body(): their_scale = lax.ppermute(scale, 'fl', flip)  28.2 us
    reduce_scatter x1, waiting for transfers between devices, body(): grad16 = lax.psum_scatter(blocks, 'fz', scatter_dimension=0)  26.2 us
    ppermute x3, waiting for transfers between devices, passed_along(): return lax.ppermute(value, axis, pairs)  21.5 us
    all_gather x1, waiting for transfers between devices, body(): gathered = lax.all_gather(gathered, 'fz', axis=1)  19.4 us
    all_gather x1, blocking collectives, body(): gathered = lax.all_gather(params, 'fl', axis=0)  8.82 us
    ppermute x3, starting transfers between devices, passed_along(): return lax.ppermute(value, axis, pairs)  8.25 us
    ppermute x2, starting transfers between devices, body(): their_errors = lax.ppermute(errors, 'fl', flip)  5.97 us
    ppermute x2, waiting for transfers between devices, body(): their_errors = lax.ppermute(errors, 'fl', flip)  5.94 us
  transfers between devices with their start and end apart: 9, of which 6 were waited for; matrix products, arithmetic and copies ran while one was open for 6% of the time, Pallas kernels for 0%

profile of v13, /device:TPU:6, one launch (start us, length us, event | category | flops | bytes accessed | tf_op | source)
XLA Modules:
  0.0 169.3 jit_solution(738772523115085665)
XLA Ops:
  7.2 0.0 all-gather.3.cloned.1.call-start
  8.0 1.2 divide_convert_fusion
  9.2 8.8 %all_gather.10 = bf16[2,256,512]{2,1,0:T(8,128)(2,1)} all-gather(bf16[1,256,512]{2,1,0:T(8,128)(2,1)S(1)} %divide_convert_fusion), channel_id=1, replica_groups=mesh['replica'=32,'fl'=2,'fz'=8] {'fl'}, dimensions={0}, use_global_device_ids=true | all-gather | bytes 786432 | tf_op jit(solution)/shard_map/all_gather | solution.py:36
  18.1 0.0 reduce-scatter.2.cloned.1.call-start
  18.1 2.8 %dynamic-slice_bitcast_fusion = bf16[384,2048]{1,0:T(8,128)(2,1)} fusion(bf16[1,384,4096]{2,1,0:T(8,128)(2,1)} %param.15, s32[]{:T(128)S(6)} %select_n.8), kind=kLoop, calls=%fused_computation.13 | loop fusion | bytes 3145732 | tf_op jit(solution)/shard_map/dynamic_slice | solution.py:48
  20.9 3.5 %collective-permute-start.9 = (bf16[384,2048]{1,0:T(8,128)(2,1)}, bf16[384,2048]{1,0:T(8,128)(2,1)}, u32[]{:S(2)}, u32[]{:S(2)}) collective-permute-start(bf16[384,2048]{1,0:T(8,128)(2,1)} %dynamic-slice_bitcast_fusion), channel_id=1, source_target_pairs={{0,8},{8,0},{1,9},{9,1},{2,10},{10,2},{3,11},{11,3},{4,12},{12,4},... | collective-permute-start | bytes 4718600 | tf_op jit(solution)/shard_map/ppermute | solution.py:49
  24.4 0.7 fusion
  25.1 2.4 %collective-permute-start.10 = (f32[384,1]{0,1:T(1,128)S(1)}, f32[384,1]{0,1:T(1,128)S(1)}, u32[]{:S(2)}, u32[]{:S(2)}) collective-permute-start(f32[384,1]{0,1:T(1,128)S(1)} %rsqrt.16), channel_id=1, source_target_pairs={{0,8},{8,0},{1,9},{9,1},{2,10},{10,2},{3,11},{11,3},{4,12},{12,4},... | collective-permute-start | bytes 4616 | tf_op jit(solution)/shard_map/ppermute | solution.py:50
  27.5 2.7 %fusion.2 = bf16[384,4096]{1,0:T(8,128)(2,1)} fusion(bf16[1,384,4096]{2,1,0:T(8,128)(2,1)S(1)} %copy-done, f32[4096]{0:T(1024)S(1)} %copy-done.4, f32[384]{0:T(512)S(1)} %add_rsqrt_fusion), kind=kLoop, calls=%fused_computation.4 | loop fusion | flops 6291456 | bytes 6309376 | tf_op jit(solution)/shard_map/convert_element_type | solution.py:42
  30.2 28.2 %collective-permute-done.10 = f32[384,1]{0,1:T(1,128)S(1)} collective-permute-done((f32[384,1]{0,1:T(1,128)S(1)}, f32[384,1]{0,1:T(1,128)S(1)}, u32[]{:S(2)}, u32[]{:S(2)}) %collective-permute-start.10) | collective-permute-done | bytes 1568 | tf_op jit(solution)/shard_map/ppermute | solution.py:50
  58.5 3.1 %multiply_convert_fusion = bf16[384,2048]{1,0:T(8,128)(2,1)} fusion(bf16[384,2048]{1,0:T(8,128)(2,1)} %collective-permute-done.9, f32[2048]{0:T(1024)S(1)} %dynamic_slice.14, f32[384]{0:T(512)S(1)} %reduce), kind=kLoop, calls=%fused_computation.8 | loop fusion | flops 3145728 | bytes 3155456 | tf_op jit(solution)/shard_map/convert_element_type | solution.py:52
  61.5 19.4 %all-gather.3.cloned.1.call-done = bf16[2,2048,512]{2,1,0:T(8,128)(2,1)} async-done(((bf16[2,256,512]{2,1,0:T(8,128)(2,1)}), bf16[2,2048,512]{2,1,0:T(8,128)(2,1)}) %all-gather.3.cloned.1.call-update) | async-done | bytes 4194320 | tf_op jit(solution)/shard_map/all_gather | solution.py:37
  81.0 3.3 %fusion.25 = bf16[192,512]{1,0:T(8,128)(2,1)S(1)} fusion(bf16[4096,512]{1,0:T(8,128)(2,1)} %bitcast.36, bf16[384,4096]{1,0:T(8,128)(2,1)S(1)} %copy-done.1, bf16[1,384,512]{2,1,0:T(8,128)(2,1)} %param.16), kind=kOutput, calls=%fused_computation.20 | convolution fusion | flops 805797888 | bytes 6160384 | tf_op jit(solution)/shard_map/dot_general | solution.py:58
  84.3 0.2 copy-done.5
  84.5 0.1 copy-done.6
  84.6 1.0 fusion.28
  85.6 0.8 fusion.35
  86.3 3.5 %collective-permute-start.11 = (bf16[192,512]{1,0:T(8,128)(2,1)S(1)}, bf16[192,512]{1,0:T(8,128)(2,1)S(1)}, u32[]{:S(2)}, u32[]{:S(2)}) collective-permute-start(bf16[192,512]{1,0:T(8,128)(2,1)S(1)} %fusion.25), channel_id=1, source_target_pairs={{0,8},{8,0},{1,9},{9,1},{2,10},{10,2},{3,11},{11,3},{4,12},{12,4},... | collective-permute-start | bytes 589832 | tf_op jit(solution)/shard_map/ppermute | solution.py:62
  89.9 2.4 %collective-permute-start.12 = (bf16[192,512]{1,0:T(8,128)(2,1)S(1)}, bf16[192,512]{1,0:T(8,128)(2,1)S(1)}, u32[]{:S(2)}, u32[]{:S(2)}) collective-permute-start(bf16[192,512]{1,0:T(8,128)(2,1)S(1)} %fusion.28), channel_id=1, source_target_pairs={{0,8},{8,0},{1,9},{9,1},{2,10},{10,2},{3,11},{11,3},{4,12},{12,4},... | collective-permute-start | bytes 589832 | tf_op jit(solution)/shard_map/ppermute | solution.py:62
  92.3 0.8 add_convert_fusion.2
  93.1 5.9 %collective-permute-done.12 = bf16[192,512]{1,0:T(8,128)(2,1)S(1)} collective-permute-done((bf16[192,512]{1,0:T(8,128)(2,1)S(1)}, bf16[192,512]{1,0:T(8,128)(2,1)S(1)}, u32[]{:S(2)}, u32[]{:S(2)}) %collective-permute-start.12) | collective-permute-done | bytes 196640 | tf_op jit(solution)/shard_map/ppermute | solution.py:62
  99.1 0.8 fusion.31
  99.9 2.1 %add_convert_fusion = bf16[2048,512]{1,0:T(8,128)(2,1)} fusion(bf16[2048,512]{1,0:T(8,128)(2,1)S(1)} %add_convert_fusion.2, f32[2048,512]{1,0:T(8,128)S(1)} %fusion.31, bf16[192,512]{1,0:T(8,128)(2,1)S(1)} %collective-permute-done.11, bf16[384,2048]{1,0:T(8,128)(2,1)S(1)} %copy-done.2), kind=kOutput, calls=%fused_computation.5 | convolution fusion | flops 408944640 | bytes 9371648 | tf_op jit(solution)/shard_map/dot_general | solution.py:64
  102.6 16.7 %conditional.5 = (f32[256,512]{1,0:T(8,128)}, f32[1]{0:T(128)}) conditional(s32[]{:T(128)} %bitcast.10, (f32[256,512]{1,0:T(8,128)S(1)}, f32[1]{0:T(128)}) %tuple.57, (f32[256,512]{1,0:T(8,128)S(1)}, f32[1]{0:T(128)}) %tuple.58, (f32[256,512]{1,0:T(8,128)S(1)}, f32[1]{0:T(128)}) %tuple.59), branch_computations={%region_2.0_spmd, %region_3.0_spmd, %region_4.0_spmd} | conditional | bytes 2097264 | solution.py:25
  102.6 1.9 %collective-permute-start = (f32[256,512]{1,0:T(8,128)S(1)}, f32[256,512]{1,0:T(8,128)}, u32[]{:S(2)}, u32[]{:S(2)}) collective-permute-start(f32[256,512]{1,0:T(8,128)S(1)} %get-tuple-element.25), channel_id=1, source_target_pairs={{0,16},{16,32},{32,48},{48,64},{64,80},{80,96},{96,112},{112,128},... | collective-permute-start | bytes 1572872 | tf_op jit(solution)/shard_map/cond/branch_0_fun/ppermute | solution.py:16
  104.6 4.4 %collective-permute-start.1 = (f32[1]{0:T(128)}, f32[1]{0:T(128)}, u32[]{:S(2)}, u32[]{:S(2)}) collective-permute-start(f32[1]{0:T(128)} %get-tuple-element.26), channel_id=1, source_target_pairs={{0,16},{16,32},{32,48},{48,64},{64,80},{80,96},{96,112},{112,128},... | collective-permute-start | bytes 20 | tf_op jit(solution)/shard_map/cond/branch_0_fun/ppermute | solution.py:16
  109.0 10.4 %collective-permute-done.1 = f32[1]{0:T(128)} collective-permute-done((f32[1]{0:T(128)}, f32[1]{0:T(128)}, u32[]{:S(2)}, u32[]{:S(2)}) %collective-permute-start.1) | collective-permute-done | bytes 36 | tf_op jit(solution)/shard_map/cond/branch_0_fun/ppermute | solution.py:16
  119.9 26.2 %reduce-scatter.2.cloned.1.call-done = bf16[1,256,512]{2,1,0:T(8,128)(2,1)} async-done(((bf16[8,256,512]{2,1,0:T(8,128)(2,1)}), bf16[1,256,512]{2,1,0:T(8,128)(2,1)}) %reduce-scatter.2.cloned.1.call-update) | async-done | bytes 262160 | tf_op jit(solution)/shard_map/reduce_scatter | solution.py:73
  146.1 13.1 %conditional.6 = (bf16[256,512]{1,0:T(8,128)(2,1)}) conditional(s32[]{:T(128)} %bitcast.10, bf16[256,512]{1,0:T(8,128)(2,1)} %bitcast.33, bf16[256,512]{1,0:T(8,128)(2,1)} %bitcast.34, bf16[256,512]{1,0:T(8,128)(2,1)} %bitcast.35), branch_computations={%region_5.0_spmd, %region_6.0_spmd, %region_7.0_spmd} | conditional | bytes 1048624
  146.1 1.9 %collective-permute-start.6 = (bf16[256,512]{1,0:T(8,128)(2,1)}, bf16[256,512]{1,0:T(8,128)(2,1)}, u32[]{:S(2)}, u32[]{:S(2)}) collective-permute-start(bf16[256,512]{1,0:T(8,128)(2,1)} %param.3), channel_id=1, source_target_pairs={{0,16},{16,32},{32,48},{48,64},{64,80},{80,96},{96,112},{112,128},... | collective-permute-start | bytes 786440 | tf_op jit(solution)/shard_map/cond/branch_0_fun/ppermute | solution.py:16
  148.0 11.1 %collective-permute-done.6 = bf16[256,512]{1,0:T(8,128)(2,1)} collective-permute-done((bf16[256,512]{1,0:T(8,128)(2,1)}, bf16[256,512]{1,0:T(8,128)(2,1)}, u32[]{:S(2)}, u32[]{:S(2)}) %collective-permute-start.6) | collective-permute-done | bytes 262176 | tf_op jit(solution)/shard_map/cond/branch_0_fun/ppermute | solution.py:16
  159.2 2.1 %multiply_bitcast_fusion = f32[1,256,512]{2,1,0:T(8,128)} fusion(f32[256,512]{1,0:T(8,128)} %get-tuple-element.41, bf16[256,512]{1,0:T(8,128)(2,1)} %get-tuple-element.49, bf16[1,256,512]{2,1,0:T(8,128)(2,1)} %reduce-scatter.2.cloned.1.call-done, f32[1,256,512]{2,1,0:T(8,128)S(1)} %copy-done.3), kind=kLoop, calls=%fused_computation.28 | loop fusion | flops 1048576 | bytes 2097152 | tf_op jit(solution)/shard_map/broadcast_in_dim | solution.py:79
  (21 shorter events, 0.1 us)
Async XLA Ops:
  7.2 17.3 %copy-start = (bf16[1,384,4096]{2,1,0:T(8,128)(2,1)S(1)}, bf16[1,384,4096]{2,1,0:T(8,128)(2,1)}, u32[]{:S(2)}) copy-start(bf16[1,384,4096]{2,1,0:T(8,128)(2,1)} %param.15) | copy-start | bytes 9437188
  7.2 73.8 %all-gather.3.cloned.1.call-start = ((), (), s32[]{:S(2)}) async-start(), calls=%async_computation.2 | async-start | bytes 4718592 | tf_op jit(solution)/shard_map/all_gather | solution.py:37
  18.1 128.1 %reduce-scatter.2.cloned.1.call-start = ((), (), s32[]{:S(2)}) async-start(), calls=%async_computation.1 | async-start | bytes 2359296 | tf_op jit(solution)/shard_map/reduce_scatter | solution.py:73
  18.1 9.4 %copy-start.4 = (f32[4096]{0:T(1024)S(1)}, f32[4096]{0:T(1024)}, u32[]{:S(2)}) copy-start(f32[4096]{0:T(1024)} %param.17) | copy-start | bytes 49156
  20.9 37.5 %collective-permute-start.9 = (bf16[384,2048]{1,0:T(8,128)(2,1)}, bf16[384,2048]{1,0:T(8,128)(2,1)}, u32[]{:S(2)}, u32[]{:S(2)}) collective-permute-start(bf16[384,2048]{1,0:T(8,128)(2,1)} %dynamic-slice_bitcast_fusion), channel_id=1, source_target_pairs={{0,8},{8,0},{1,9},{9,1},{2,10},{10,2},{3,11},{11,3},{4,12},{12,4},... | collective-permute-start | bytes 4718600 | tf_op jit(solution)/shard_map/ppermute | solution.py:49
  25.1 33.3 %collective-permute-start.10 = (f32[384,1]{0,1:T(1,128)S(1)}, f32[384,1]{0,1:T(1,128)S(1)}, u32[]{:S(2)}, u32[]{:S(2)}) collective-permute-start(f32[384,1]{0,1:T(1,128)S(1)} %rsqrt.16), channel_id=1, source_target_pairs={{0,8},{8,0},{1,9},{9,1},{2,10},{10,2},{3,11},{11,3},{4,12},{12,4},... | collective-permute-start | bytes 4616 | tf_op jit(solution)/shard_map/ppermute | solution.py:50
  30.2 50.8 %copy-start.1 = (bf16[384,4096]{1,0:T(8,128)(2,1)S(1)}, bf16[384,4096]{1,0:T(8,128)(2,1)}, u32[]{:S(2)}) copy-start(bf16[384,4096]{1,0:T(8,128)(2,1)} %fusion.2) | copy-start | bytes 9437188
  81.0 3.5 %copy-start.5 = (bf16[2,2048,512]{2,1,0:T(8,128)(2,1)S(1)}, bf16[2,2048,512]{2,1,0:T(8,128)(2,1)}, u32[]{:S(2)}) copy-start(bf16[2,2048,512]{2,1,0:T(8,128)(2,1)} %all-gather.3.cloned.1.call-done) | copy-start | bytes 12582916
  81.0 3.6 %copy-start.6 = (bf16[1,384,512]{2,1,0:T(8,128)(2,1)S(1)}, bf16[1,384,512]{2,1,0:T(8,128)(2,1)}, u32[]{:S(2)}) copy-start(bf16[1,384,512]{2,1,0:T(8,128)(2,1)} %param.16) | copy-start | bytes 1179652
  86.3 12.7 %copy-start.2 = (bf16[384,2048]{1,0:T(8,128)(2,1)S(1)}, bf16[384,2048]{1,0:T(8,128)(2,1)}, u32[]{:S(2)}) copy-start(bf16[384,2048]{1,0:T(8,128)(2,1)} %multiply_convert_fusion) | copy-start | bytes 4718596
  86.3 13.5 %collective-permute-start.11 = (bf16[192,512]{1,0:T(8,128)(2,1)S(1)}, bf16[192,512]{1,0:T(8,128)(2,1)S(1)}, u32[]{:S(2)}, u32[]{:S(2)}) collective-permute-start(bf16[192,512]{1,0:T(8,128)(2,1)S(1)} %fusion.25), channel_id=1, source_target_pairs={{0,8},{8,0},{1,9},{9,1},{2,10},{10,2},{3,11},{11,3},{4,12},{12,4},... | collective-permute-start | bytes 589832 | tf_op jit(solution)/shard_map/ppermute | solution.py:62
  89.9 9.2 %collective-permute-start.12 = (bf16[192,512]{1,0:T(8,128)(2,1)S(1)}, bf16[192,512]{1,0:T(8,128)(2,1)S(1)}, u32[]{:S(2)}, u32[]{:S(2)}) collective-permute-start(bf16[192,512]{1,0:T(8,128)(2,1)S(1)} %fusion.28), channel_id=1, source_target_pairs={{0,8},{8,0},{1,9},{9,1},{2,10},{10,2},{3,11},{11,3},{4,12},{12,4},... | collective-permute-start | bytes 589832 | tf_op jit(solution)/shard_map/ppermute | solution.py:62
  99.8 2.8 %copy-start.3 = (f32[1,256,512]{2,1,0:T(8,128)S(1)}, f32[1,256,512]{2,1,0:T(8,128)}, u32[]{:S(2)}) copy-start(f32[1,256,512]{2,1,0:T(8,128)} %param.12) | copy-start | bytes 1572868
  102.6 16.7 %collective-permute-start = (f32[256,512]{1,0:T(8,128)S(1)}, f32[256,512]{1,0:T(8,128)}, u32[]{:S(2)}, u32[]{:S(2)}) collective-permute-start(f32[256,512]{1,0:T(8,128)S(1)} %get-tuple-element.25), channel_id=1, source_target_pairs={{0,16},{16,32},{32,48},{48,64},{64,80},{80,96},{96,112},{112,128},... | collective-permute-start | bytes 1572872 | tf_op jit(solution)/shard_map/cond/branch_0_fun/ppermute | solution.py:16
  104.6 14.8 %collective-permute-start.1 = (f32[1]{0:T(128)}, f32[1]{0:T(128)}, u32[]{:S(2)}, u32[]{:S(2)}) collective-permute-start(f32[1]{0:T(128)} %get-tuple-element.26), channel_id=1, source_target_pairs={{0,16},{16,32},{32,48},{48,64},{64,80},{80,96},{96,112},{112,128},... | collective-permute-start | bytes 20 | tf_op jit(solution)/shard_map/cond/branch_0_fun/ppermute | solution.py:16
  146.1 13.1 %collective-permute-start.6 = (bf16[256,512]{1,0:T(8,128)(2,1)}, bf16[256,512]{1,0:T(8,128)(2,1)}, u32[]{:S(2)}, u32[]{:S(2)}) collective-permute-start(bf16[256,512]{1,0:T(8,128)(2,1)} %param.3), channel_id=1, source_target_pairs={{0,16},{16,32},{32,48},{48,64},{64,80},{80,96},{96,112},{112,128},... | collective-permute-start | bytes 786440 | tf_op jit(solution)/shard_map/cond/branch_0_fun/ppermute | solution.py:16
Sparse Core Ops, SparseCore 0:
  18.2 62.7 all-gather.2
  102.1 43.9 reduce-scatter.1

commit v14 on v10

--- a/solution.py
+++ b/solution.py
@@ -67,10 +67,9 @@
     early, weight, blocks = lax.optimization_barrier((numer, push_weights, blocks))
     peer_numer, peer_weight = to_peer(send_to_peer, (early, weight), power)
     grad16 = lax.psum_scatter(blocks, "fz", scatter_dimension=0)
+    numer_mean, grad16 = lax.optimization_barrier((0.5 * (numer + peer_numer), grad16))
     peer_grad16 = to_peer(send_to_peer, grad16, power)
-    updated = numer - 0.3 * grad16.astype(jnp.float32)
-    peer_updated = peer_numer - 0.3 * peer_grad16.astype(jnp.float32)
-    mixed_numerators = 0.5 * (updated + peer_updated)
+    mixed_numerators = numer_mean - 0.15 * (grad16.astype(jnp.float32) + peer_grad16.astype(jnp.float32))
     mixed_weights = 0.5 * (push_weights + peer_weight)
     return (mixed_numerators[None], mixed_weights)
 

time: 173 us -> 170 us (0.983)
  starting transfers between devices: 26.6 us -> 17.6 us
  waiting for transfers between devices: 96.6 us -> 102 us
    reduce_scatter x1, waiting for transfers between devices: 14.5 us -> 26 us  [body(): grad16 = lax.psum_scatter(blocks, 'fz', scatter_dimension=0)]
    ppermute x3, starting transfers between devices: 17.2 us -> 8.26 us  [passed_along(): return lax.ppermute(value, axis, pairs)]
    ppermute x3, waiting for transfers between devices: 26 us -> 19.6 us  [passed_along(): return lax.ppermute(value, axis, pairs)]
  transfers between devices with their start and end apart: 8 -> 8, of which waited for: 5 -> 5; matrix products, arithmetic and copies ran while one was open for 8% -> 9% of each run, Pallas kernels for 0% -> 0%
where the time goes in v14:
time: 170 us; the launch traced here: 168 us
  waiting for transfers between devices  102 us (60%)
  starting transfers between devices  17.6 us (10%)
  between operations  17.3 us (10%)
  matrix products  11.4 us (7%)
  blocking collectives  8.82 us (5%)
  other arithmetic  7.84 us (5%)
  local copies, waits for them, and re-layouts  3.03 us (2%)
    all_gather x1, waiting for transfers between devices, body(): gathered = lax.all_gather(gathered, 'fz', axis=1)  52.8 us
    reduce_scatter x1, waiting for transfers between devices, body(): grad16 = lax.psum_scatter(blocks, 'fz', scatter_dimension=0)  26 us
    ppermute x3, waiting for transfers between devices, passed_along(): return lax.ppermute(value, axis, pairs)  19.6 us
    all_gather x1, blocking collectives, body(): gathered = lax.all_gather(params, 'fl', axis=0)  8.82 us
    ppermute x3, starting transfers between devices, passed_along(): return lax.ppermute(value, axis, pairs)  8.26 us
    dot_general x2, matrix products, body(): jnp.dot(normed[span], full_params, preferred_element_type=jnp.float32)  7.01 us
    ppermute x2, starting transfers between devices, body(): their_errors = lax.ppermute(errors, 'fl', flip)  5.84 us
    ppermute x1, starting transfers between devices, body(): their_cols = lax.ppermute(partner_cols, 'fl', flip)  3.47 us
  transfers between devices with their start and end apart: 8, of which 5 were waited for; matrix products, arithmetic and copies ran while one was open for 9% of the time, Pallas kernels for 0%

profile of v14, /device:TPU:6, one launch (start us, length us, event | category | flops | bytes accessed | tf_op | source)
XLA Modules:
  0.0 167.9 jit_solution(947982615437136373)
XLA Ops:
  7.2 0.0 copy-start
  7.2 0.0 all-gather.3.cloned.1.call-start
  8.0 1.2 divide_convert_fusion
  9.2 8.8 %all_gather.10 = bf16[2,256,512]{2,1,0:T(8,128)(2,1)} all-gather(bf16[1,256,512]{2,1,0:T(8,128)(2,1)S(1)} %divide_convert_fusion), channel_id=1, replica_groups=mesh['replica'=32,'fl'=2,'fz'=8] {'fl'}, dimensions={0}, use_global_device_ids=true | all-gather | bytes 786432 | tf_op jit(solution)/shard_map/all_gather | solution.py:36
  18.0 0.0 all-gather.3.cloned.1.call-update
  18.1 0.0 reduce-scatter.2.cloned.1.call-start
  18.1 2.6 %fusion = f32[384]{0:T(512)S(1)} fusion(bf16[1,384,4096]{2,1,0:T(8,128)(2,1)} %param.15), kind=kLoop, calls=%fused_computation.2 | loop fusion | flops 4718208 | bytes 3147264 | tf_op jit(solution)/shard_map/reduce_sum | solution.py:40
  20.7 1.0 fusion.2
  21.8 1.7 copy-done.1
  23.4 1.3 constant_dynamic-slice_fusion
  24.8 3.5 %collective-permute-start.9 = (bf16[384,2048]{1,0:T(8,128)(2,1)}, bf16[384,2048]{1,0:T(8,128)(2,1)S(1)}, u32[]{:S(2)}, u32[]{:S(2)}) collective-permute-start(bf16[384,2048]{1,0:T(8,128)(2,1)} %constant_dynamic-slice_fusion), channel_id=1, source_target_pairs={{0,8},{8,0},{1,9},{9,1},{2,10},{10,2},{3,11},{11,3},{4,12},{12,4},... | collective-permute-start | bytes 4718600 | tf_op jit(solution)/shard_map/ppermute | solution.py:48
  28.2 52.8 %all-gather.3.cloned.1.call-done = bf16[2,2048,512]{2,1,0:T(8,128)(2,1)} async-done(((bf16[2,256,512]{2,1,0:T(8,128)(2,1)}), bf16[2,2048,512]{2,1,0:T(8,128)(2,1)}) %all-gather.3.cloned.1.call-update) | async-done | bytes 4194320 | tf_op jit(solution)/shard_map/all_gather | solution.py:37
  81.0 3.8 %fusion.28 = bf16[192,512]{1,0:T(8,128)(2,1)S(1)} fusion(bf16[4096,512]{1,0:T(8,128)(2,1)} %bitcast.34, bf16[384,4096]{1,0:T(8,128)(2,1)} %copy-done.1, bf16[1,384,512]{2,1,0:T(8,128)(2,1)S(1)} %copy-done.5), kind=kOutput, calls=%fused_computation.19 | convolution fusion | flops 805797888 | bytes 6160384 | tf_op jit(solution)/shard_map/dot_general | solution.py:54
  84.8 3.4 %collective-permute-start.11 = (bf16[192,512]{1,0:T(8,128)(2,1)S(1)}, bf16[192,512]{1,0:T(8,128)(2,1)S(1)}, u32[]{:S(2)}, u32[]{:S(2)}) collective-permute-start(bf16[192,512]{1,0:T(8,128)(2,1)S(1)} %fusion.28), channel_id=1, source_target_pairs={{0,8},{8,0},{1,9},{9,1},{2,10},{10,2},{3,11},{11,3},{4,12},{12,4},... | collective-permute-start | bytes 589832 | tf_op jit(solution)/shard_map/ppermute | solution.py:58
  88.2 3.2 %fusion.25 = bf16[192,512]{1,0:T(8,128)(2,1)S(1)} fusion(bf16[4096,512]{1,0:T(8,128)(2,1)} %bitcast.35, bf16[384,4096]{1,0:T(8,128)(2,1)S(1)} %copy-done.2, bf16[1,384,512]{2,1,0:T(8,128)(2,1)S(1)} %copy-done.5), kind=kOutput, calls=%fused_computation.18 | convolution fusion | flops 805797888 | bytes 6160384 | tf_op jit(solution)/shard_map/dot_general | solution.py:54
  91.5 2.4 %collective-permute-start.10 = (bf16[192,512]{1,0:T(8,128)(2,1)S(1)}, bf16[192,512]{1,0:T(8,128)(2,1)S(1)}, u32[]{:S(2)}, u32[]{:S(2)}) collective-permute-start(bf16[192,512]{1,0:T(8,128)(2,1)S(1)} %fusion.25), channel_id=1, source_target_pairs={{0,8},{8,0},{1,9},{9,1},{2,10},{10,2},{3,11},{11,3},{4,12},{12,4},... | collective-permute-start | bytes 589832 | tf_op jit(solution)/shard_map/ppermute | solution.py:58
  93.9 0.8 fusion.35
  94.7 0.8 add_convert_fusion.2
  95.5 0.8 fusion.31
  96.2 3.3 %collective-permute-done.10 = bf16[192,512]{1,0:T(8,128)(2,1)S(1)} collective-permute-done((bf16[192,512]{1,0:T(8,128)(2,1)S(1)}, bf16[192,512]{1,0:T(8,128)(2,1)S(1)}, u32[]{:S(2)}, u32[]{:S(2)}) %collective-permute-start.10) | collective-permute-done | bytes 196640 | tf_op jit(solution)/shard_map/ppermute | solution.py:58
  99.5 2.1 %add_convert_fusion = bf16[2048,512]{1,0:T(8,128)(2,1)} fusion(bf16[2048,512]{1,0:T(8,128)(2,1)S(1)} %add_convert_fusion.2, f32[2048,512]{1,0:T(8,128)S(1)} %fusion.31, bf16[192,512]{1,0:T(8,128)(2,1)S(1)} %collective-permute-done.10, bf16[384,2048]{1,0:T(8,128)(2,1)S(1)} %collective-permute-done.9), kind=kOutput, calls=%fused_computation.5 | convolution fusion | flops 408944640 | bytes 9371648 | tf_op jit(solution)/shard_map/dot_general | solution.py:60
  101.6 0.0 reduce-scatter.2.cloned.1.call-update
  102.3 14.9 %conditional.5 = (f32[256,512]{1,0:T(8,128)}, f32[1]{0:T(128)}) conditional(s32[]{:T(128)} %bitcast.1, (f32[256,512]{1,0:T(8,128)S(1)}, f32[1]{0:T(128)}) %tuple.59, (f32[256,512]{1,0:T(8,128)S(1)}, f32[1]{0:T(128)}) %tuple.60, (f32[256,512]{1,0:T(8,128)S(1)}, f32[1]{0:T(128)}) %tuple.61), branch_computations={%region_1.0_spmd, %region_2.0_spmd, %region_3.0_spmd} | conditional | bytes 2097264 | solution.py:25
  102.3 1.9 %collective-permute-start = (f32[256,512]{1,0:T(8,128)S(1)}, f32[256,512]{1,0:T(8,128)}, u32[]{:S(2)}, u32[]{:S(2)}) collective-permute-start(f32[256,512]{1,0:T(8,128)S(1)} %get-tuple-element.25), channel_id=1, source_target_pairs={{0,16},{16,32},{32,48},{48,64},{64,80},{80,96},{96,112},{112,128},... | collective-permute-start | bytes 1572872 | tf_op jit(solution)/shard_map/cond/branch_0_fun/ppermute | solution.py:16
  104.3 4.4 %collective-permute-start.1 = (f32[1]{0:T(128)}, f32[1]{0:T(128)}, u32[]{:S(2)}, u32[]{:S(2)}) collective-permute-start(f32[1]{0:T(128)} %get-tuple-element.26), channel_id=1, source_target_pairs={{0,16},{16,32},{32,48},{48,64},{64,80},{80,96},{96,112},{112,128},... | collective-permute-start | bytes 20 | tf_op jit(solution)/shard_map/cond/branch_0_fun/ppermute | solution.py:16
  108.7 8.5 %collective-permute-done.1 = f32[1]{0:T(128)} collective-permute-done((f32[1]{0:T(128)}, f32[1]{0:T(128)}, u32[]{:S(2)}, u32[]{:S(2)}) %collective-permute-start.1) | collective-permute-done | bytes 36 | tf_op jit(solution)/shard_map/cond/branch_0_fun/ppermute | solution.py:16
  117.8 1.1 add_multiply_fusion
  119.0 26.0 %reduce-scatter.2.cloned.1.call-done = bf16[1,256,512]{2,1,0:T(8,128)(2,1)} async-done(((bf16[8,256,512]{2,1,0:T(8,128)(2,1)}), bf16[1,256,512]{2,1,0:T(8,128)(2,1)}) %reduce-scatter.2.cloned.1.call-update) | async-done | bytes 262160 | tf_op jit(solution)/shard_map/reduce_scatter | solution.py:69
  145.0 13.0 %conditional.6 = (bf16[256,512]{1,0:T(8,128)(2,1)}) conditional(s32[]{:T(128)} %bitcast.1, bf16[256,512]{1,0:T(8,128)(2,1)} %bitcast.30, bf16[256,512]{1,0:T(8,128)(2,1)} %bitcast.31, bf16[256,512]{1,0:T(8,128)(2,1)} %bitcast.32), branch_computations={%region_5.0_spmd, %region_6.0_spmd, %region_7.0_spmd} | conditional | bytes 1048624
  145.0 1.9 %collective-permute-start.6 = (bf16[256,512]{1,0:T(8,128)(2,1)}, bf16[256,512]{1,0:T(8,128)(2,1)}, u32[]{:S(2)}, u32[]{:S(2)}) collective-permute-start(bf16[256,512]{1,0:T(8,128)(2,1)} %param.3), channel_id=1, source_target_pairs={{0,16},{16,32},{32,48},{48,64},{64,80},{80,96},{96,112},{112,128},... | collective-permute-start | bytes 786440 | tf_op jit(solution)/shard_map/cond/branch_0_fun/ppermute | solution.py:16
  146.9 11.1 %collective-permute-done.6 = bf16[256,512]{1,0:T(8,128)(2,1)} collective-permute-done((bf16[256,512]{1,0:T(8,128)(2,1)}, bf16[256,512]{1,0:T(8,128)(2,1)}, u32[]{:S(2)}, u32[]{:S(2)}) %collective-permute-start.6) | collective-permute-done | bytes 262176 | tf_op jit(solution)/shard_map/cond/branch_0_fun/ppermute | solution.py:16
  158.0 1.9 %subtract_bitcast_fusion = f32[1,256,512]{2,1,0:T(8,128)} fusion(f32[256,512]{1,0:T(8,128)S(1)} %add_multiply_fusion, bf16[256,512]{1,0:T(8,128)(2,1)} %get-tuple-element.53, bf16[256,512]{1,0:T(8,128)(2,1)} %bitcast.33), kind=kLoop, calls=%fused_computation.26 | loop fusion | flops 655360 | bytes 1572864 | tf_op jit(solution)/shard_map/broadcast_in_dim | solution.py:74
  (14 shorter events, 0.0 us)
Async XLA Ops:
  7.2 13.6 %copy-start = (bf16[1,384,4096]{2,1,0:T(8,128)(2,1)S(1)}, bf16[1,384,4096]{2,1,0:T(8,128)(2,1)}, u32[]{:S(2)}) copy-start(bf16[1,384,4096]{2,1,0:T(8,128)(2,1)} %param.15) | copy-start | bytes 9437188
  7.2 13.6 %copy-start.4 = (f32[4096]{0:T(1024)S(1)}, f32[4096]{0:T(1024)}, u32[]{:S(2)}) copy-start(f32[4096]{0:T(1024)} %param.17) | copy-start | bytes 49156
  7.2 73.8 %all-gather.3.cloned.1.call-start = ((), (), s32[]{:S(2)}) async-start(), calls=%async_computation.2 | async-start | bytes 4718592 | tf_op jit(solution)/shard_map/all_gather | solution.py:37
  18.1 126.9 %reduce-scatter.2.cloned.1.call-start = ((), (), s32[]{:S(2)}) async-start(), calls=%async_computation.1 | async-start | bytes 2359296 | tf_op jit(solution)/shard_map/reduce_scatter | solution.py:69
  21.7 1.7 %copy-start.1 = (bf16[384,4096]{1,0:T(8,128)(2,1)}, bf16[384,4096]{1,0:T(8,128)(2,1)S(1)}, u32[]{:S(2)}) copy-start(bf16[384,4096]{1,0:T(8,128)(2,1)S(1)} %fusion.2) | copy-start | bytes 9437188
  23.4 57.6 %copy-start.5 = (bf16[1,384,512]{2,1,0:T(8,128)(2,1)S(1)}, bf16[1,384,512]{2,1,0:T(8,128)(2,1)}, u32[]{:S(2)}) copy-start(bf16[1,384,512]{2,1,0:T(8,128)(2,1)} %param.16) | copy-start | bytes 1179652
  24.8 70.7 %collective-permute-start.9 = (bf16[384,2048]{1,0:T(8,128)(2,1)}, bf16[384,2048]{1,0:T(8,128)(2,1)S(1)}, u32[]{:S(2)}, u32[]{:S(2)}) collective-permute-start(bf16[384,2048]{1,0:T(8,128)(2,1)} %constant_dynamic-slice_fusion), channel_id=1, source_target_pairs={{0,8},{8,0},{1,9},{9,1},{2,10},{10,2},{3,11},{11,3},{4,12},{12,4},... | collective-permute-start | bytes 4718600 | tf_op jit(solution)/shard_map/ppermute | solution.py:48
  81.0 7.2 %copy-start.2 = (bf16[384,4096]{1,0:T(8,128)(2,1)S(1)}, bf16[384,4096]{1,0:T(8,128)(2,1)}, u32[]{:S(2)}) copy-start(bf16[384,4096]{1,0:T(8,128)(2,1)} %copy-done.1) | copy-start | bytes 9437188
  84.8 10.6 %collective-permute-start.11 = (bf16[192,512]{1,0:T(8,128)(2,1)S(1)}, bf16[192,512]{1,0:T(8,128)(2,1)S(1)}, u32[]{:S(2)}, u32[]{:S(2)}) collective-permute-start(bf16[192,512]{1,0:T(8,128)(2,1)S(1)} %fusion.28), channel_id=1, source_target_pairs={{0,8},{8,0},{1,9},{9,1},{2,10},{10,2},{3,11},{11,3},{4,12},{12,4},... | collective-permute-start | bytes 589832 | tf_op jit(solution)/shard_map/ppermute | solution.py:58
  91.5 8.1 %collective-permute-start.10 = (bf16[192,512]{1,0:T(8,128)(2,1)S(1)}, bf16[192,512]{1,0:T(8,128)(2,1)S(1)}, u32[]{:S(2)}, u32[]{:S(2)}) collective-permute-start(bf16[192,512]{1,0:T(8,128)(2,1)S(1)} %fusion.25), channel_id=1, source_target_pairs={{0,8},{8,0},{1,9},{9,1},{2,10},{10,2},{3,11},{11,3},{4,12},{12,4},... | collective-permute-start | bytes 589832 | tf_op jit(solution)/shard_map/ppermute | solution.py:58
  96.2 6.1 %copy-start.3 = (f32[1,256,512]{2,1,0:T(8,128)S(1)}, f32[1,256,512]{2,1,0:T(8,128)}, u32[]{:S(2)}) copy-start(f32[1,256,512]{2,1,0:T(8,128)} %param.12) | copy-start | bytes 1572868
  102.3 14.9 %collective-permute-start = (f32[256,512]{1,0:T(8,128)S(1)}, f32[256,512]{1,0:T(8,128)}, u32[]{:S(2)}, u32[]{:S(2)}) collective-permute-start(f32[256,512]{1,0:T(8,128)S(1)} %get-tuple-element.25), channel_id=1, source_target_pairs={{0,16},{16,32},{32,48},{48,64},{64,80},{80,96},{96,112},{112,128},... | collective-permute-start | bytes 1572872 | tf_op jit(solution)/shard_map/cond/branch_0_fun/ppermute | solution.py:16
  104.3 13.0 %collective-permute-start.1 = (f32[1]{0:T(128)}, f32[1]{0:T(128)}, u32[]{:S(2)}, u32[]{:S(2)}) collective-permute-start(f32[1]{0:T(128)} %get-tuple-element.26), channel_id=1, source_target_pairs={{0,16},{16,32},{32,48},{48,64},{64,80},{80,96},{96,112},{112,128},... | collective-permute-start | bytes 20 | tf_op jit(solution)/shard_map/cond/branch_0_fun/ppermute | solution.py:16
  145.0 13.0 %collective-permute-start.6 = (bf16[256,512]{1,0:T(8,128)(2,1)}, bf16[256,512]{1,0:T(8,128)(2,1)}, u32[]{:S(2)}, u32[]{:S(2)}) collective-permute-start(bf16[256,512]{1,0:T(8,128)(2,1)} %param.3), channel_id=1, source_target_pairs={{0,16},{16,32},{32,48},{48,64},{64,80},{80,96},{96,112},{112,128},... | collective-permute-start | bytes 786440 | tf_op jit(solution)/shard_map/cond/branch_0_fun/ppermute | solution.py:16
Sparse Core Ops, SparseCore 0:
  18.2 62.7 all-gather.2
  101.8 43.1 reduce-scatter.1

commit v15 on v14

--- a/solution.py
+++ b/solution.py
@@ -47,10 +47,9 @@
     partner_cols = lax.dynamic_slice_in_dim(normed, (n_pair - 1 - side) * row_width, row_width, axis=1)
     their_cols = lax.ppermute(partner_cols, "fl", flip)
     contract = (((0,), (0,)), ((), ()))
-    half = tokens // 2
+    cut = tokens * 2 // 3
     mine = theirs = None
-    for part in range(2):
-        span = slice(part * half, (part + 1) * half)
+    for span in (slice(0, cut), slice(cut, tokens)):
         keys = jnp.dot(normed[span], full_params, preferred_element_type=jnp.float32) / math.sqrt(features)
         errors = ((keys - targets[0, span].astype(jnp.float32)) / math.sqrt(replica_tokens)).astype(
             jnp.bfloat16

time: 170 us -> 172 us (1.012)
  starting transfers between devices: 17.6 us -> 22.4 us
    ppermute x3, starting transfers between devices: 8.26 us -> 13 us  [passed_along(): return lax.ppermute(value, axis, pairs)]
    reduce_scatter x1, waiting for transfers between devices: 26 us -> 21.5 us  [body(): grad16 = lax.psum_scatter(blocks, 'fz', scatter_dimension=0)]
    dot_general x2, matrix products: 7.01 us -> 4.32 us  [body(): jnp.dot(normed[span], full_params, preferred_element_type=jnp.float32)]
    dot_general x2, matrix products: 2.87 us -> 5.14 us  [body(): lax.dot_general(their_cols[span], their_errors, contract, preferred_eleme...]
    ppermute x3, waiting for transfers between devices: 19.6 us -> 21.6 us  [passed_along(): return lax.ppermute(value, axis, pairs)]
  transfers between devices with their start and end apart: 8 -> 8, of which waited for: 5 -> 5; matrix products, arithmetic and copies ran while one was open for 9% -> 8% of each run, Pallas kernels for 0% -> 0%
where the time goes in v15:
time: 172 us; the launch traced here: 170 us
  waiting for transfers between devices  101 us (59%)
  starting transfers between devices  22.4 us (13%)
  between operations  17.2 us (10%)
  matrix products  10.9 us (6%)
  blocking collectives  8.82 us (5%)
  other arithmetic  8.04 us (5%)
    all_gather x1, waiting for transfers between devices, body(): gathered = lax.all_gather(gathered, 'fz', axis=1)  54.1 us
    ppermute x3, waiting for transfers between devices, passed_along(): return lax.ppermute(value, axis, pairs)  21.6 us
    reduce_scatter x1, waiting for transfers between devices, body(): grad16 = lax.psum_scatter(blocks, 'fz', scatter_dimension=0)  21.5 us
    ppermute x3, starting transfers between devices, passed_along(): return lax.ppermute(value, axis, pairs)  13 us
    all_gather x1, blocking collectives, body(): gathered = lax.all_gather(params, 'fl', axis=0)  8.82 us
    ppermute x2, starting transfers between devices, body(): their_errors = lax.ppermute(errors, 'fl', flip)  5.84 us
    dot_general x2, matrix products, body(): lax.dot_general(their_cols[span], their_errors, contract, preferred_eleme...  5.14 us
    dot_general x2, matrix products, body(): jnp.dot(normed[span], full_params, preferred_element_type=jnp.float32)  4.32 us
  transfers between devices with their start and end apart: 8, of which 5 were waited for; matrix products, arithmetic and copies ran while one was open for 8% of the time, Pallas kernels for 0%

profile of v15, /device:TPU:6, one launch (start us, length us, event | category | flops | bytes accessed | tf_op | source)
XLA Modules:
  0.0 169.8 jit_solution(9998501863242835746)
XLA Ops:
  7.2 0.0 all-gather.3.cloned.1.call-start
  7.9 1.1 divide_convert_fusion
  9.0 8.8 %all_gather.10 = bf16[2,256,512]{2,1,0:T(8,128)(2,1)} all-gather(bf16[1,256,512]{2,1,0:T(8,128)(2,1)S(1)} %divide_convert_fusion), channel_id=1, replica_groups=mesh['replica'=32,'fl'=2,'fz'=8] {'fl'}, dimensions={0}, use_global_device_ids=true | all-gather | bytes 786432 | tf_op jit(solution)/shard_map/all_gather | solution.py:36
  17.8 0.0 all-gather.3.cloned.1.call-update
  17.8 0.0 reduce-scatter.2.cloned.1.call-start
  17.9 0.0 copy-start
  17.9 2.7 %fusion = f32[384]{0:T(512)S(1)} fusion(bf16[1,384,4096]{2,1,0:T(8,128)(2,1)} %param.15), kind=kLoop, calls=%fused_computation.2 | loop fusion | flops 4718208 | bytes 3147264 | tf_op jit(solution)/shard_map/reduce_sum | solution.py:40
  20.6 0.1 copy-done
  20.7 1.2 fusion.2
  21.9 1.3 constant_dynamic-slice_fusion
  23.2 3.5 %collective-permute-start.9 = (bf16[384,2048]{1,0:T(8,128)(2,1)}, bf16[384,2048]{1,0:T(8,128)(2,1)}, u32[]{:S(2)}, u32[]{:S(2)}) collective-permute-start(bf16[384,2048]{1,0:T(8,128)(2,1)} %constant_dynamic-slice_fusion), channel_id=1, source_target_pairs={{0,8},{8,0},{1,9},{9,1},{2,10},{10,2},{3,11},{11,3},{4,12},{12,4},... | collective-permute-start | bytes 4718600 | tf_op jit(solution)/shard_map/ppermute | solution.py:48
  26.6 54.1 %all-gather.3.cloned.1.call-done = bf16[2,2048,512]{2,1,0:T(8,128)(2,1)} async-done(((bf16[2,256,512]{2,1,0:T(8,128)(2,1)}), bf16[2,2048,512]{2,1,0:T(8,128)(2,1)}) %all-gather.3.cloned.1.call-update) | async-done | bytes 4194320 | tf_op jit(solution)/shard_map/all_gather | solution.py:37
  80.7 3.1 %fusion.19 = bf16[128,512]{1,0:T(8,128)(2,1)S(1)} fusion(bf16[4096,512]{1,0:T(8,128)(2,1)} %bitcast.27, bf16[384,4096]{1,0:T(8,128)(2,1)S(1)} %fusion.2, bf16[1,384,512]{2,1,0:T(8,128)(2,1)S(1)} %copy-done.3), kind=kOutput, calls=%fused_computation.17 | convolution fusion | flops 537198592 | bytes 5505024 | tf_op jit(solution)/shard_map/dot_general | solution.py:53
  83.8 3.4 %collective-permute-start.11 = (bf16[128,512]{1,0:T(8,128)(2,1)S(1)}, bf16[128,512]{1,0:T(8,128)(2,1)S(1)}, u32[]{:S(2)}, u32[]{:S(2)}) collective-permute-start(bf16[128,512]{1,0:T(8,128)(2,1)S(1)} %fusion.19), channel_id=1, source_target_pairs={{0,8},{8,0},{1,9},{9,1},{2,10},{10,2},{3,11},{11,3},{4,12},{12,4},... | collective-permute-start | bytes 393224 | tf_op jit(solution)/shard_map/ppermute | solution.py:57
  87.2 1.3 fusion.14
  88.5 2.4 %collective-permute-start.10 = (bf16[256,512]{1,0:T(8,128)(2,1)S(1)}, bf16[256,512]{1,0:T(8,128)(2,1)S(1)}, u32[]{:S(2)}, u32[]{:S(2)}) collective-permute-start(bf16[256,512]{1,0:T(8,128)(2,1)S(1)} %fusion.14), channel_id=1, source_target_pairs={{0,8},{8,0},{1,9},{9,1},{2,10},{10,2},{3,11},{11,3},{4,12},{12,4},... | collective-permute-start | bytes 786440 | tf_op jit(solution)/shard_map/ppermute | solution.py:57
  90.9 0.7 fusion.22
  91.7 0.7 add_convert_fusion.2
  92.5 1.8 %fusion.24 = f32[2048,512]{1,0:T(8,128)S(1)} fusion(bf16[128,512]{1,0:T(8,128)(2,1)S(1)} %collective-permute-done.11, bf16[384,2048]{1,0:T(8,128)(2,1)} %collective-permute-done.9), kind=kOutput, calls=%fused_computation.22 | convolution fusion | flops 268435456 | bytes 4849664 | tf_op jit(solution)/shard_map/dot_general | solution.py:59
  94.2 3.7 %collective-permute-done.10 = bf16[256,512]{1,0:T(8,128)(2,1)S(1)} collective-permute-done((bf16[256,512]{1,0:T(8,128)(2,1)S(1)}, bf16[256,512]{1,0:T(8,128)(2,1)S(1)}, u32[]{:S(2)}, u32[]{:S(2)}) %collective-permute-start.10) | collective-permute-done | bytes 262176 | tf_op jit(solution)/shard_map/ppermute | solution.py:57
  98.0 3.4 %add_convert_fusion = bf16[2048,512]{1,0:T(8,128)(2,1)} fusion(bf16[2048,512]{1,0:T(8,128)(2,1)S(1)} %add_convert_fusion.2, f32[2048,512]{1,0:T(8,128)S(1)} %fusion.24, bf16[256,512]{1,0:T(8,128)(2,1)S(1)} %collective-permute-done.10, bf16[384,2048]{1,0:T(8,128)(2,1)} %collective-permute-done.9), kind=kOutput, calls=%fused_computation.5 | convolution fusion | flops 543162368 | bytes 9699328 | tf_op jit(solution)/shard_map/dot_general | solution.py:59
  101.3 0.0 reduce-scatter.2.cloned.1.call-update
  102.0 19.7 %conditional.5 = (f32[256,512]{1,0:T(8,128)}, f32[1]{0:T(128)}) conditional(s32[]{:T(128)} %bitcast.1, (f32[256,512]{1,0:T(8,128)S(1)}, f32[1]{0:T(128)}) %tuple.59, (f32[256,512]{1,0:T(8,128)S(1)}, f32[1]{0:T(128)}) %tuple.60, (f32[256,512]{1,0:T(8,128)S(1)}, f32[1]{0:T(128)}) %tuple.61), branch_computations={%region_1.0_spmd, %region_2.0_spmd, %region_3.0_spmd} | conditional | bytes 2097264 | solution.py:25
  102.0 4.3 %collective-permute-start.2 = (f32[256,512]{1,0:T(8,128)S(1)}, f32[256,512]{1,0:T(8,128)}, u32[]{:S(2)}, u32[]{:S(2)}) collective-permute-start(f32[256,512]{1,0:T(8,128)S(1)} %get-tuple-element.27), channel_id=1, source_target_pairs={{0,32},{16,48},{32,64},{48,80},{64,96},{80,112},{96,128},{112,144}... | collective-permute-start | bytes 1572872 | tf_op jit(solution)/shard_map/cond/branch_1_fun/ppermute | solution.py:16
  106.4 4.6 %collective-permute-start.3 = (f32[1]{0:T(128)}, f32[1]{0:T(128)}, u32[]{:S(2)}, u32[]{:S(2)}) collective-permute-start(f32[1]{0:T(128)} %get-tuple-element.28), channel_id=1, source_target_pairs={{0,32},{16,48},{32,64},{48,80},{64,96},{80,112},{96,128},{112,144}... | collective-permute-start | bytes 20 | tf_op jit(solution)/shard_map/cond/branch_1_fun/ppermute | solution.py:16
  111.0 10.7 %collective-permute-done.3 = f32[1]{0:T(128)} collective-permute-done((f32[1]{0:T(128)}, f32[1]{0:T(128)}, u32[]{:S(2)}, u32[]{:S(2)}) %collective-permute-start.3) | collective-permute-done | bytes 36 | tf_op jit(solution)/shard_map/cond/branch_1_fun/ppermute | solution.py:16
  122.3 1.1 add_multiply_fusion
  123.4 21.5 %reduce-scatter.2.cloned.1.call-done = bf16[1,256,512]{2,1,0:T(8,128)(2,1)} async-done(((bf16[8,256,512]{2,1,0:T(8,128)(2,1)}), bf16[1,256,512]{2,1,0:T(8,128)(2,1)}) %reduce-scatter.2.cloned.1.call-update) | async-done | bytes 262160 | tf_op jit(solution)/shard_map/reduce_scatter | solution.py:68
  144.9 15.0 %conditional.6 = (bf16[256,512]{1,0:T(8,128)(2,1)}) conditional(s32[]{:T(128)} %bitcast.1, bf16[256,512]{1,0:T(8,128)(2,1)} %bitcast.32, bf16[256,512]{1,0:T(8,128)(2,1)} %bitcast.33, bf16[256,512]{1,0:T(8,128)(2,1)} %bitcast.34), branch_computations={%region_5.0_spmd, %region_6.0_spmd, %region_7.0_spmd} | conditional | bytes 1048624
  144.9 4.0 %collective-permute-start.7 = (bf16[256,512]{1,0:T(8,128)(2,1)}, bf16[256,512]{1,0:T(8,128)(2,1)}, u32[]{:S(2)}, u32[]{:S(2)}) collective-permute-start(bf16[256,512]{1,0:T(8,128)(2,1)} %param.4), channel_id=1, source_target_pairs={{0,32},{16,48},{32,64},{48,80},{64,96},{80,112},{96,128},{112,144}... | collective-permute-start | bytes 786440 | tf_op jit(solution)/shard_map/cond/branch_1_fun/ppermute | solution.py:16
  148.9 10.9 %collective-permute-done.7 = bf16[256,512]{1,0:T(8,128)(2,1)} collective-permute-done((bf16[256,512]{1,0:T(8,128)(2,1)}, bf16[256,512]{1,0:T(8,128)(2,1)}, u32[]{:S(2)}, u32[]{:S(2)}) %collective-permute-start.7) | collective-permute-done | bytes 262176 | tf_op jit(solution)/shard_map/cond/branch_1_fun/ppermute | solution.py:16
  159.9 1.9 %subtract_bitcast_fusion = f32[1,256,512]{2,1,0:T(8,128)} fusion(f32[256,512]{1,0:T(8,128)S(1)} %add_multiply_fusion, bf16[256,512]{1,0:T(8,128)(2,1)} %get-tuple-element.53, bf16[256,512]{1,0:T(8,128)(2,1)} %bitcast.35), kind=kLoop, calls=%fused_computation.25 | loop fusion | flops 655360 | bytes 1572864 | tf_op jit(solution)/shard_map/broadcast_in_dim | solution.py:73
  (12 shorter events, 0.0 us)
Async XLA Ops:
  7.2 13.4 %copy-start.4 = (f32[4096]{0:T(1024)S(1)}, f32[4096]{0:T(1024)}, u32[]{:S(2)}) copy-start(f32[4096]{0:T(1024)} %param.17) | copy-start | bytes 49156
  7.2 73.6 %all-gather.3.cloned.1.call-start = ((), (), s32[]{:S(2)}) async-start(), calls=%async_computation.2 | async-start | bytes 4718592 | tf_op jit(solution)/shard_map/all_gather | solution.py:37
  17.8 127.1 %reduce-scatter.2.cloned.1.call-start = ((), (), s32[]{:S(2)}) async-start(), calls=%async_computation.1 | async-start | bytes 2359296 | tf_op jit(solution)/shard_map/reduce_scatter | solution.py:68
  17.9 2.8 %copy-start = (bf16[1,384,4096]{2,1,0:T(8,128)(2,1)S(1)}, bf16[1,384,4096]{2,1,0:T(8,128)(2,1)}, u32[]{:S(2)}) copy-start(bf16[1,384,4096]{2,1,0:T(8,128)(2,1)} %param.15) | copy-start | bytes 9437188
  21.9 58.9 %copy-start.3 = (bf16[1,384,512]{2,1,0:T(8,128)(2,1)S(1)}, bf16[1,384,512]{2,1,0:T(8,128)(2,1)}, u32[]{:S(2)}) copy-start(bf16[1,384,512]{2,1,0:T(8,128)(2,1)} %param.16) | copy-start | bytes 1179652
  23.2 69.3 %collective-permute-start.9 = (bf16[384,2048]{1,0:T(8,128)(2,1)}, bf16[384,2048]{1,0:T(8,128)(2,1)}, u32[]{:S(2)}, u32[]{:S(2)}) collective-permute-start(bf16[384,2048]{1,0:T(8,128)(2,1)} %constant_dynamic-slice_fusion), channel_id=1, source_target_pairs={{0,8},{8,0},{1,9},{9,1},{2,10},{10,2},{3,11},{11,3},{4,12},{12,4},... | collective-permute-start | bytes 4718600 | tf_op jit(solution)/shard_map/ppermute | solution.py:48
  80.7 6.5 %copy-start.1 = (bf16[2,2048,512]{2,1,0:T(8,128)(2,1)S(1)}, bf16[2,2048,512]{2,1,0:T(8,128)(2,1)}, u32[]{:S(2)}) copy-start(bf16[2,2048,512]{2,1,0:T(8,128)(2,1)} %all-gather.3.cloned.1.call-done) | copy-start | bytes 12582916
  83.8 8.6 %collective-permute-start.11 = (bf16[128,512]{1,0:T(8,128)(2,1)S(1)}, bf16[128,512]{1,0:T(8,128)(2,1)S(1)}, u32[]{:S(2)}, u32[]{:S(2)}) collective-permute-start(bf16[128,512]{1,0:T(8,128)(2,1)S(1)} %fusion.19), channel_id=1, source_target_pairs={{0,8},{8,0},{1,9},{9,1},{2,10},{10,2},{3,11},{11,3},{4,12},{12,4},... | collective-permute-start | bytes 393224 | tf_op jit(solution)/shard_map/ppermute | solution.py:57
  88.5 9.5 %collective-permute-start.10 = (bf16[256,512]{1,0:T(8,128)(2,1)S(1)}, bf16[256,512]{1,0:T(8,128)(2,1)S(1)}, u32[]{:S(2)}, u32[]{:S(2)}) collective-permute-start(bf16[256,512]{1,0:T(8,128)(2,1)S(1)} %fusion.14), channel_id=1, source_target_pairs={{0,8},{8,0},{1,9},{9,1},{2,10},{10,2},{3,11},{11,3},{4,12},{12,4},... | collective-permute-start | bytes 786440 | tf_op jit(solution)/shard_map/ppermute | solution.py:57
  94.2 7.8 %copy-start.2 = (f32[1,256,512]{2,1,0:T(8,128)S(1)}, f32[1,256,512]{2,1,0:T(8,128)}, u32[]{:S(2)}) copy-start(f32[1,256,512]{2,1,0:T(8,128)} %param.12) | copy-start | bytes 1572868
  102.0 19.7 %collective-permute-start.2 = (f32[256,512]{1,0:T(8,128)S(1)}, f32[256,512]{1,0:T(8,128)}, u32[]{:S(2)}, u32[]{:S(2)}) collective-permute-start(f32[256,512]{1,0:T(8,128)S(1)} %get-tuple-element.27), channel_id=1, source_target_pairs={{0,32},{16,48},{32,64},{48,80},{64,96},{80,112},{96,128},{112,144}... | collective-permute-start | bytes 1572872 | tf_op jit(solution)/shard_map/cond/branch_1_fun/ppermute | solution.py:16
  106.4 15.4 %collective-permute-start.3 = (f32[1]{0:T(128)}, f32[1]{0:T(128)}, u32[]{:S(2)}, u32[]{:S(2)}) collective-permute-start(f32[1]{0:T(128)} %get-tuple-element.28), channel_id=1, source_target_pairs={{0,32},{16,48},{32,64},{48,80},{64,96},{80,112},{96,128},{112,144}... | collective-permute-start | bytes 20 | tf_op jit(solution)/shard_map/cond/branch_1_fun/ppermute | solution.py:16
  144.9 14.9 %collective-permute-start.7 = (bf16[256,512]{1,0:T(8,128)(2,1)}, bf16[256,512]{1,0:T(8,128)(2,1)}, u32[]{:S(2)}, u32[]{:S(2)}) collective-permute-start(bf16[256,512]{1,0:T(8,128)(2,1)} %param.4), channel_id=1, source_target_pairs={{0,32},{16,48},{32,64},{48,80},{64,96},{80,112},{96,128},{112,144}... | collective-permute-start | bytes 786440 | tf_op jit(solution)/shard_map/cond/branch_1_fun/ppermute | solution.py:16
Sparse Core Ops, SparseCore 0:
  17.9 62.7 all-gather.2
  101.5 43.3 reduce-scatter.1
